TPU v7x, 32 devices: a whole 2x2x4 slice. The times are simulated.
32 devices in a mesh: seq: 8 (over z, y), exp: 4 (over x, core).
Axes of the slice: x: 2, y: 2, z: 4, core: 2. Of those that a mesh axis runs over, the one named last changes fastest.
Arguments:
- hidden: bfloat16 [4, 1024, 2048], P('exp', 'seq'), may hold values from -6 to 6
- lengths: int32 [4, 4], P('exp'), may hold values from 1 to 512, 1024 in all within a row
- attn_gain: float32 [2048], replicated, may hold values from 0 to 10
- w_qkv: bfloat16 [2048, 3, 16, 128], P(None, None, 'seq'), may hold values from -0.125 to 0.125
- w_out: bfloat16 [16, 128, 2048], P('seq'), may hold values from -0.125 to 0.125
- moe_gain: float32 [2048], replicated, may hold values from 0.5 to 1.5
- router: bfloat16 [2048, 16], replicated, may hold values from -8 to 8
- routes: int32 [4, 1024, 6], P('exp', 'seq'), may hold values from 0 to 15, all different within a row; in each aligned block of 128 rows (0 to 127, 128 to 255, ..., all dimensions but the last counted through in order) at most 56 rows name the same one
- w_gate_up: bfloat16 [32, 2, 704, 2048], P(('seq', 'exp')), may hold values from -0.125 to 0.125
- w_down: bfloat16 [32, 704, 2048], P(('seq', 'exp')), may hold values from -0.15625 to 0.15625
- final_gain: float32 [2048], replicated, may hold values from 0.5 to 1.5
- lm_head: bfloat16 [102400, 2048], P(('seq', 'exp')), may hold values from -4 to 4
Outputs:
- layer_out: bfloat16 [4, 1024, 2048], P('exp', 'seq')
- logprobs: float32 [16, 102400], P(None, ('seq', 'exp'))
Inputs may be any that keep to these rules, and one draw needn't show every extreme that they name: `routes`: in the rows of one device no expert is named by more than 56 rows; in some devices one expert is named by exactly 56 rows. `lengths`: each row sums to 1024; its largest entry is 512.
All inputs are finite; a program needn't handle non-finite values.
Results may differ from a plain program's by a relative error of at most 0.0095.
The roundings to bfloat16 on the way count: a program that leaves them out, or rounds other values in their place, can miss the bound.
Values may be sent and summed in bfloat16 or wider, within the bound.
No kernel may reach another device: no remote copies, remote signals or barrier semaphores. Data moves between devices by JAX's collectives and lax.ppermute only.
A program may use at most 128 MiB of HBM per device.

v0:
```python
import jax
import jax.numpy as jnp
from jax import lax
from jax.sharding import PartitionSpec as P

epsilon = 1e-06


def joined(value, axis, join):
    pieces = jax.tree.map(lambda part: lax.all_gather(part, axis), value)
    head = jax.tree.map(lambda part: part[0], pieces)
    tail = jax.tree.map(lambda part: part[1:], pieces)
    subtotal, _ = lax.scan(lambda subtotal, piece: (join(subtotal, piece), None), head, tail)
    return subtotal


def rms_scale(values, gain):
    widened = values.astype(jnp.float32)
    inverse = lax.rsqrt(jnp.mean(widened * widened, axis=-1, keepdims=True) + epsilon)
    return widened * inverse * gain


def segment_layout(prompt_lengths, count):
    ends = jnp.cumsum(prompt_lengths)
    starts = ends - prompt_lengths
    places = jnp.arange(count, dtype=jnp.int32)
    member = ((places[:, None] >= starts[None, :]) & (places[:, None] < ends[None, :])).astype(
        jnp.int32
    )
    numbers = jnp.arange(prompt_lengths.shape[0], dtype=jnp.int32)
    segment = jnp.sum(member * numbers[None, :], axis=1)
    offset = places - jnp.sum(member * starts[None, :], axis=1)
    return (segment, offset)


def rotary(values, positions):
    half_size = values.shape[-1] // 2
    freqs = 10000.0 ** (-2.0 * jnp.arange(half_size, dtype=jnp.float32) / values.shape[-1])
    angles = positions.astype(jnp.float32)[:, None] * freqs[None, :]
    cosine = jnp.cos(angles)[:, None, :]
    sine = jnp.sin(angles)[:, None, :]
    first_half = values[..., :half_size]
    second_half = values[..., half_size:]
    return jnp.concatenate(
        [first_half * cosine - second_half * sine, second_half * cosine + first_half * sine],
        axis=-1,
    )


def pair_swap(value):
    count = lax.axis_size("exp")
    return lax.ppermute(value, "exp", [(i, i ^ 1) for i in range(count)])


def merge_softmax(earlier, later):
    highest = jnp.maximum(earlier[0], later[0])
    return (
        highest,
        earlier[1] * jnp.exp(earlier[0] - highest) + later[1] * jnp.exp(later[0] - highest),
    )


def per_device(
    hidden,
    lengths,
    attn_gain,
    w_qkv,
    w_out,
    moe_gain,
    router,
    routes,
    w_gate_up,
    w_down,
    final_gain,
    lm_head,
):
    seq_count = lax.axis_size("seq")
    group_count = lax.axis_size("exp")
    device_count = seq_count * group_count
    token_rows = hidden[0]
    tok_rows = token_rows.shape[0]
    model_width = token_rows.shape[1]
    group_tokens = tok_rows * seq_count
    head_count = w_qkv.shape[2]
    head_size = w_qkv.shape[3]
    scale_factor = head_size ** (-0.5)
    prompt_lengths = lengths[0]
    segment, offset = segment_layout(prompt_lengths, group_tokens)
    normed = rms_scale(token_rows, attn_gain).astype(jnp.bfloat16)
    group_normed = lax.all_gather(normed, "seq", axis=0, tiled=True)
    core = lax.axis_index("exp") % 2
    half_size = head_size // 2
    own_half = lax.dynamic_slice_in_dim(w_out, core * half_size, half_size, axis=1)
    own_weight = lax.all_to_all(
        jnp.broadcast_to(own_half[None], (seq_count,) + own_half.shape),
        "seq",
        split_axis=0,
        concat_axis=0,
        tiled=True,
    ).reshape((-1,) + own_half.shape[1:])
    qkv = jnp.einsum("td,dshe->tshe", group_normed, w_qkv, preferred_element_type=jnp.float32)
    query = rotary(qkv[:, 0], offset).astype(jnp.bfloat16)
    keys = rotary(qkv[:, 1], offset).astype(jnp.bfloat16)
    values = qkv[:, 2].astype(jnp.bfloat16)
    block_count = 4
    block_rows = group_tokens // block_count
    key_places = jnp.arange(group_tokens, dtype=jnp.int32)

    def one_block(block_index):
        first_row = block_index * block_rows
        key_count = first_row + block_rows
        block_query = query[first_row:key_count]
        block_segment = segment[first_row:key_count]
        query_places = key_places[first_row:key_count]
        scores = (
            jnp.einsum(
                "qhd,khd->hqk", block_query, keys[:key_count], preferred_element_type=jnp.float32
            )
            * scale_factor
        )
        allowed = (block_segment[:, None] == segment[None, :key_count]) & (
            key_places[None, :key_count] <= query_places[:, None]
        )
        scores = jnp.where(allowed[None], scores, -1e30)
        highest = jnp.max(scores, axis=2, keepdims=True)
        weights = jnp.exp(scores - highest)
        probs = (weights / jnp.sum(weights, axis=2, keepdims=True)).astype(jnp.bfloat16)
        return jnp.einsum(
            "hqk,khd->qhd", probs, values[:key_count], preferred_element_type=jnp.float32
        ).astype(jnp.bfloat16)

    blocks = jnp.concatenate([one_block(index) for index in range(block_count)], axis=0)
    own_weight, blocks = lax.optimization_barrier((own_weight, blocks))
    heads_flat = blocks.reshape(group_tokens, head_count * head_size)
    regrouped = lax.all_to_all(heads_flat, "seq", split_axis=0, concat_axis=1, tiled=True)
    other_weight = pair_swap(own_weight)
    regrouped = regrouped.reshape(tok_rows, -1, head_size)
    own_heads = lax.dynamic_slice_in_dim(regrouped, core * half_size, half_size, axis=2)
    other_heads = lax.dynamic_slice_in_dim(regrouped, (1 - core) * half_size, half_size, axis=2)
    mixed = jnp.einsum(
        "thd,hdo->to", own_heads, own_weight, preferred_element_type=jnp.float32
    ) + jnp.einsum("thd,hdo->to", other_heads, other_weight, preferred_element_type=jnp.float32)
    middle = (token_rows.astype(jnp.float32) + mixed).astype(jnp.bfloat16)
    expert_in = rms_scale(middle, moe_gain).astype(jnp.bfloat16)
    logits = jnp.dot(expert_in, router, preferred_element_type=jnp.float32)
    expert_count = router.shape[1]
    token_routes = routes[0]
    top_count = token_routes.shape[1]
    expert_ids = jnp.arange(expert_count, dtype=jnp.int32)
    chosen_mask = token_routes[:, :, None] == expert_ids[None, None, :]
    chosen = jnp.sum(jnp.where(chosen_mask, logits[:, None, :], 0.0), axis=2)
    gates = jax.nn.softmax(chosen, axis=-1)
    capacity = max(2, tok_rows * top_count * 7 // (6 * expert_count))
    flat_mask = chosen_mask.reshape(tok_rows * top_count, expert_count).astype(jnp.int32)
    earlier_count = jnp.cumsum(flat_mask, axis=0) - flat_mask
    slot_index = jnp.sum(earlier_count * flat_mask, axis=1)
    target = (token_routes.reshape(-1) * capacity + slot_index).reshape(tok_rows, top_count)
    slot_total = expert_count * capacity
    placed = target[:, :, None] == jnp.arange(slot_total, dtype=jnp.int32)[None, None, :]
    shares = device_count // expert_count
    assert capacity % shares == 0
    per_dest = capacity // shares
    dispatch_table = jnp.any(placed, axis=1).astype(jnp.bfloat16)
    dispatch_table = dispatch_table.reshape(tok_rows, device_count, per_dest)
    slot_weights = jnp.sum(jnp.where(placed, gates[:, :, None], 0.0), axis=1)
    slot_weights = slot_weights.reshape(tok_rows, device_count, per_dest)
    outgoing = jnp.einsum(
        "tsc,tm->scm", dispatch_table, expert_in, preferred_element_type=jnp.float32
    ).astype(jnp.bfloat16)
    gate_up = w_gate_up[0]
    down_weight = w_down[0]
    other_gate_up = pair_swap(gate_up)
    other_down = pair_swap(down_weight)
    arrived = lax.all_to_all(outgoing, ("seq", "exp"), split_axis=0, concat_axis=0, tiled=True)

    def share_part(pair, down):
        both = jnp.einsum("scd,gfd->scgf", arrived, pair, preferred_element_type=jnp.float32)
        act = (jax.nn.silu(both[:, :, 0]) * both[:, :, 1]).astype(jnp.bfloat16)
        part = jnp.einsum("scf,fd->scd", act, down, preferred_element_type=jnp.float32)
        return part.astype(jnp.bfloat16).astype(jnp.float32)

    part_sum = share_part(gate_up, down_weight) + share_part(other_gate_up, other_down)
    returned = lax.all_to_all(
        part_sum.astype(jnp.bfloat16), ("seq", "exp"), split_axis=0, concat_axis=0, tiled=True
    )
    routed = jnp.einsum(
        "tsc,scm->tm",
        slot_weights,
        returned.astype(jnp.float32),
        precision=lax.Precision.HIGHEST,
        preferred_element_type=jnp.float32,
    )
    layer_rows = (middle.astype(jnp.float32) + routed).astype(jnp.bfloat16)
    prompt_count = prompt_lengths.shape[0]
    last_places = jnp.cumsum(prompt_lengths) - 1
    here_places = lax.axis_index("seq") * tok_rows + jnp.arange(tok_rows, dtype=jnp.int32)
    select_table = (last_places[:, None] == here_places[None, :]).astype(jnp.bfloat16)
    picked = jnp.dot(select_table, layer_rows, preferred_element_type=jnp.float32)
    outgoing_rows = jnp.broadcast_to(
        picked.astype(jnp.bfloat16)[None], (device_count, prompt_count, model_width)
    )
    arrived_rows = lax.all_to_all(
        outgoing_rows, ("seq", "exp"), split_axis=0, concat_axis=0, tiled=True
    ).astype(jnp.float32)
    last_rows = jnp.sum(
        arrived_rows.reshape(seq_count, group_count * prompt_count, model_width), axis=0
    )
    final = rms_scale(last_rows, final_gain).astype(jnp.bfloat16)
    vocab_scores = lax.dot_general(
        final, lm_head, (((1,), (1,)), ((), ())), preferred_element_type=jnp.float32
    )
    local_peak = jnp.max(vocab_scores, axis=1)
    local_total = jnp.sum(jnp.exp(vocab_scores - local_peak[:, None]), axis=1)
    local_stats = jnp.stack([local_peak, local_total])
    all_stats = lax.all_to_all(
        jnp.broadcast_to(local_stats[None], (device_count,) + local_stats.shape),
        ("seq", "exp"),
        split_axis=0,
        concat_axis=0,
        tiled=True,
    )
    all_peaks = all_stats[:, 0]
    global_peak = jnp.max(all_peaks, axis=0)
    global_total = jnp.sum(all_stats[:, 1] * jnp.exp(all_peaks - global_peak[None]), axis=0)
    logprobs = vocab_scores - (global_peak + jnp.log(global_total))[:, None]
    return (layer_rows[None], logprobs)


def solution(mesh):
    return jax.shard_map(
        per_device,
        mesh=mesh,
        in_specs=(
            P("exp", "seq", None),
            P("exp", None),
            P(),
            P(None, None, "seq", None),
            P("seq", None, None),
            P(),
            P(),
            P("exp", "seq", None),
            P(("seq", "exp"), None, None, None),
            P(("seq", "exp"), None, None),
            P(),
            P(("seq", "exp"), None),
        ),
        out_specs=(P("exp", "seq", None), P(None, ("seq", "exp"))),
        check_vma=False,
    )
```

profile of v0, /device:TPU:0, one launch (start us, length us, event | category | flops | bytes accessed | tf_op | source)
XLA Modules:
  0.0 496.6 jit_solution(13074911632502741158)
XLA Ops:
  7.2 1.3 fusion.40
  8.5 2.0 fusion.42
  10.7 2.5 broadcast_in_dim.68
  13.2 7.4 %all-to-all-start = ((bf16[8,2,64,2048]{3,2,1,0:T(8,128)(2,1)}), bf16[8,2,64,2048]{3,2,1,0:T(8,128)(2,1)}, u32[]{:S(2)}, u32[]{:S(2)}) async-start(bf16[8,2,64,2048]{3,2,1,0:T(8,128)(2,1)} %broadcast_in_dim.68), calls=%async_computation | async-start | bytes 8388608 | tf_op jit(solution)/shard_map/all_to_all | solution.py:94
  20.8 8.7 %copy.98 = bf16[2048,3,2,128]{0,3,2,1:T(8,128)(2,1)} copy(bf16[2048,3,2,128]{3,2,1,0:T(2,128)(2,1)} %param.15) | data formatting | bytes 6291456 | tf_op args[3]
  29.9 0.8 compare_and_fusion.1
  30.7 0.9 compare_and_fusion
  31.6 1.1 fusion.45
  32.7 1.8 multiply_cosine_fusion
  34.5 126.0 %all-gather.2.cloned.1.call-done = bf16[1024,2048]{1,0:T(8,128)(2,1)} async-done(((bf16[128,2048]{1,0:T(8,128)(2,1)}), bf16[1024,2048]{1,0:T(8,128)(2,1)}) %all-gather.2.cloned.1.call-update) | async-done | bytes 4194320 | tf_op jit(solution)/shard_map/all_gather | solution.py:90
  160.5 6.2 %fusion.160 = f32[1024,768]{0,1:S(1)} fusion(bf16[1024,2048]{1,0:T(8,128)(2,1)} %all-gather.2.cloned.1.call-done, bf16[2048,768]{0,1:T(8,128)(2,1)} %bitcast.155), kind=kOutput, calls=%fused_computation.194 | convolution fusion | flops 3221225472 | bytes 10485760
  167.1 0.8 copy-done.5
  168.0 1.1 subtract_convert_fusion
  169.0 1.3 fusion.154
  170.3 1.5 fusion.149
  171.9 0.3 fusion.35
  172.2 0.3 fusion.36
  172.5 1.7 fusion.37
  174.2 1.9 fusion.144
  176.1 2.3 fusion.143
  178.4 2.0 fusion.38
  180.5 0.6 fusion.39
  181.4 0.9 copy.108
  182.3 3.7 all-to-all-start.1
  186.4 1.7 reduce-window.11
  188.7 0.5 fusion.16
  189.5 11.6 %all-to-all-done.1 = bf16[8,128,256]{1,2,0:T(8,128)(2,1)S(1)} async-done(((bf16[8,128,256]{1,2,0:T(8,128)(2,1)}), bf16[8,128,256]{1,2,0:T(8,128)(2,1)S(1)}, u32[]{:S(2)}, u32[]{:S(2)}) %all-to-all-start.1) | async-done | bytes 524320 | tf_op jit(solution)/shard_map/all_to_all | solution.py:135
  201.1 2.9 convolution_bitcast_fusion.2
  204.1 3.1 multiply_reduce_fusion
  207.2 1.2 convolution_convert_fusion
  208.4 4.1 copy.118
  212.5 4.0 all-to-all-start.2
  216.6 0.5 collective-permute-start.2
  217.1 93.3 %all-to-all-done.2 = bf16[32,28,2048]{2,1,0:T(8,128)(2,1)} async-done(((bf16[32,28,2048]{2,1,0:T(8,128)(2,1)}), bf16[32,28,2048]{2,1,0:T(8,128)(2,1)}, u32[]{:S(2)}, u32[]{:S(2)}) %all-to-all-start.2) | async-done | bytes 3670048 | tf_op jit(solution)/shard_map/all_to_all | solution.py:174
  310.3 12.6 %fusion.6 = f32[32,28,2,704]{3,0,2,1:T(8,128)S(1)} fusion(bf16[1,2,704,2048]{3,2,1,0:T(8,128)(2,1)} %param.20, bf16[32,28,2048,1]{2,1,0,3:T(8,128)(2,1)} %bitcast.28), kind=kOutput, calls=%fused_computation.7 | convolution fusion | flops 5167382528 | bytes 14483456 | tf_op jit(solution)/shard_map/scd,gfd->scgf/dot_general | solution.py:177
  323.0 3.3 fusion.11
  326.3 12.5 %fusion.4 = f32[32,28,2,704]{3,0,2,1:T(8,128)S(1)} fusion(bf16[2,704,2048]{2,1,0:T(8,128)(2,1)} %collective-permute-done.1, bf16[32,28,2048,1]{2,1,0,3:T(8,128)(2,1)} %bitcast.28), kind=kOutput, calls=%fused_computation.5 | convolution fusion | flops 5167382528 | bytes 14483456 | tf_op jit(solution)/shard_map/scd,gfd->scgf/dot_general | solution.py:177
  338.8 5.2 %add_convert_fusion = bf16[32,28,2048]{2,0,1:T(8,128)(2,1)S(1)} fusion(bf16[32,28,2048]{2,0,1:T(8,128)(2,1)S(1)} %fusion.11, bf16[704,2048]{1,0:T(8,128)(2,1)} %collective-permute-done.2, f32[32,28,2,704]{3,0,2,1:T(8,128)S(1)} %fusion.4), kind=kOutput, calls=%fused_computation.4 | convolution fusion | flops 2596651008 | bytes 15269888 | tf_op jit(solution)/shard_map/scf,fd->scd/dot_general | solution.py:179
  344.0 4.0 copy.122
  348.1 4.2 all-to-all-start.3
  352.3 0.3 fusion.140
  352.7 0.4 select_reduce_fusion
  353.3 92.8 %all-to-all-done.3 = bf16[32,28,2048]{2,1,0:T(8,128)(2,1)} async-done(((bf16[32,28,2048]{2,1,0:T(8,128)(2,1)}), bf16[32,28,2048]{2,1,0:T(8,128)(2,1)}, u32[]{:S(2)}, u32[]{:S(2)}) %all-to-all-start.3) | async-done | bytes 3670048 | tf_op jit(solution)/shard_map/all_to_all | solution.py:183
  446.1 4.1 fusion.22
  450.7 19.1 %all_to_all.41 = bf16[32,4,2048]{2,1,0:T(4,128)(2,1)S(1)} all-to-all(bf16[32,4,2048]{2,1,0:T(4,128)(2,1)S(1)} %broadcast_in_dim.86), channel_id=1, replica_groups=mesh['seq'=8,'exp'=4] {'seq','exp'}, dimensions={0} | all-to-all | bytes 1048576 | tf_op jit(solution)/shard_map/all_to_all | solution.py:202
  470.1 8.4 %fusion.159 = (f32[16]{0:T(128)S(1)}, f32[16,3200]{1,0:T(8,128)S(1)}) fusion(bf16[3200,2048]{1,0:T(8,128)(2,1)} %param.23, f32[16,2048]{1,0:T(8,128)S(1)} %reduce_sum.159, f32[2048]{0:T(1024)S(1)} %copy-done.12, f32[16]{0:T(128)S(1)} %add_rsqrt_fusion), kind=kOutput, calls=%fused_computation.193 | convolution fusion | flops 209864688 | bytes 13451392 | tf_op jit(solution)/shard_map/dot_general | solution.py:209
  478.8 10.1 %all_to_all.42 = f32[32,2,16]{2,1,0:T(2,128)S(1)} all-to-all(f32[32,2,16]{2,1,0:T(2,128)S(1)} %broadcast_in_dim.87), channel_id=1, replica_groups=mesh['seq'=8,'exp'=4] {'seq','exp'}, dimensions={0} | all-to-all | bytes 8192 | tf_op jit(solution)/shard_map/all_to_all | solution.py:215
  489.0 0.8 broadcast_subtract_fusion
  (97 shorter events, 4.2 us)
Async XLA Ops:
  7.2 3.5 copy-start
  7.2 153.3 %all-gather.2.cloned.1.call-start = ((), (), s32[]{:S(2)}) async-start(), calls=%async_computation.6 | async-start | bytes 4718592 | tf_op jit(solution)/shard_map/all_gather | solution.py:90
  13.2 7.4 %copy-start.14 = (s32[1,4]{1,0:T(1,128)S(1)}, s32[1,4]{1,0:T(1,128)}, u32[]{:S(2)}) copy-start(s32[1,4]{1,0:T(1,128)} %param.13) | copy-start | bytes 52
  13.2 168.0 %all-to-all-start = ((bf16[8,2,64,2048]{3,2,1,0:T(8,128)(2,1)}), bf16[8,2,64,2048]{3,2,1,0:T(8,128)(2,1)}, u32[]{:S(2)}, u32[]{:S(2)}) async-start(bf16[8,2,64,2048]{3,2,1,0:T(8,128)(2,1)} %broadcast_in_dim.68), calls=%async_computation | async-start | bytes 8388608 | tf_op jit(solution)/shard_map/all_to_all | solution.py:94
  166.9 1.0 copy-start.5
  166.9 1.0 copy-start.6
  169.0 2.8 copy-start.4
  172.5 1.8 copy-start.8
  174.2 1.9 copy-start.7
  178.4 2.1 copy-start.15
  181.1 4.9 copy-start.11
  181.2 22.9 %collective-permute-start = (bf16[16,64,2048]{2,1,0:T(8,128)(2,1)}, bf16[16,64,2048]{2,1,0:T(8,128)(2,1)}, u32[]{:S(2)}, u32[]{:S(2)}) collective-permute-start(bf16[16,64,2048]{2,1,0:T(8,128)(2,1)} %bitcast.1), channel_id=1, source_target_pairs={{0,1},{1,0},{2,3},{3,2},{4,5},{5,4},{6,7},{7,6},{8,9},{9,8},{10,11... | collective-permute-start | bytes 12582920 | tf_op jit(solution)/shard_map/ppermute | solution.py:52
  182.3 18.8 %all-to-all-start.1 = ((bf16[8,128,256]{1,2,0:T(8,128)(2,1)}), bf16[8,128,256]{1,2,0:T(8,128)(2,1)S(1)}, u32[]{:S(2)}, u32[]{:S(2)}) async-start(bf16[8,128,256]{1,2,0:T(8,128)(2,1)} %copy.108), calls=%async_computation.1 | async-start | bytes 1048576 | tf_op jit(solution)/shard_map/all_to_all | solution.py:135
  189.4 14.7 %copy-start.2 = (bf16[1,128,2048]{2,1,0:T(8,128)(2,1)S(1)}, bf16[1,128,2048]{2,1,0:T(8,128)(2,1)}, u32[]{:S(2)}) copy-start(bf16[1,128,2048]{2,1,0:T(8,128)(2,1)} %param.12) | copy-start | bytes 1572868
  204.1 3.1 copy-start.10
  212.5 97.8 %all-to-all-start.2 = ((bf16[32,28,2048]{2,1,0:T(8,128)(2,1)}), bf16[32,28,2048]{2,1,0:T(8,128)(2,1)}, u32[]{:S(2)}, u32[]{:S(2)}) async-start(bf16[32,28,2048]{2,1,0:T(8,128)(2,1)} %copy.118), calls=%async_computation.2 | async-start | bytes 8388608 | tf_op jit(solution)/shard_map/all_to_all | solution.py:174
  216.5 109.8 %collective-permute-start.1 = (bf16[2,704,2048]{2,1,0:T(8,128)(2,1)}, bf16[2,704,2048]{2,1,0:T(8,128)(2,1)}, u32[]{:S(2)}, u32[]{:S(2)}) collective-permute-start(bf16[2,704,2048]{2,1,0:T(8,128)(2,1)} %bitcast.171), channel_id=1, source_target_pairs={{0,1},{1,0},{2,3},{3,2},{4,5},{5,4},{6,7},{7,6},{8,9},{9,8},{10,11... | collective-permute-start | bytes 17301512 | tf_op jit(solution)/shard_map/ppermute | solution.py:52
  216.6 122.2 %collective-permute-start.2 = (bf16[704,2048]{1,0:T(8,128)(2,1)}, bf16[704,2048]{1,0:T(8,128)(2,1)}, u32[]{:S(2)}, u32[]{:S(2)}) collective-permute-start(bf16[704,2048]{1,0:T(8,128)(2,1)} %bitcast.172), channel_id=1, source_target_pairs={{0,1},{1,0},{2,3},{3,2},{4,5},{5,4},{6,7},{7,6},{8,9},{9,8},{10,11... | collective-permute-start | bytes 8650760 | tf_op jit(solution)/shard_map/ppermute | solution.py:52
  310.3 12.6 %copy-start.13 = (bf16[1,704,2048]{2,1,0:T(8,128)(2,1)S(1)}, bf16[1,704,2048]{2,1,0:T(8,128)(2,1)}, u32[]{:S(2)}) copy-start(bf16[1,704,2048]{2,1,0:T(8,128)(2,1)} %param.21) | copy-start | bytes 8650756
  348.1 4.2 copy-start.9
  348.1 98.0 %all-to-all-start.3 = ((bf16[32,28,2048]{2,1,0:T(8,128)(2,1)}), bf16[32,28,2048]{2,1,0:T(8,128)(2,1)}, u32[]{:S(2)}, u32[]{:S(2)}) async-start(bf16[32,28,2048]{2,1,0:T(8,128)(2,1)} %copy.122), calls=%async_computation.3 | async-start | bytes 8388608 | tf_op jit(solution)/shard_map/all_to_all | solution.py:183
  450.2 28.3 %copy-start.3 = (bf16[128,2048]{1,0:T(8,128)(2,1)}, bf16[128,2048]{1,0:T(8,128)(2,1)S(1)}, u32[]{:S(2)}) copy-start(bf16[128,2048]{1,0:T(8,128)(2,1)S(1)} %fusion.22) | copy-start | bytes 1572868
  450.2 19.9 %copy-start.12 = (f32[2048]{0:T(1024)S(1)}, f32[2048]{0:T(1024)}, u32[]{:S(2)}) copy-start(f32[2048]{0:T(1024)} %param.22) | copy-start | bytes 24580
  470.1 19.7 %copy-start.1 = (bf16[2,128,2048]{2,1,0:T(8,128)(2,1)S(1)}, bf16[2,128,2048]{2,1,0:T(8,128)(2,1)}, u32[]{:S(2)}) copy-start(bf16[2,128,2048]{2,1,0:T(8,128)(2,1)} %param.16) | copy-start | bytes 3145732
Sparse Core Ops, SparseCore 0:
  10.7 149.7 all-gather.1
where the time goes:
time: 498 us; the launch traced here: 497 us
  waiting for transfers between devices  324 us (65%)
  matrix products  72.1 us (14%)
  blocking collectives  29.2 us (6%)
  local copies, waits for them, and re-layouts  23.2 us (5%)
  starting transfers between devices  20 us (4%)
  between operations  14.7 us (3%)
  other arithmetic  13.8 us (3%)
    all_gather x1, waiting for transfers between devices, per_device(): group_normed = lax.all_gather(normed, 'seq', axis=0, tiled=True)  126 us
    all_to_all x1, waiting for transfers between devices, per_device(): lax.all_to_all(outgoing, ('seq', 'exp'), split_axis=0, concat_axis=0, til...  93.3 us
    all_to_all x1, waiting for transfers between devices, per_device(): lax.all_to_all(part_sum.astype(jnp.bfloat16), ('seq', 'exp'), split_axis=...  92.8 us
    dot_general x2, matrix products, share_part(): jnp.einsum('scd,gfd->scgf', arrived, pair, preferred_element_type=jnp.flo...  25.1 us
    all_to_all x1, blocking collectives, per_device(): lax.all_to_all(outgoing_rows, ('seq', 'exp'), split_axis=0, concat_axis=0...  19.1 us
    all_to_all x1, waiting for transfers between devices, per_device(): lax.all_to_all(heads_flat, 'seq', split_axis=0, concat_axis=1, tiled=True)  11.6 us
    all_to_all x1, blocking collectives, per_device(): lax.all_to_all(jnp.broadcast_to(local_stats[None], (device_count,) + loca...  10.1 us
  transfers between devices with their start and end apart: 8, of which 4 were waited for; matrix products, arithmetic and copies ran while one was open for 15% of the time, Pallas kernels for 0%

commit v1 on v0

--- a/solution.py
+++ b/solution.py
@@ -164,32 +164,42 @@
     dispatch_table = dispatch_table.reshape(tok_rows, device_count, per_dest)
     slot_weights = jnp.sum(jnp.where(placed, gates[:, :, None], 0.0), axis=1)
     slot_weights = slot_weights.reshape(tok_rows, device_count, per_dest)
-    outgoing = jnp.einsum(
-        "tsc,tm->scm", dispatch_table, expert_in, preferred_element_type=jnp.float32
-    ).astype(jnp.bfloat16)
     gate_up = w_gate_up[0]
     down_weight = w_down[0]
     other_gate_up = pair_swap(gate_up)
     other_down = pair_swap(down_weight)
-    arrived = lax.all_to_all(outgoing, ("seq", "exp"), split_axis=0, concat_axis=0, tiled=True)
-
-    def share_part(pair, down):
-        both = jnp.einsum("scd,gfd->scgf", arrived, pair, preferred_element_type=jnp.float32)
+
+    def share_part(rows, pair, down):
+        both = jnp.einsum("scd,gfd->scgf", rows, pair, preferred_element_type=jnp.float32)
         act = (jax.nn.silu(both[:, :, 0]) * both[:, :, 1]).astype(jnp.bfloat16)
         part = jnp.einsum("scf,fd->scd", act, down, preferred_element_type=jnp.float32)
         return part.astype(jnp.bfloat16).astype(jnp.float32)
 
-    part_sum = share_part(gate_up, down_weight) + share_part(other_gate_up, other_down)
-    returned = lax.all_to_all(
-        part_sum.astype(jnp.bfloat16), ("seq", "exp"), split_axis=0, concat_axis=0, tiled=True
-    )
-    routed = jnp.einsum(
-        "tsc,scm->tm",
-        slot_weights,
-        returned.astype(jnp.float32),
-        precision=lax.Precision.HIGHEST,
-        preferred_element_type=jnp.float32,
-    )
+    cuts = [0, per_dest // 2, per_dest]
+    routed = jnp.zeros((tok_rows, model_width), jnp.float32)
+    for low, high in zip(cuts[:-1], cuts[1:]):
+        outgoing = jnp.einsum(
+            "tsc,tm->scm",
+            dispatch_table[:, :, low:high],
+            expert_in,
+            preferred_element_type=jnp.float32,
+        ).astype(jnp.bfloat16)
+        arrived = lax.all_to_all(
+            outgoing, ("seq", "exp"), split_axis=0, concat_axis=0, tiled=True
+        )
+        part_sum = share_part(arrived, gate_up, down_weight) + share_part(
+            arrived, other_gate_up, other_down
+        )
+        returned = lax.all_to_all(
+            part_sum.astype(jnp.bfloat16), ("seq", "exp"), split_axis=0, concat_axis=0, tiled=True
+        )
+        routed = routed + jnp.einsum(
+            "tsc,scm->tm",
+            slot_weights[:, :, low:high],
+            returned.astype(jnp.float32),
+            precision=lax.Precision.HIGHEST,
+            preferred_element_type=jnp.float32,
+        )
     layer_rows = (middle.astype(jnp.float32) + routed).astype(jnp.bfloat16)
     prompt_count = prompt_lengths.shape[0]
     last_places = jnp.cumsum(prompt_lengths) - 1

time: 498 us -> 482 us (0.968); the launches traced: 497 us -> 474 us
  waiting for transfers between devices: 324 us -> 283 us
  starting transfers between devices: 20 us -> 29.3 us
  matrix products: 72.1 us -> 78.6 us
    all_to_all x1 -> x2, waiting for transfers between devices: 92.8 us -> 72 us  [per_device(): lax.all_to_all(part_sum.astype(jnp.bfloat16), ('seq', 'exp'), split_axis=...]
    all_to_all x1 -> x2, waiting for transfers between devices: 93.3 us -> 73.5 us  [per_device(): lax.all_to_all(outgoing, ('seq', 'exp'), split_axis=0, concat_axis=0, til...]
    dot_general x4 -> x8, matrix products: 30.4 us -> 38.9 us  [the longest x4 30.5 us: share_part(): jnp.einsum('scd,gfd->scgf', rows, pair, preferred_element_type=jnp.float32)]
  transfers between devices with their start and end apart: 8 -> 10, of which waited for: 4 -> 6; matrix products, arithmetic and copies ran while one was open for 15% -> 21% of each run, Pallas kernels for 0% -> 0%
where the time goes in v1:
time: 482 us; the launch traced here: 474 us
  waiting for transfers between devices  283 us (59%)
  matrix products  78.6 us (16%)
  blocking collectives  29.5 us (6%)
  starting transfers between devices  29.3 us (6%)
  local copies, waits for them, and re-layouts  24.6 us (5%)
  between operations  15.1 us (3%)
  other arithmetic  13.9 us (3%)
    all_gather x1, waiting for transfers between devices, per_device(): group_normed = lax.all_gather(normed, 'seq', axis=0, tiled=True)  126 us
    all_to_all x2, waiting for transfers between devices, per_device(): lax.all_to_all(outgoing, ('seq', 'exp'), split_axis=0, concat_axis=0, til...  73.5 us
    all_to_all x2, waiting for transfers between devices, per_device(): lax.all_to_all(part_sum.astype(jnp.bfloat16), ('seq', 'exp'), split_axis=...  72 us
    dot_general x4, matrix products, share_part(): jnp.einsum('scd,gfd->scgf', rows, pair, preferred_element_type=jnp.float32)  30.5 us
    all_to_all x1, blocking collectives, per_device(): lax.all_to_all(outgoing_rows, ('seq', 'exp'), split_axis=0, concat_axis=0...  19.4 us
    all_to_all x1, waiting for transfers between devices, per_device(): lax.all_to_all(heads_flat, 'seq', split_axis=0, concat_axis=1, tiled=True)  11.6 us
    all_to_all x1, blocking collectives, per_device(): lax.all_to_all(jnp.broadcast_to(local_stats[None], (device_count,) + loca...  10.1 us
    unnamed x41, local copies, waits for them, and re-layouts  9.94 us
  transfers between devices with their start and end apart: 10, of which 6 were waited for; matrix products, arithmetic and copies ran while one was open for 21% of the time, Pallas kernels for 0%

profile of v1, /device:TPU:0, one launch (start us, length us, event | category | flops | bytes accessed | tf_op | source)
XLA Modules:
  0.0 474.1 jit_solution(6275954380588577804)
XLA Ops:
  7.2 1.3 fusion.54
  8.5 2.0 fusion.56
  10.7 2.5 broadcast_in_dim.68
  13.2 7.4 %all-to-all-start = ((bf16[8,2,64,2048]{3,2,1,0:T(8,128)(2,1)}), bf16[8,2,64,2048]{3,2,1,0:T(8,128)(2,1)}, u32[]{:S(2)}, u32[]{:S(2)}) async-start(bf16[8,2,64,2048]{3,2,1,0:T(8,128)(2,1)} %broadcast_in_dim.68), calls=%async_computation | async-start | bytes 8388608 | tf_op jit(solution)/shard_map/all_to_all | solution.py:94
  20.8 8.8 %copy.126 = bf16[2048,3,2,128]{0,3,2,1:T(8,128)(2,1)} copy(bf16[2048,3,2,128]{3,2,1,0:T(2,128)(2,1)} %param.15) | data formatting | bytes 6291456 | tf_op args[3]
  30.7 0.9 compare_and_fusion
  31.7 1.1 fusion.59
  32.7 1.8 multiply_cosine_fusion
  34.5 126.0 %all-gather.2.cloned.1.call-done = bf16[1024,2048]{1,0:T(8,128)(2,1)} async-done(((bf16[128,2048]{1,0:T(8,128)(2,1)}), bf16[1024,2048]{1,0:T(8,128)(2,1)}) %all-gather.2.cloned.1.call-update) | async-done | bytes 4194320 | tf_op jit(solution)/shard_map/all_gather | solution.py:90
  160.5 6.2 %fusion.189 = f32[1024,768]{0,1:S(1)} fusion(bf16[1024,2048]{1,0:T(8,128)(2,1)} %all-gather.2.cloned.1.call-done, bf16[2048,768]{0,1:T(8,128)(2,1)} %bitcast.193), kind=kOutput, calls=%fused_computation.227 | convolution fusion | flops 3221225472 | bytes 10485760
  168.0 1.1 subtract_convert_fusion
  169.0 1.3 fusion.183
  170.3 1.5 fusion.178
  172.5 1.7 fusion.51
  174.2 1.9 fusion.173
  176.2 2.2 fusion.172
  178.4 2.0 fusion.52
  182.1 0.9 copy.136
  183.0 4.0 all-to-all-start.1
  187.1 1.7 reduce-window.11
  190.3 11.6 %all-to-all-done.1 = bf16[8,128,256]{1,2,0:T(8,128)(2,1)S(1)} async-done(((bf16[8,128,256]{1,2,0:T(8,128)(2,1)}), bf16[8,128,256]{1,2,0:T(8,128)(2,1)S(1)}, u32[]{:S(2)}, u32[]{:S(2)}) %all-to-all-start.1) | async-done | bytes 524320 | tf_op jit(solution)/shard_map/all_to_all | solution.py:135
  201.9 3.0 convolution_bitcast_fusion.3
  204.9 3.1 multiply_reduce_fusion
  208.8 2.4 copy.155
  211.2 3.8 all-to-all-start.4
  215.6 2.3 copy.147
  217.9 45.9 %all-to-all-done.4 = bf16[32,14,2048]{2,1,0:T(8,128)(2,1)} async-done(((bf16[32,14,2048]{2,1,0:T(8,128)(2,1)}), bf16[32,14,2048]{2,1,0:T(8,128)(2,1)}, u32[]{:S(2)}, u32[]{:S(2)}) %all-to-all-start.4) | async-done | bytes 1835040 | tf_op jit(solution)/shard_map/all_to_all | solution.py:187
  263.8 4.3 all-to-all-start.2
  268.6 7.7 %fusion.8 = f32[32,14,2,704]{3,0,2,1:T(8,128)S(1)} fusion(bf16[1,2,704,2048]{3,2,1,0:T(8,128)(2,1)} %param.20, bf16[32,14,2048,1]{2,1,0,3:T(8,128)(2,1)} %bitcast.40), kind=kOutput, calls=%fused_computation.8 | convolution fusion | flops 2583691264 | bytes 10125312 | tf_op jit(solution)/shard_map/scd,gfd->scgf/dot_general | solution.py:173
  276.2 1.6 convolution_convert_fusion.1
  277.9 7.5 %fusion.4 = f32[32,14,2,704]{3,0,1,2:T(8,128)S(1)} fusion(bf16[2,704,2048]{2,1,0:T(8,128)(2,1)} %collective-permute-done.1, bf16[32,14,2048]{2,1,0:T(8,128)(2,1)} %all-to-all-done.4), kind=kOutput, calls=%fused_computation.4 | convolution fusion | flops 2583691264 | bytes 10125312 | tf_op jit(solution)/shard_map/scd,gfd->scgf/dot_general | solution.py:173
  285.4 1.7 add_convert_fusion
  287.1 2.3 copy.160
  289.4 27.5 %all-to-all-done.2 = bf16[32,14,2048]{2,1,0:T(8,128)(2,1)} async-done(((bf16[32,14,2048]{2,1,0:T(8,128)(2,1)}), bf16[32,14,2048]{2,1,0:T(8,128)(2,1)}, u32[]{:S(2)}, u32[]{:S(2)}) %all-to-all-start.2) | async-done | bytes 1835040 | tf_op jit(solution)/shard_map/all_to_all | solution.py:187
  317.0 4.4 all-to-all-start.5
  321.4 7.7 %fusion.10 = f32[32,14,2,704]{3,0,2,1:T(8,128)S(1)} fusion(bf16[1,2,704,2048]{3,2,1,0:T(8,128)(2,1)} %param.20, bf16[32,14,2048,1]{2,1,0,3:T(8,128)(2,1)} %bitcast.28), kind=kOutput, calls=%fused_computation.10 | convolution fusion | flops 2583691264 | bytes 10125312 | tf_op jit(solution)/shard_map/scd,gfd->scgf/dot_general | solution.py:173
  329.0 1.6 convolution_convert_fusion.4
  330.7 7.7 %fusion.6 = f32[32,14,2,704]{3,0,2,1:T(8,128)S(1)} fusion(bf16[2,704,2048]{2,1,0:T(8,128)(2,1)} %collective-permute-done.1, bf16[32,14,2048,1]{2,1,0,3:T(8,128)(2,1)} %bitcast.28), kind=kOutput, calls=%fused_computation.6 | convolution fusion | flops 2583691264 | bytes 10125312 | tf_op jit(solution)/shard_map/scd,gfd->scgf/dot_general | solution.py:173
  338.4 1.7 add_convert_fusion.1
  340.1 2.4 copy.151
  342.4 27.8 %all-to-all-done.5 = bf16[32,14,2048]{2,1,0:T(8,128)(2,1)} async-done(((bf16[32,14,2048]{2,1,0:T(8,128)(2,1)}), bf16[32,14,2048]{2,1,0:T(8,128)(2,1)}, u32[]{:S(2)}, u32[]{:S(2)}) %all-to-all-start.5) | async-done | bytes 1835040 | tf_op jit(solution)/shard_map/all_to_all | solution.py:193
  370.2 4.4 all-to-all-start.3
  375.7 3.6 convolution_bitcast_fusion
  379.2 44.3 %all-to-all-done.3 = bf16[32,14,2048]{2,1,0:T(8,128)(2,1)} async-done(((bf16[32,14,2048]{2,1,0:T(8,128)(2,1)}), bf16[32,14,2048]{2,1,0:T(8,128)(2,1)}, u32[]{:S(2)}, u32[]{:S(2)}) %all-to-all-start.3) | async-done | bytes 1835040 | tf_op jit(solution)/shard_map/all_to_all | solution.py:193
  423.5 3.6 fusion.25
  427.6 19.4 %all_to_all.51 = bf16[32,4,2048]{2,1,0:T(4,128)(2,1)S(1)} all-to-all(bf16[32,4,2048]{2,1,0:T(4,128)(2,1)S(1)} %broadcast_in_dim.86), channel_id=1, replica_groups=mesh['seq'=8,'exp'=4] {'seq','exp'}, dimensions={0} | all-to-all | bytes 1048576 | tf_op jit(solution)/shard_map/all_to_all | solution.py:212
  447.2 8.4 %fusion.188 = (f32[16]{0:T(128)S(1)}, f32[16,3200]{1,0:T(8,128)S(1)}) fusion(bf16[3200,2048]{1,0:T(8,128)(2,1)} %param.23, f32[16,2048]{1,0:T(8,128)S(1)} %reduce_sum.159, f32[2048]{0:T(1024)S(1)} %copy-done.12, f32[16]{0:T(128)S(1)} %add_rsqrt_fusion), kind=kOutput, calls=%fused_computation.226 | convolution fusion | flops 209864688 | bytes 13451392 | tf_op jit(solution)/shard_map/dot_general | solution.py:219
  455.9 10.1 %all_to_all.52 = f32[32,2,16]{2,1,0:T(2,128)S(1)} all-to-all(f32[32,2,16]{2,1,0:T(2,128)S(1)} %broadcast_in_dim.87), channel_id=1, replica_groups=mesh['seq'=8,'exp'=4] {'seq','exp'}, dimensions={0} | all-to-all | bytes 8192 | tf_op jit(solution)/shard_map/all_to_all | solution.py:225
  (118 shorter events, 11.1 us)
Async XLA Ops:
  7.2 3.5 copy-start
  7.2 153.3 %all-gather.2.cloned.1.call-start = ((), (), s32[]{:S(2)}) async-start(), calls=%async_computation.8 | async-start | bytes 4718592 | tf_op jit(solution)/shard_map/all_gather | solution.py:90
  13.2 7.4 %copy-start.17 = (s32[1,4]{1,0:T(1,128)S(1)}, s32[1,4]{1,0:T(1,128)}, u32[]{:S(2)}) copy-start(s32[1,4]{1,0:T(1,128)} %param.13) | copy-start | bytes 52
  13.2 168.0 %all-to-all-start = ((bf16[8,2,64,2048]{3,2,1,0:T(8,128)(2,1)}), bf16[8,2,64,2048]{3,2,1,0:T(8,128)(2,1)}, u32[]{:S(2)}, u32[]{:S(2)}) async-start(bf16[8,2,64,2048]{3,2,1,0:T(8,128)(2,1)} %broadcast_in_dim.68), calls=%async_computation | async-start | bytes 8388608 | tf_op jit(solution)/shard_map/all_to_all | solution.py:94
  166.9 1.0 copy-start.5
  166.9 1.0 copy-start.6
  169.0 2.8 copy-start.4
  172.5 1.8 copy-start.8
  174.2 2.0 copy-start.7
  178.4 2.1 copy-start.18
  180.5 1.2 copy-start.10
  181.1 23.8 %collective-permute-start = (bf16[16,64,2048]{2,1,0:T(8,128)(2,1)}, bf16[16,64,2048]{2,1,0:T(8,128)(2,1)}, u32[]{:S(2)}, u32[]{:S(2)}) collective-permute-start(bf16[16,64,2048]{2,1,0:T(8,128)(2,1)} %bitcast.1), channel_id=1, source_target_pairs={{0,1},{1,0},{2,3},{3,2},{4,5},{5,4},{6,7},{7,6},{8,9},{9,8},{10,11... | collective-permute-start | bytes 12582920 | tf_op jit(solution)/shard_map/ppermute | solution.py:52
  181.2 96.6 %collective-permute-start.1 = (bf16[2,704,2048]{2,1,0:T(8,128)(2,1)}, bf16[2,704,2048]{2,1,0:T(8,128)(2,1)}, u32[]{:S(2)}, u32[]{:S(2)}) collective-permute-start(bf16[2,704,2048]{2,1,0:T(8,128)(2,1)} %bitcast.209), channel_id=1, source_target_pairs={{0,1},{1,0},{2,3},{3,2},{4,5},{5,4},{6,7},{7,6},{8,9},{9,8},{10,11... | collective-permute-start | bytes 17301512 | tf_op jit(solution)/shard_map/ppermute | solution.py:52
  183.0 18.9 %all-to-all-start.1 = ((bf16[8,128,256]{1,2,0:T(8,128)(2,1)}), bf16[8,128,256]{1,2,0:T(8,128)(2,1)S(1)}, u32[]{:S(2)}, u32[]{:S(2)}) async-start(bf16[8,128,256]{1,2,0:T(8,128)(2,1)} %copy.136), calls=%async_computation.1 | async-start | bytes 1048576 | tf_op jit(solution)/shard_map/all_to_all | solution.py:135
  201.9 3.0 copy-start.2
  204.9 3.1 copy-start.11
  211.2 52.6 %all-to-all-start.4 = ((bf16[32,14,2048]{2,1,0:T(8,128)(2,1)}), bf16[32,14,2048]{2,1,0:T(8,128)(2,1)}, u32[]{:S(2)}, u32[]{:S(2)}) async-start(bf16[32,14,2048]{2,1,0:T(8,128)(2,1)} %copy.155), calls=%async_computation.4 | async-start | bytes 4194304 | tf_op jit(solution)/shard_map/all_to_all | solution.py:187
  263.8 53.2 %all-to-all-start.2 = ((bf16[32,14,2048]{2,1,0:T(8,128)(2,1)}), bf16[32,14,2048]{2,1,0:T(8,128)(2,1)}, u32[]{:S(2)}, u32[]{:S(2)}) async-start(bf16[32,14,2048]{2,1,0:T(8,128)(2,1)} %copy.147), calls=%async_computation.2 | async-start | bytes 4194304 | tf_op jit(solution)/shard_map/all_to_all | solution.py:187
  268.1 17.3 %collective-permute-start.2 = (bf16[704,2048]{1,0:T(8,128)(2,1)}, bf16[704,2048]{1,0:T(8,128)(2,1)S(1)}, u32[]{:S(2)}, u32[]{:S(2)}) collective-permute-start(bf16[704,2048]{1,0:T(8,128)(2,1)} %bitcast.210), channel_id=1, source_target_pairs={{0,1},{1,0},{2,3},{3,2},{4,5},{5,4},{6,7},{7,6},{8,9},{9,8},{10,11... | collective-permute-start | bytes 8650760 | tf_op jit(solution)/shard_map/ppermute | solution.py:52
  268.6 7.7 %copy-start.13 = (bf16[1,704,2048]{2,1,0:T(8,128)(2,1)S(1)}, bf16[1,704,2048]{2,1,0:T(8,128)(2,1)}, u32[]{:S(2)}) copy-start(bf16[1,704,2048]{2,1,0:T(8,128)(2,1)} %param.21) | copy-start | bytes 8650756
  285.4 1.7 copy-start.15
  317.0 53.2 %all-to-all-start.5 = ((bf16[32,14,2048]{2,1,0:T(8,128)(2,1)}), bf16[32,14,2048]{2,1,0:T(8,128)(2,1)}, u32[]{:S(2)}, u32[]{:S(2)}) async-start(bf16[32,14,2048]{2,1,0:T(8,128)(2,1)} %copy.160), calls=%async_computation.5 | async-start | bytes 4194304 | tf_op jit(solution)/shard_map/all_to_all | solution.py:193
  321.3 7.7 %copy-start.14 = (bf16[1,704,2048]{2,1,0:T(8,128)(2,1)S(1)}, bf16[1,704,2048]{2,1,0:T(8,128)(2,1)}, u32[]{:S(2)}) copy-start(bf16[1,704,2048]{2,1,0:T(8,128)(2,1)} %param.21) | copy-start | bytes 8650756
  330.7 7.7 %copy-start.16 = (bf16[704,2048]{1,0:T(8,128)(2,1)S(1)}, bf16[704,2048]{1,0:T(8,128)(2,1)}, u32[]{:S(2)}) copy-start(bf16[704,2048]{1,0:T(8,128)(2,1)} %copy-done.15) | copy-start | bytes 8650756
  342.4 32.2 %copy-start.9 = (bf16[2048,16]{0,1:T(8,128)(2,1)S(1)}, bf16[2048,16]{0,1:T(8,128)(2,1)}, u32[]{:S(2)}) copy-start(bf16[2048,16]{0,1:T(8,128)(2,1)} %param.18) | copy-start | bytes 196612
  370.2 53.3 %all-to-all-start.3 = ((bf16[32,14,2048]{2,1,0:T(8,128)(2,1)}), bf16[32,14,2048]{2,1,0:T(8,128)(2,1)}, u32[]{:S(2)}, u32[]{:S(2)}) async-start(bf16[32,14,2048]{2,1,0:T(8,128)(2,1)} %copy.151), calls=%async_computation.3 | async-start | bytes 4194304 | tf_op jit(solution)/shard_map/all_to_all | solution.py:193
  427.1 20.0 %copy-start.3 = (bf16[128,2048]{1,0:T(8,128)(2,1)}, bf16[128,2048]{1,0:T(8,128)(2,1)S(1)}, u32[]{:S(2)}) copy-start(bf16[128,2048]{1,0:T(8,128)(2,1)S(1)} %fusion.25) | copy-start | bytes 1572868
  427.5 19.7 %copy-start.12 = (f32[2048]{0:T(1024)S(1)}, f32[2048]{0:T(1024)}, u32[]{:S(2)}) copy-start(f32[2048]{0:T(1024)} %param.22) | copy-start | bytes 24580
  447.2 19.7 %copy-start.1 = (bf16[2,128,2048]{2,1,0:T(8,128)(2,1)S(1)}, bf16[2,128,2048]{2,1,0:T(8,128)(2,1)}, u32[]{:S(2)}) copy-start(bf16[2,128,2048]{2,1,0:T(8,128)(2,1)} %param.16) | copy-start | bytes 3145732
Sparse Core Ops, SparseCore 0:
  10.7 149.7 all-gather.1

commit v2 on v1

--- a/solution.py
+++ b/solution.py
@@ -88,16 +88,17 @@
     segment, offset = segment_layout(prompt_lengths, group_tokens)
     normed = rms_scale(token_rows, attn_gain).astype(jnp.bfloat16)
     group_normed = lax.all_gather(normed, "seq", axis=0, tiled=True)
-    core = lax.axis_index("exp") % 2
-    half_size = head_size // 2
-    own_half = lax.dynamic_slice_in_dim(w_out, core * half_size, half_size, axis=1)
-    own_weight = lax.all_to_all(
-        jnp.broadcast_to(own_half[None], (seq_count,) + own_half.shape),
+    part_size = head_size // group_count
+    own_part = lax.dynamic_slice_in_dim(
+        w_out, lax.axis_index("exp") * part_size, part_size, axis=1
+    )
+    seq_part = lax.all_to_all(
+        jnp.broadcast_to(own_part[None], (seq_count,) + own_part.shape),
         "seq",
         split_axis=0,
         concat_axis=0,
         tiled=True,
-    ).reshape((-1,) + own_half.shape[1:])
+    ).reshape((1, -1) + own_part.shape[1:])
     qkv = jnp.einsum("td,dshe->tshe", group_normed, w_qkv, preferred_element_type=jnp.float32)
     query = rotary(qkv[:, 0], offset).astype(jnp.bfloat16)
     keys = rotary(qkv[:, 1], offset).astype(jnp.bfloat16)
@@ -130,16 +131,32 @@
         ).astype(jnp.bfloat16)
 
     blocks = jnp.concatenate([one_block(index) for index in range(block_count)], axis=0)
-    own_weight, blocks = lax.optimization_barrier((own_weight, blocks))
     heads_flat = blocks.reshape(group_tokens, head_count * head_size)
     regrouped = lax.all_to_all(heads_flat, "seq", split_axis=0, concat_axis=1, tiled=True)
-    other_weight = pair_swap(own_weight)
-    regrouped = regrouped.reshape(tok_rows, -1, head_size)
-    own_heads = lax.dynamic_slice_in_dim(regrouped, core * half_size, half_size, axis=2)
-    other_heads = lax.dynamic_slice_in_dim(regrouped, (1 - core) * half_size, half_size, axis=2)
-    mixed = jnp.einsum(
-        "thd,hdo->to", own_heads, own_weight, preferred_element_type=jnp.float32
-    ) + jnp.einsum("thd,hdo->to", other_heads, other_weight, preferred_element_type=jnp.float32)
+    exp_index = lax.axis_index("exp")
+    x_count = group_count // 2
+    pieces, owners = [seq_part[0]], [exp_index]
+    for step in range(1, x_count):
+        pieces.append(
+            lax.ppermute(
+                seq_part[0],
+                "exp",
+                [(i, (i + 2 * step) % group_count) for i in range(group_count)],
+            )
+        )
+        owners.append((exp_index - 2 * step) % group_count)
+    partner_pieces = pair_swap(jnp.stack(pieces))
+    pieces = pieces + [partner_pieces[step] for step in range(x_count)]
+    owners = owners + [owner ^ 1 for owner in owners]
+    regrouped = regrouped.reshape(tok_rows, -1, group_count, part_size)
+    mixed = jnp.zeros((tok_rows, model_width), jnp.float32)
+    for piece, owner in zip(pieces, owners):
+        mixed = mixed + jnp.einsum(
+            "thd,hdo->to",
+            lax.dynamic_index_in_dim(regrouped, owner, axis=2, keepdims=False),
+            piece,
+            preferred_element_type=jnp.float32,
+        )
     middle = (token_rows.astype(jnp.float32) + mixed).astype(jnp.bfloat16)
     expert_in = rms_scale(middle, moe_gain).astype(jnp.bfloat16)
     logits = jnp.dot(expert_in, router, preferred_element_type=jnp.float32)

time: 482 us -> 482 us (level)
  waiting for transfers between devices: 283 us -> 184 us
  blocking collectives: 29.5 us -> 123 us
  matrix products: 78.6 us -> 85.3 us
  other arithmetic: 13.9 us -> 19.3 us
    all_gather x1, waiting for transfers between devices: 126 us -> 0.01 us  [per_device(): group_normed = lax.all_gather(normed, 'seq', axis=0, tiled=True)]
    all_to_all x0 -> x1, blocking collectives: none -> 93.4 us  [per_device(): lax.all_to_all(jnp.broadcast_to(own_part[None], (seq_count,) + own_part.s...]
    ppermute x0 -> x1, waiting for transfers between devices: none -> 26.9 us  [per_device(): lax.ppermute(seq_part[0], 'exp', [(i, (i + 2 * step) % group_count) for i...]
    all_to_all x1 -> x0, starting transfers between devices: 7.41 us -> none  [per_device(): lax.all_to_all(jnp.broadcast_to(own_half[None], (seq_count,) + own_half.s...]
    another operation x5 -> x6, other arithmetic: 3.22 us -> 8.57 us
    unnamed x41 -> x49, local copies, waits for them, and re-layouts: 9.94 us -> 9.93 us
  transfers between devices with their start and end apart: 10 -> 10, of which waited for: 6 -> 6; matrix products, arithmetic and copies ran while one was open for 21% -> 23% of each run, Pallas kernels for 0% -> 0%
where the time goes in v2:
time: 482 us; the launch traced here: 474 us
  waiting for transfers between devices  184 us (38%)
  blocking collectives  123 us (26%)
  matrix products  85.3 us (18%)
  starting transfers between devices  24.8 us (5%)
  local copies, waits for them, and re-layouts  22.4 us (5%)
  other arithmetic  19.3 us (4%)
  between operations  15.1 us (3%)
    all_to_all x1, blocking collectives, per_device(): lax.all_to_all(jnp.broadcast_to(own_part[None], (seq_count,) + own_part.s...  93.4 us
    all_to_all x2, waiting for transfers between devices, per_device(): lax.all_to_all(outgoing, ('seq', 'exp'), split_axis=0, concat_axis=0, til...  73.4 us
    all_to_all x2, waiting for transfers between devices, per_device(): lax.all_to_all(part_sum.astype(jnp.bfloat16), ('seq', 'exp'), split_axis=...  72 us
    dot_general x4, matrix products, share_part(): jnp.einsum('scd,gfd->scgf', rows, pair, preferred_element_type=jnp.float32)  30.5 us
    ppermute x1, waiting for transfers between devices, per_device(): lax.ppermute(seq_part[0], 'exp', [(i, (i + 2 * step) % group_count) for i...  26.9 us
    all_to_all x1, blocking collectives, per_device(): lax.all_to_all(outgoing_rows, ('seq', 'exp'), split_axis=0, concat_axis=0...  19.4 us
    all_to_all x1, waiting for transfers between devices, per_device(): lax.all_to_all(heads_flat, 'seq', split_axis=0, concat_axis=1, tiled=True)  11.7 us
    all_to_all x1, blocking collectives, per_device(): lax.all_to_all(jnp.broadcast_to(local_stats[None], (device_count,) + loca...  10.1 us
  transfers between devices with their start and end apart: 10, of which 6 were waited for; matrix products, arithmetic and copies ran while one was open for 23% of the time, Pallas kernels for 0%

profile of v2, /device:TPU:0, one launch (start us, length us, event | category | flops | bytes accessed | tf_op | source)
XLA Modules:
  0.0 473.9 jit_solution(17904789338687338779)
XLA Ops:
  8.5 2.0 fusion.58
  10.9 93.4 %all_to_all.51 = bf16[8,2,32,2048]{3,2,1,0:T(8,128)(2,1)S(1)} all-to-all(bf16[8,2,32,2048]{3,2,1,0:T(8,128)(2,1)S(1)} %broadcast_in_dim.80), channel_id=1, replica_groups=mesh['seq'=8,'exp'=4] {'seq'}, dimensions={0} | all-to-all | bytes 4194304 | tf_op jit(solution)/shard_map/all_to_all | solution.py:95
  104.3 1.5 collective-permute-start
  106.1 8.7 %copy.125 = bf16[2048,3,2,128]{0,3,2,1:T(8,128)(2,1)} copy(bf16[2048,3,2,128]{3,2,1,0:T(2,128)(2,1)} %param.15) | data formatting | bytes 6291456 | tf_op args[3]
  118.2 1.8 multiply_cosine_fusion
  120.0 26.9 %collective-permute-done = bf16[16,32,2048]{2,1,0:T(8,128)(2,1)} collective-permute-done((bf16[16,32,2048]{2,1,0:T(8,128)(2,1)S(1)}, bf16[16,32,2048]{2,1,0:T(8,128)(2,1)}, u32[]{:S(2)}, u32[]{:S(2)}) %collective-permute-start) | collective-permute-done | bytes 2097184 | tf_op jit(solution)/shard_map/ppermute | solution.py:141
  146.9 4.0 pad_maximum_fusion
  150.9 6.2 %fusion.199 = f32[1024,768]{0,1:S(1)} fusion(bf16[1024,2048]{1,0:T(8,128)(2,1)} %all-gather.2.cloned.1.call-done, bf16[2048,768]{0,1:T(8,128)(2,1)} %bitcast.226), kind=kOutput, calls=%fused_computation.242 | convolution fusion | flops 3221225472 | bytes 10485760
  157.1 1.4 convert.17
  160.8 1.4 fusion.193
  162.2 1.6 fusion.188
  164.9 2.2 fusion.52
  167.1 2.4 fusion.53
  169.5 2.9 fusion.183
  172.4 2.3 fusion.182
  174.7 2.1 fusion.54
  176.9 1.7 fusion.55
  179.6 5.9 %all-to-all-start = ((bf16[8,128,256]{1,2,0:T(8,128)(2,1)}), bf16[8,128,256]{1,2,0:T(8,128)(2,1)S(1)}, u32[]{:S(2)}, u32[]{:S(2)}) async-start(bf16[8,128,256]{1,2,0:T(8,128)(2,1)} %copy.135), calls=%async_computation | async-start | bytes 1048576 | tf_op jit(solution)/shard_map/all_to_all | solution.py:135
  185.7 1.7 reduce-window.11
  188.9 11.7 %all-to-all-done = bf16[8,128,256]{1,2,0:T(8,128)(2,1)S(1)} async-done(((bf16[8,128,256]{1,2,0:T(8,128)(2,1)}), bf16[8,128,256]{1,2,0:T(8,128)(2,1)S(1)}, u32[]{:S(2)}, u32[]{:S(2)}) %all-to-all-start) | async-done | bytes 524320 | tf_op jit(solution)/shard_map/all_to_all | solution.py:135
  201.2 2.1 convolution_bitcast_fusion.3
  203.3 2.1 convolution_bitcast_fusion.2
  205.4 2.4 multiply_reduce_fusion
  208.6 2.4 copy.154
  211.0 3.8 all-to-all-start.4
  215.4 2.3 copy.146
  217.8 45.9 %all-to-all-done.4 = bf16[32,14,2048]{2,1,0:T(8,128)(2,1)} async-done(((bf16[32,14,2048]{2,1,0:T(8,128)(2,1)}), bf16[32,14,2048]{2,1,0:T(8,128)(2,1)}, u32[]{:S(2)}, u32[]{:S(2)}) %all-to-all-start.4) | async-done | bytes 1835040 | tf_op jit(solution)/shard_map/all_to_all | solution.py:204
  263.7 4.3 all-to-all-start.2
  268.4 7.7 %fusion.8 = f32[32,14,2,704]{3,0,2,1:T(8,128)S(1)} fusion(bf16[1,2,704,2048]{3,2,1,0:T(8,128)(2,1)} %param.20, bf16[32,14,2048,1]{2,1,0,3:T(8,128)(2,1)} %bitcast.50), kind=kOutput, calls=%fused_computation.8 | convolution fusion | flops 2583691264 | bytes 10125312 | tf_op jit(solution)/shard_map/scd,gfd->scgf/dot_general | solution.py:190
  276.1 1.6 convolution_convert_fusion.1
  277.8 7.5 %fusion.4 = f32[32,14,2,704]{3,0,1,2:T(8,128)S(1)} fusion(bf16[2,704,2048]{2,1,0:T(8,128)(2,1)} %collective-permute-done.2, bf16[32,14,2048]{2,1,0:T(8,128)(2,1)} %all-to-all-done.4), kind=kOutput, calls=%fused_computation.4 | convolution fusion | flops 2583691264 | bytes 10125312 | tf_op jit(solution)/shard_map/scd,gfd->scgf/dot_general | solution.py:190
  285.3 1.7 add_convert_fusion
  287.0 2.4 copy.159
  289.4 27.5 %all-to-all-done.2 = bf16[32,14,2048]{2,1,0:T(8,128)(2,1)} async-done(((bf16[32,14,2048]{2,1,0:T(8,128)(2,1)}), bf16[32,14,2048]{2,1,0:T(8,128)(2,1)}, u32[]{:S(2)}, u32[]{:S(2)}) %all-to-all-start.2) | async-done | bytes 1835040 | tf_op jit(solution)/shard_map/all_to_all | solution.py:204
  316.9 4.4 all-to-all-start.5
  321.2 7.7 %fusion.10 = f32[32,14,2,704]{3,0,2,1:T(8,128)S(1)} fusion(bf16[1,2,704,2048]{3,2,1,0:T(8,128)(2,1)} %param.20, bf16[32,14,2048,1]{2,1,0,3:T(8,128)(2,1)} %bitcast.38), kind=kOutput, calls=%fused_computation.10 | convolution fusion | flops 2583691264 | bytes 10125312 | tf_op jit(solution)/shard_map/scd,gfd->scgf/dot_general | solution.py:190
  328.9 1.6 convolution_convert_fusion.4
  330.6 7.7 %fusion.6 = f32[32,14,2,704]{3,0,2,1:T(8,128)S(1)} fusion(bf16[2,704,2048]{2,1,0:T(8,128)(2,1)} %collective-permute-done.2, bf16[32,14,2048,1]{2,1,0,3:T(8,128)(2,1)} %bitcast.38), kind=kOutput, calls=%fused_computation.6 | convolution fusion | flops 2583691264 | bytes 10125312 | tf_op jit(solution)/shard_map/scd,gfd->scgf/dot_general | solution.py:190
  338.3 1.7 add_convert_fusion.1
  339.9 2.4 copy.150
  342.3 27.8 %all-to-all-done.5 = bf16[32,14,2048]{2,1,0:T(8,128)(2,1)} async-done(((bf16[32,14,2048]{2,1,0:T(8,128)(2,1)}), bf16[32,14,2048]{2,1,0:T(8,128)(2,1)}, u32[]{:S(2)}, u32[]{:S(2)}) %all-to-all-start.5) | async-done | bytes 1835040 | tf_op jit(solution)/shard_map/all_to_all | solution.py:210
  370.1 4.4 all-to-all-start.3
  375.5 3.6 convolution_bitcast_fusion
  379.1 44.3 %all-to-all-done.3 = bf16[32,14,2048]{2,1,0:T(8,128)(2,1)} async-done(((bf16[32,14,2048]{2,1,0:T(8,128)(2,1)}), bf16[32,14,2048]{2,1,0:T(8,128)(2,1)}, u32[]{:S(2)}, u32[]{:S(2)}) %all-to-all-start.3) | async-done | bytes 1835040 | tf_op jit(solution)/shard_map/all_to_all | solution.py:210
  423.4 3.6 fusion.27
  427.4 19.4 %all_to_all.52 = bf16[32,4,2048]{2,1,0:T(4,128)(2,1)S(1)} all-to-all(bf16[32,4,2048]{2,1,0:T(4,128)(2,1)S(1)} %broadcast_in_dim.86), channel_id=1, replica_groups=mesh['seq'=8,'exp'=4] {'seq','exp'}, dimensions={0} | all-to-all | bytes 1048576 | tf_op jit(solution)/shard_map/all_to_all | solution.py:229
  447.1 8.4 %fusion.198 = (f32[16]{0:T(128)S(1)}, f32[16,3200]{1,0:T(8,128)S(1)}) fusion(bf16[3200,2048]{1,0:T(8,128)(2,1)} %param.23, f32[16,2048]{1,0:T(8,128)S(1)} %reduce_sum.159, f32[2048]{0:T(1024)S(1)} %copy-done.16, f32[16]{0:T(128)S(1)} %add_rsqrt_fusion), kind=kOutput, calls=%fused_computation.241 | convolution fusion | flops 209864688 | bytes 13451392 | tf_op jit(solution)/shard_map/dot_general | solution.py:236
  455.8 10.1 %all_to_all.53 = f32[32,2,16]{2,1,0:T(2,128)S(1)} all-to-all(f32[32,2,16]{2,1,0:T(2,128)S(1)} %broadcast_in_dim.87), channel_id=1, replica_groups=mesh['seq'=8,'exp'=4] {'seq','exp'}, dimensions={0} | all-to-all | bytes 8192 | tf_op jit(solution)/shard_map/all_to_all | solution.py:242
  (130 shorter events, 16.4 us)
Async XLA Ops:
  7.2 3.4 copy-start
  7.2 143.7 %all-gather.2.cloned.1.call-start = ((), (), s32[]{:S(2)}) async-start(), calls=%async_computation.8 | async-start | bytes 4718592 | tf_op jit(solution)/shard_map/all_gather | solution.py:90
  10.9 95.0 %copy-start.21 = (s32[1,4]{1,0:T(1,128)S(1)}, s32[1,4]{1,0:T(1,128)}, u32[]{:S(2)}) copy-start(s32[1,4]{1,0:T(1,128)} %param.13) | copy-start | bytes 52
  104.3 42.6 %collective-permute-start = (bf16[16,32,2048]{2,1,0:T(8,128)(2,1)S(1)}, bf16[16,32,2048]{2,1,0:T(8,128)(2,1)}, u32[]{:S(2)}, u32[]{:S(2)}) collective-permute-start(bf16[16,32,2048]{2,1,0:T(8,128)(2,1)S(1)} %bitcast.221), channel_id=1, source_target_pairs={{0,2},{1,3},{2,0},{3,1},{4,6},{5,7},{6,4},{7,5},{8,10},{9,11},{10,... | collective-permute-start | bytes 6291464 | tf_op jit(solution)/shard_map/ppermute | solution.py:141
  105.9 171.9 %collective-permute-start.2 = (bf16[2,704,2048]{2,1,0:T(8,128)(2,1)}, bf16[2,704,2048]{2,1,0:T(8,128)(2,1)}, u32[]{:S(2)}, u32[]{:S(2)}) collective-permute-start(bf16[2,704,2048]{2,1,0:T(8,128)(2,1)} %bitcast.39), channel_id=1, source_target_pairs={{0,1},{1,0},{2,3},{3,2},{4,5},{5,4},{6,7},{7,6},{8,9},{9,8},{10,11... | collective-permute-start | bytes 17301512 | tf_op jit(solution)/shard_map/ppermute | solution.py:52
  106.1 8.9 %copy-start.14 = (s32[1,128,6]{1,0,2:T(1,128)S(1)}, s32[1,128,6]{1,0,2:T(1,128)}, u32[]{:S(2)}) copy-start(s32[1,128,6]{1,0,2:T(1,128)} %param.19) | copy-start | bytes 9220
  150.9 50.2 %collective-permute-start.1 = (bf16[2,16,32,2048]{3,2,1,0:T(8,128)(2,1)}, bf16[2,16,32,2048]{3,2,1,0:T(8,128)(2,1)}, u32[]{:S(2)}, u32[]{:S(2)}) collective-permute-start(bf16[2,16,32,2048]{3,2,1,0:T(8,128)(2,1)} %pad_maximum_fusion), channel_id=1, source_target_pairs={{0,1},{1,0},{2,3},{3,2},{4,5},{5,4},{6,7},{7,6},{8,9},{9,8},{10,11... | collective-permute-start | bytes 12582920 | tf_op jit(solution)/shard_map/ppermute | solution.py:52
  158.5 0.9 copy-start.8
  158.5 1.0 copy-start.9
  160.8 3.0 copy-start.5
  160.8 3.0 copy-start.6
  160.8 3.0 copy-start.7
  169.5 2.9 copy-start.10
  174.7 2.2 copy-start.22
  176.9 1.7 copy-start.11
  176.9 1.7 copy-start.12
  179.6 21.0 %all-to-all-start = ((bf16[8,128,256]{1,2,0:T(8,128)(2,1)}), bf16[8,128,256]{1,2,0:T(8,128)(2,1)S(1)}, u32[]{:S(2)}, u32[]{:S(2)}) async-start(bf16[8,128,256]{1,2,0:T(8,128)(2,1)} %copy.135), calls=%async_computation | async-start | bytes 1048576 | tf_op jit(solution)/shard_map/all_to_all | solution.py:135
  200.7 2.6 copy-start.3
  203.2 2.1 copy-start.2
  205.4 2.4 copy-start.15
  211.0 52.7 %all-to-all-start.4 = ((bf16[32,14,2048]{2,1,0:T(8,128)(2,1)}), bf16[32,14,2048]{2,1,0:T(8,128)(2,1)}, u32[]{:S(2)}, u32[]{:S(2)}) async-start(bf16[32,14,2048]{2,1,0:T(8,128)(2,1)} %copy.154), calls=%async_computation.4 | async-start | bytes 4194304 | tf_op jit(solution)/shard_map/all_to_all | solution.py:204
  263.7 53.2 %all-to-all-start.2 = ((bf16[32,14,2048]{2,1,0:T(8,128)(2,1)}), bf16[32,14,2048]{2,1,0:T(8,128)(2,1)}, u32[]{:S(2)}, u32[]{:S(2)}) async-start(bf16[32,14,2048]{2,1,0:T(8,128)(2,1)} %copy.146), calls=%async_computation.2 | async-start | bytes 4194304 | tf_op jit(solution)/shard_map/all_to_all | solution.py:204
  268.0 17.3 %collective-permute-start.3 = (bf16[704,2048]{1,0:T(8,128)(2,1)}, bf16[704,2048]{1,0:T(8,128)(2,1)S(1)}, u32[]{:S(2)}, u32[]{:S(2)}) collective-permute-start(bf16[704,2048]{1,0:T(8,128)(2,1)} %bitcast.244), channel_id=1, source_target_pairs={{0,1},{1,0},{2,3},{3,2},{4,5},{5,4},{6,7},{7,6},{8,9},{9,8},{10,11... | collective-permute-start | bytes 8650760 | tf_op jit(solution)/shard_map/ppermute | solution.py:52
  268.4 7.7 %copy-start.17 = (bf16[1,704,2048]{2,1,0:T(8,128)(2,1)S(1)}, bf16[1,704,2048]{2,1,0:T(8,128)(2,1)}, u32[]{:S(2)}) copy-start(bf16[1,704,2048]{2,1,0:T(8,128)(2,1)} %param.21) | copy-start | bytes 8650756
  285.3 1.7 copy-start.19
  316.9 53.2 %all-to-all-start.5 = ((bf16[32,14,2048]{2,1,0:T(8,128)(2,1)}), bf16[32,14,2048]{2,1,0:T(8,128)(2,1)}, u32[]{:S(2)}, u32[]{:S(2)}) async-start(bf16[32,14,2048]{2,1,0:T(8,128)(2,1)} %copy.159), calls=%async_computation.5 | async-start | bytes 4194304 | tf_op jit(solution)/shard_map/all_to_all | solution.py:210
  321.2 7.7 %copy-start.18 = (bf16[1,704,2048]{2,1,0:T(8,128)(2,1)S(1)}, bf16[1,704,2048]{2,1,0:T(8,128)(2,1)}, u32[]{:S(2)}) copy-start(bf16[1,704,2048]{2,1,0:T(8,128)(2,1)} %param.21) | copy-start | bytes 8650756
  330.6 7.7 %copy-start.20 = (bf16[704,2048]{1,0:T(8,128)(2,1)S(1)}, bf16[704,2048]{1,0:T(8,128)(2,1)}, u32[]{:S(2)}) copy-start(bf16[704,2048]{1,0:T(8,128)(2,1)} %copy-done.19) | copy-start | bytes 8650756
  342.3 32.2 %copy-start.13 = (bf16[2048,16]{0,1:T(8,128)(2,1)S(1)}, bf16[2048,16]{0,1:T(8,128)(2,1)}, u32[]{:S(2)}) copy-start(bf16[2048,16]{0,1:T(8,128)(2,1)} %param.18) | copy-start | bytes 196612
  370.1 53.3 %all-to-all-start.3 = ((bf16[32,14,2048]{2,1,0:T(8,128)(2,1)}), bf16[32,14,2048]{2,1,0:T(8,128)(2,1)}, u32[]{:S(2)}, u32[]{:S(2)}) async-start(bf16[32,14,2048]{2,1,0:T(8,128)(2,1)} %copy.150), calls=%async_computation.3 | async-start | bytes 4194304 | tf_op jit(solution)/shard_map/all_to_all | solution.py:210
  426.9 20.0 %copy-start.4 = (bf16[128,2048]{1,0:T(8,128)(2,1)}, bf16[128,2048]{1,0:T(8,128)(2,1)S(1)}, u32[]{:S(2)}) copy-start(bf16[128,2048]{1,0:T(8,128)(2,1)S(1)} %fusion.27) | copy-start | bytes 1572868
  427.4 19.7 %copy-start.16 = (f32[2048]{0:T(1024)S(1)}, f32[2048]{0:T(1024)}, u32[]{:S(2)}) copy-start(f32[2048]{0:T(1024)} %param.22) | copy-start | bytes 24580
  447.1 19.7 %copy-start.1 = (bf16[2,128,2048]{2,1,0:T(8,128)(2,1)S(1)}, bf16[2,128,2048]{2,1,0:T(8,128)(2,1)}, u32[]{:S(2)}) copy-start(bf16[2,128,2048]{2,1,0:T(8,128)(2,1)} %param.16) | copy-start | bytes 3145732
Sparse Core Ops, SparseCore 0:
  10.7 106.6 all-gather.1

commit v3 on v2

--- a/solution.py
+++ b/solution.py
@@ -99,6 +99,18 @@
         concat_axis=0,
         tiled=True,
     ).reshape((1, -1) + own_part.shape[1:])
+    exp_index = lax.axis_index("exp")
+    x_count = group_count // 2
+    x_pieces, x_owners = [], []
+    for step in range(1, x_count):
+        x_pieces.append(
+            lax.ppermute(
+                seq_part[0],
+                "exp",
+                [(i, (i + 2 * step) % group_count) for i in range(group_count)],
+            )
+        )
+        x_owners.append((exp_index - 2 * step) % group_count)
     qkv = jnp.einsum("td,dshe->tshe", group_normed, w_qkv, preferred_element_type=jnp.float32)
     query = rotary(qkv[:, 0], offset).astype(jnp.bfloat16)
     keys = rotary(qkv[:, 1], offset).astype(jnp.bfloat16)
@@ -131,20 +143,10 @@
         ).astype(jnp.bfloat16)
 
     blocks = jnp.concatenate([one_block(index) for index in range(block_count)], axis=0)
+    x_pieces, blocks = lax.optimization_barrier((x_pieces, blocks))
     heads_flat = blocks.reshape(group_tokens, head_count * head_size)
     regrouped = lax.all_to_all(heads_flat, "seq", split_axis=0, concat_axis=1, tiled=True)
-    exp_index = lax.axis_index("exp")
-    x_count = group_count // 2
-    pieces, owners = [seq_part[0]], [exp_index]
-    for step in range(1, x_count):
-        pieces.append(
-            lax.ppermute(
-                seq_part[0],
-                "exp",
-                [(i, (i + 2 * step) % group_count) for i in range(group_count)],
-            )
-        )
-        owners.append((exp_index - 2 * step) % group_count)
+    pieces, owners = [seq_part[0]] + x_pieces, [exp_index] + x_owners
     partner_pieces = pair_swap(jnp.stack(pieces))
     pieces = pieces + [partner_pieces[step] for step in range(x_count)]
     owners = owners + [owner ^ 1 for owner in owners]

time: 482 us -> 462 us (0.959)
  blocking collectives: 123 us -> 29.5 us
  waiting for transfers between devices: 184 us -> 245 us
  starting transfers between devices: 24.8 us -> 34.6 us
    all_to_all x1 -> x0, blocking collectives: 93.4 us -> none  [per_device(): lax.all_to_all(jnp.broadcast_to(own_part[None], (seq_count,) + own_part.s...]
    all_to_all x0 -> x1, waiting for transfers between devices: none -> 77.9 us  [per_device(): lax.all_to_all(jnp.broadcast_to(own_part[None], (seq_count,) + own_part.s...]
    ppermute x1, waiting for transfers between devices: 26.9 us -> 2.91 us  [per_device(): lax.ppermute(seq_part[0], 'exp', [(i, (i + 2 * step) % group_count) for i...]
    all_gather x1, waiting for transfers between devices: 0.01 us -> 7.56 us  [per_device(): group_normed = lax.all_gather(normed, 'seq', axis=0, tiled=True)]
    all_to_all x0 -> x1, starting transfers between devices: none -> 7.41 us  [per_device(): lax.all_to_all(jnp.broadcast_to(own_part[None], (seq_count,) + own_part.s...]
  transfers between devices with their start and end apart: 10 -> 11, of which waited for: 6 -> 8; matrix products, arithmetic and copies ran while one was open for 23% -> 23% of each run, Pallas kernels for 0% -> 0%
where the time goes in v3:
time: 462 us; the launch traced here: 454 us
  waiting for transfers between devices  245 us (53%)
  matrix products  83.7 us (18%)
  starting transfers between devices  34.6 us (7%)
  blocking collectives  29.5 us (6%)
  local copies, waits for them, and re-layouts  24.5 us (5%)
  other arithmetic  21.2 us (5%)
  between operations  15.1 us (3%)
    all_to_all x1, waiting for transfers between devices, per_device(): lax.all_to_all(jnp.broadcast_to(own_part[None], (seq_count,) + own_part.s...  77.9 us
    all_to_all x2, waiting for transfers between devices, per_device(): lax.all_to_all(outgoing, ('seq', 'exp'), split_axis=0, concat_axis=0, til...  73.4 us
    all_to_all x2, waiting for transfers between devices, per_device(): lax.all_to_all(part_sum.astype(jnp.bfloat16), ('seq', 'exp'), split_axis=...  72 us
    dot_general x4, matrix products, share_part(): jnp.einsum('scd,gfd->scgf', rows, pair, preferred_element_type=jnp.float32)  30.5 us
    all_to_all x1, blocking collectives, per_device(): lax.all_to_all(outgoing_rows, ('seq', 'exp'), split_axis=0, concat_axis=0...  19.4 us
    all_to_all x1, waiting for transfers between devices, per_device(): lax.all_to_all(heads_flat, 'seq', split_axis=0, concat_axis=1, tiled=True)  11.2 us
    unnamed x49, local copies, waits for them, and re-layouts  10.6 us
    all_to_all x1, blocking collectives, per_device(): lax.all_to_all(jnp.broadcast_to(local_stats[None], (device_count,) + loca...  10.1 us
  transfers between devices with their start and end apart: 11, of which 8 were waited for; matrix products, arithmetic and copies ran while one was open for 23% of the time, Pallas kernels for 0%

profile of v3, /device:TPU:0, one launch (start us, length us, event | category | flops | bytes accessed | tf_op | source)
XLA Modules:
  0.0 453.7 jit_solution(16119000986829307182)
XLA Ops:
  8.5 2.0 fusion.58
  10.6 1.6 broadcast_in_dim.68
  12.3 7.4 %all-to-all-start = ((bf16[8,2,32,2048]{3,2,1,0:T(8,128)(2,1)}), bf16[8,2,32,2048]{3,2,1,0:T(8,128)(2,1)S(1)}, u32[]{:S(2)}, u32[]{:S(2)}) async-start(bf16[8,2,32,2048]{3,2,1,0:T(8,128)(2,1)} %broadcast_in_dim.68), calls=%async_computation | async-start | bytes 4194304 | tf_op jit(solution)/shard_map/all_to_all | solution.py:95
  19.9 8.7 %copy.125 = bf16[2048,3,2,128]{0,3,2,1:T(8,128)(2,1)} copy(bf16[2048,3,2,128]{3,2,1,0:T(2,128)(2,1)} %param.15) | data formatting | bytes 6291456 | tf_op args[3]
  31.8 1.8 multiply_cosine_fusion
  33.6 77.9 %all-to-all-done = bf16[8,2,32,2048]{3,2,1,0:T(8,128)(2,1)S(1)} async-done(((bf16[8,2,32,2048]{3,2,1,0:T(8,128)(2,1)}), bf16[8,2,32,2048]{3,2,1,0:T(8,128)(2,1)S(1)}, u32[]{:S(2)}, u32[]{:S(2)}) %all-to-all-start) | async-done | bytes 2097184 | tf_op jit(solution)/shard_map/all_to_all | solution.py:95
  113.1 7.6 %all-gather.2.cloned.1.call-done = bf16[1024,2048]{1,0:T(8,128)(2,1)} async-done(((bf16[128,2048]{1,0:T(8,128)(2,1)}), bf16[1024,2048]{1,0:T(8,128)(2,1)}) %all-gather.2.cloned.1.call-update) | async-done | bytes 4194320 | tf_op jit(solution)/shard_map/all_gather | solution.py:90
  120.7 6.2 %fusion.199 = f32[1024,768]{0,1:S(1)} fusion(bf16[1024,2048]{1,0:T(8,128)(2,1)} %all-gather.2.cloned.1.call-done, bf16[2048,768]{0,1:T(8,128)(2,1)} %bitcast.226), kind=kOutput, calls=%fused_computation.242 | convolution fusion | flops 3221225472 | bytes 10485760
  129.8 1.7 fusion.188
  131.9 3.3 convert.17
  137.8 2.4 fusion.53
  140.2 2.9 fusion.183
  143.1 2.3 fusion.182
  145.4 2.1 fusion.54
  147.6 1.6 fusion.55
  149.3 2.9 collective-permute-done
  152.2 4.0 pad_maximum_fusion
  158.0 8.0 %all-to-all-start.1 = ((bf16[8,128,256]{1,2,0:T(8,128)(2,1)}), bf16[8,128,256]{1,2,0:T(8,128)(2,1)S(1)}, u32[]{:S(2)}, u32[]{:S(2)}) async-start(bf16[8,128,256]{1,2,0:T(8,128)(2,1)} %copy.135), calls=%async_computation.1 | async-start | bytes 1048576 | tf_op jit(solution)/shard_map/all_to_all | solution.py:148
  166.2 1.7 reduce-window.11
  169.4 11.2 %all-to-all-done.1 = bf16[8,128,256]{1,2,0:T(8,128)(2,1)S(1)} async-done(((bf16[8,128,256]{1,2,0:T(8,128)(2,1)}), bf16[8,128,256]{1,2,0:T(8,128)(2,1)S(1)}, u32[]{:S(2)}, u32[]{:S(2)}) %all-to-all-start.1) | async-done | bytes 524320 | tf_op jit(solution)/shard_map/all_to_all | solution.py:148
  181.1 2.1 convolution_bitcast_fusion.3
  183.2 2.1 convolution_bitcast_fusion.2
  185.3 2.4 multiply_reduce_fusion
  188.5 2.4 copy.154
  190.9 3.6 all-to-all-start.4
  195.2 2.3 copy.146
  197.5 45.9 %all-to-all-done.4 = bf16[32,14,2048]{2,1,0:T(8,128)(2,1)} async-done(((bf16[32,14,2048]{2,1,0:T(8,128)(2,1)}), bf16[32,14,2048]{2,1,0:T(8,128)(2,1)}, u32[]{:S(2)}, u32[]{:S(2)}) %all-to-all-start.4) | async-done | bytes 1835040 | tf_op jit(solution)/shard_map/all_to_all | solution.py:206
  243.4 4.3 all-to-all-start.2
  248.2 7.7 %fusion.8 = f32[32,14,2,704]{3,0,2,1:T(8,128)S(1)} fusion(bf16[1,2,704,2048]{3,2,1,0:T(8,128)(2,1)} %param.20, bf16[32,14,2048,1]{2,1,0,3:T(8,128)(2,1)} %bitcast.50), kind=kOutput, calls=%fused_computation.8 | convolution fusion | flops 2583691264 | bytes 10125312 | tf_op jit(solution)/shard_map/scd,gfd->scgf/dot_general | solution.py:192
  255.8 1.6 convolution_convert_fusion.1
  257.5 7.5 %fusion.4 = f32[32,14,2,704]{3,0,1,2:T(8,128)S(1)} fusion(bf16[2,704,2048]{2,1,0:T(8,128)(2,1)} %collective-permute-done.2, bf16[32,14,2048]{2,1,0:T(8,128)(2,1)} %all-to-all-done.4), kind=kOutput, calls=%fused_computation.4 | convolution fusion | flops 2583691264 | bytes 10125312 | tf_op jit(solution)/shard_map/scd,gfd->scgf/dot_general | solution.py:192
  265.0 1.7 add_convert_fusion
  266.7 2.4 copy.159
  269.1 27.5 %all-to-all-done.2 = bf16[32,14,2048]{2,1,0:T(8,128)(2,1)} async-done(((bf16[32,14,2048]{2,1,0:T(8,128)(2,1)}), bf16[32,14,2048]{2,1,0:T(8,128)(2,1)}, u32[]{:S(2)}, u32[]{:S(2)}) %all-to-all-start.2) | async-done | bytes 1835040 | tf_op jit(solution)/shard_map/all_to_all | solution.py:206
  296.6 4.4 all-to-all-start.5
  301.0 7.7 %fusion.10 = f32[32,14,2,704]{3,0,2,1:T(8,128)S(1)} fusion(bf16[1,2,704,2048]{3,2,1,0:T(8,128)(2,1)} %param.20, bf16[32,14,2048,1]{2,1,0,3:T(8,128)(2,1)} %bitcast.38), kind=kOutput, calls=%fused_computation.10 | convolution fusion | flops 2583691264 | bytes 10125312 | tf_op jit(solution)/shard_map/scd,gfd->scgf/dot_general | solution.py:192
  308.7 1.6 convolution_convert_fusion.4
  310.3 7.7 %fusion.6 = f32[32,14,2,704]{3,0,2,1:T(8,128)S(1)} fusion(bf16[2,704,2048]{2,1,0:T(8,128)(2,1)} %collective-permute-done.2, bf16[32,14,2048,1]{2,1,0,3:T(8,128)(2,1)} %bitcast.38), kind=kOutput, calls=%fused_computation.6 | convolution fusion | flops 2583691264 | bytes 10125312 | tf_op jit(solution)/shard_map/scd,gfd->scgf/dot_general | solution.py:192
  318.0 1.7 add_convert_fusion.1
  319.7 2.4 copy.150
  322.0 27.8 %all-to-all-done.5 = bf16[32,14,2048]{2,1,0:T(8,128)(2,1)} async-done(((bf16[32,14,2048]{2,1,0:T(8,128)(2,1)}), bf16[32,14,2048]{2,1,0:T(8,128)(2,1)}, u32[]{:S(2)}, u32[]{:S(2)}) %all-to-all-start.5) | async-done | bytes 1835040 | tf_op jit(solution)/shard_map/all_to_all | solution.py:212
  349.8 4.4 all-to-all-start.3
  355.3 3.6 convolution_bitcast_fusion
  358.8 44.3 %all-to-all-done.3 = bf16[32,14,2048]{2,1,0:T(8,128)(2,1)} async-done(((bf16[32,14,2048]{2,1,0:T(8,128)(2,1)}), bf16[32,14,2048]{2,1,0:T(8,128)(2,1)}, u32[]{:S(2)}, u32[]{:S(2)}) %all-to-all-start.3) | async-done | bytes 1835040 | tf_op jit(solution)/shard_map/all_to_all | solution.py:212
  403.1 3.6 fusion.27
  407.2 19.4 %all_to_all.51 = bf16[32,4,2048]{2,1,0:T(4,128)(2,1)S(1)} all-to-all(bf16[32,4,2048]{2,1,0:T(4,128)(2,1)S(1)} %broadcast_in_dim.86), channel_id=1, replica_groups=mesh['seq'=8,'exp'=4] {'seq','exp'}, dimensions={0} | all-to-all | bytes 1048576 | tf_op jit(solution)/shard_map/all_to_all | solution.py:231
  426.8 8.4 %fusion.198 = (f32[16]{0:T(128)S(1)}, f32[16,3200]{1,0:T(8,128)S(1)}) fusion(bf16[3200,2048]{1,0:T(8,128)(2,1)} %param.23, f32[16,2048]{1,0:T(8,128)S(1)} %reduce_sum.159, f32[2048]{0:T(1024)S(1)} %copy-done.16, f32[16]{0:T(128)S(1)} %add_rsqrt_fusion), kind=kOutput, calls=%fused_computation.241 | convolution fusion | flops 209864688 | bytes 13451392 | tf_op jit(solution)/shard_map/dot_general | solution.py:238
  435.5 10.1 %all_to_all.52 = f32[32,2,16]{2,1,0:T(2,128)S(1)} all-to-all(f32[32,2,16]{2,1,0:T(2,128)S(1)} %broadcast_in_dim.87), channel_id=1, replica_groups=mesh['seq'=8,'exp'=4] {'seq','exp'}, dimensions={0} | all-to-all | bytes 8192 | tf_op jit(solution)/shard_map/all_to_all | solution.py:244
  (131 shorter events, 20.7 us)
Async XLA Ops:
  7.2 3.4 copy-start
  7.2 113.5 %all-gather.2.cloned.1.call-start = ((), (), s32[]{:S(2)}) async-start(), calls=%async_computation.8 | async-start | bytes 4718592 | tf_op jit(solution)/shard_map/all_gather | solution.py:90
  12.3 7.4 %copy-start.21 = (s32[1,4]{1,0:T(1,128)S(1)}, s32[1,4]{1,0:T(1,128)}, u32[]{:S(2)}) copy-start(s32[1,4]{1,0:T(1,128)} %param.13) | copy-start | bytes 52
  12.3 99.3 %all-to-all-start = ((bf16[8,2,32,2048]{3,2,1,0:T(8,128)(2,1)}), bf16[8,2,32,2048]{3,2,1,0:T(8,128)(2,1)S(1)}, u32[]{:S(2)}, u32[]{:S(2)}) async-start(bf16[8,2,32,2048]{3,2,1,0:T(8,128)(2,1)} %broadcast_in_dim.68), calls=%async_computation | async-start | bytes 4194304 | tf_op jit(solution)/shard_map/all_to_all | solution.py:95
  111.6 40.6 %collective-permute-start = (bf16[16,32,2048]{2,1,0:T(8,128)(2,1)S(1)}, bf16[16,32,2048]{2,1,0:T(8,128)(2,1)}, u32[]{:S(2)}, u32[]{:S(2)}) collective-permute-start(bf16[16,32,2048]{2,1,0:T(8,128)(2,1)S(1)} %bitcast.221), channel_id=1, source_target_pairs={{0,2},{1,3},{2,0},{3,1},{4,6},{5,7},{6,4},{7,5},{8,10},{9,11},{10,... | collective-permute-start | bytes 6291464 | tf_op jit(solution)/shard_map/ppermute | solution.py:107
  126.8 1.7 copy-start.2
  126.9 1.7 copy-start.9
  126.9 1.7 copy-start.10
  129.8 1.7 copy-start.6
  129.8 1.7 copy-start.7
  129.8 1.7 copy-start.8
  140.2 2.9 copy-start.11
  145.4 2.2 copy-start.22
  147.6 1.7 copy-start.12
  152.2 4.5 copy-start.14
  156.2 24.8 %collective-permute-start.1 = (bf16[2,16,32,2048]{3,2,1,0:T(8,128)(2,1)}, bf16[2,16,32,2048]{3,2,1,0:T(8,128)(2,1)}, u32[]{:S(2)}, u32[]{:S(2)}) collective-permute-start(bf16[2,16,32,2048]{3,2,1,0:T(8,128)(2,1)} %pad_maximum_fusion), channel_id=1, source_target_pairs={{0,1},{1,0},{2,3},{3,2},{4,5},{5,4},{6,7},{7,6},{8,9},{9,8},{10,11... | collective-permute-start | bytes 12582920 | tf_op jit(solution)/shard_map/ppermute | solution.py:52
  156.2 101.3 %collective-permute-start.2 = (bf16[2,704,2048]{2,1,0:T(8,128)(2,1)}, bf16[2,704,2048]{2,1,0:T(8,128)(2,1)}, u32[]{:S(2)}, u32[]{:S(2)}) collective-permute-start(bf16[2,704,2048]{2,1,0:T(8,128)(2,1)} %bitcast.39), channel_id=1, source_target_pairs={{0,1},{1,0},{2,3},{3,2},{4,5},{5,4},{6,7},{7,6},{8,9},{9,8},{10,11... | collective-permute-start | bytes 17301512 | tf_op jit(solution)/shard_map/ppermute | solution.py:52
  158.0 22.6 %all-to-all-start.1 = ((bf16[8,128,256]{1,2,0:T(8,128)(2,1)}), bf16[8,128,256]{1,2,0:T(8,128)(2,1)S(1)}, u32[]{:S(2)}, u32[]{:S(2)}) async-start(bf16[8,128,256]{1,2,0:T(8,128)(2,1)} %copy.135), calls=%async_computation.1 | async-start | bytes 1048576 | tf_op jit(solution)/shard_map/all_to_all | solution.py:148
  180.6 2.6 copy-start.4
  183.2 2.1 copy-start.3
  185.3 2.4 copy-start.15
  190.9 52.5 %all-to-all-start.4 = ((bf16[32,14,2048]{2,1,0:T(8,128)(2,1)}), bf16[32,14,2048]{2,1,0:T(8,128)(2,1)}, u32[]{:S(2)}, u32[]{:S(2)}) async-start(bf16[32,14,2048]{2,1,0:T(8,128)(2,1)} %copy.154), calls=%async_computation.4 | async-start | bytes 4194304 | tf_op jit(solution)/shard_map/all_to_all | solution.py:206
  243.4 53.2 %all-to-all-start.2 = ((bf16[32,14,2048]{2,1,0:T(8,128)(2,1)}), bf16[32,14,2048]{2,1,0:T(8,128)(2,1)}, u32[]{:S(2)}, u32[]{:S(2)}) async-start(bf16[32,14,2048]{2,1,0:T(8,128)(2,1)} %copy.146), calls=%async_computation.2 | async-start | bytes 4194304 | tf_op jit(solution)/shard_map/all_to_all | solution.py:206
  247.7 17.3 %collective-permute-start.3 = (bf16[704,2048]{1,0:T(8,128)(2,1)}, bf16[704,2048]{1,0:T(8,128)(2,1)S(1)}, u32[]{:S(2)}, u32[]{:S(2)}) collective-permute-start(bf16[704,2048]{1,0:T(8,128)(2,1)} %bitcast.244), channel_id=1, source_target_pairs={{0,1},{1,0},{2,3},{3,2},{4,5},{5,4},{6,7},{7,6},{8,9},{9,8},{10,11... | collective-permute-start | bytes 8650760 | tf_op jit(solution)/shard_map/ppermute | solution.py:52
  248.2 7.7 %copy-start.17 = (bf16[1,704,2048]{2,1,0:T(8,128)(2,1)S(1)}, bf16[1,704,2048]{2,1,0:T(8,128)(2,1)}, u32[]{:S(2)}) copy-start(bf16[1,704,2048]{2,1,0:T(8,128)(2,1)} %param.21) | copy-start | bytes 8650756
  265.0 1.7 copy-start.19
  296.6 53.2 %all-to-all-start.5 = ((bf16[32,14,2048]{2,1,0:T(8,128)(2,1)}), bf16[32,14,2048]{2,1,0:T(8,128)(2,1)}, u32[]{:S(2)}, u32[]{:S(2)}) async-start(bf16[32,14,2048]{2,1,0:T(8,128)(2,1)} %copy.159), calls=%async_computation.5 | async-start | bytes 4194304 | tf_op jit(solution)/shard_map/all_to_all | solution.py:212
  301.0 7.7 %copy-start.18 = (bf16[1,704,2048]{2,1,0:T(8,128)(2,1)S(1)}, bf16[1,704,2048]{2,1,0:T(8,128)(2,1)}, u32[]{:S(2)}) copy-start(bf16[1,704,2048]{2,1,0:T(8,128)(2,1)} %param.21) | copy-start | bytes 8650756
  310.3 7.7 %copy-start.20 = (bf16[704,2048]{1,0:T(8,128)(2,1)S(1)}, bf16[704,2048]{1,0:T(8,128)(2,1)}, u32[]{:S(2)}) copy-start(bf16[704,2048]{1,0:T(8,128)(2,1)} %copy-done.19) | copy-start | bytes 8650756
  322.0 32.2 %copy-start.13 = (bf16[2048,16]{0,1:T(8,128)(2,1)S(1)}, bf16[2048,16]{0,1:T(8,128)(2,1)}, u32[]{:S(2)}) copy-start(bf16[2048,16]{0,1:T(8,128)(2,1)} %param.18) | copy-start | bytes 196612
  349.8 53.3 %all-to-all-start.3 = ((bf16[32,14,2048]{2,1,0:T(8,128)(2,1)}), bf16[32,14,2048]{2,1,0:T(8,128)(2,1)}, u32[]{:S(2)}, u32[]{:S(2)}) async-start(bf16[32,14,2048]{2,1,0:T(8,128)(2,1)} %copy.150), calls=%async_computation.3 | async-start | bytes 4194304 | tf_op jit(solution)/shard_map/all_to_all | solution.py:212
  406.7 20.0 %copy-start.5 = (bf16[128,2048]{1,0:T(8,128)(2,1)}, bf16[128,2048]{1,0:T(8,128)(2,1)S(1)}, u32[]{:S(2)}) copy-start(bf16[128,2048]{1,0:T(8,128)(2,1)S(1)} %fusion.27) | copy-start | bytes 1572868
  407.2 19.7 %copy-start.16 = (f32[2048]{0:T(1024)S(1)}, f32[2048]{0:T(1024)}, u32[]{:S(2)}) copy-start(f32[2048]{0:T(1024)} %param.22) | copy-start | bytes 24580
  426.8 19.7 %copy-start.1 = (bf16[2,128,2048]{2,1,0:T(8,128)(2,1)S(1)}, bf16[2,128,2048]{2,1,0:T(8,128)(2,1)}, u32[]{:S(2)}) copy-start(bf16[2,128,2048]{2,1,0:T(8,128)(2,1)} %param.16) | copy-start | bytes 3145732
Sparse Core Ops, SparseCore 0:
  10.7 109.8 all-gather.1

commit v4 on v3

--- a/solution.py
+++ b/solution.py
@@ -92,6 +92,7 @@
     own_part = lax.dynamic_slice_in_dim(
         w_out, lax.axis_index("exp") * part_size, part_size, axis=1
     )
+    own_part, group_normed = lax.optimization_barrier((own_part, group_normed))
     seq_part = lax.all_to_all(
         jnp.broadcast_to(own_part[None], (seq_count,) + own_part.shape),
         "seq",
@@ -143,9 +144,9 @@
         ).astype(jnp.bfloat16)
 
     blocks = jnp.concatenate([one_block(index) for index in range(block_count)], axis=0)
-    x_pieces, blocks = lax.optimization_barrier((x_pieces, blocks))
     heads_flat = blocks.reshape(group_tokens, head_count * head_size)
     regrouped = lax.all_to_all(heads_flat, "seq", split_axis=0, concat_axis=1, tiled=True)
+    x_pieces, regrouped = lax.optimization_barrier((x_pieces, regrouped))
     pieces, owners = [seq_part[0]] + x_pieces, [exp_index] + x_owners
     partner_pieces = pair_swap(jnp.stack(pieces))
     pieces = pieces + [partner_pieces[step] for step in range(x_count)]

time: 462 us -> 480 us (1.039)
  blocking collectives: 29.5 us -> 47.9 us
  waiting for transfers between devices: 245 us -> 260 us
  starting transfers between devices: 34.6 us -> 24.9 us
    all_gather x1, waiting for transfers between devices: 7.56 us -> 67 us  [per_device(): group_normed = lax.all_gather(normed, 'seq', axis=0, tiled=True)]
    all_to_all x1, waiting for transfers between devices: 77.9 us -> 26.4 us  [per_device(): lax.all_to_all(jnp.broadcast_to(own_part[None], (seq_count,) + own_part.s...]
    all_to_all x0 -> x1, blocking collectives: none -> 18.4 us  [per_device(): lax.all_to_all(heads_flat, 'seq', split_axis=0, concat_axis=1, tiled=True)]
    ppermute x1, waiting for transfers between devices: 2.91 us -> 18 us  [per_device(): lax.ppermute(seq_part[0], 'exp', [(i, (i + 2 * step) % group_count) for i...]
    all_to_all x1 -> x0, waiting for transfers between devices: 11.2 us -> none  [per_device(): lax.all_to_all(heads_flat, 'seq', split_axis=0, concat_axis=1, tiled=True)]
    all_to_all x1 -> x0, starting transfers between devices: 8.01 us -> none  [per_device(): lax.all_to_all(heads_flat, 'seq', split_axis=0, concat_axis=1, tiled=True)]
    unnamed x49 -> x47, local copies, waits for them, and re-layouts: 10.6 us -> 9.08 us
  transfers between devices with their start and end apart: 11 -> 10, of which waited for: 8 -> 8; matrix products, arithmetic and copies ran while one was open for 23% -> 21% of each run, Pallas kernels for 0% -> 0%
where the time goes in v4:
time: 480 us; the launch traced here: 472 us
  waiting for transfers between devices  260 us (54%)
  matrix products  83.6 us (17%)
  blocking collectives  47.9 us (10%)
  starting transfers between devices  24.9 us (5%)
  local copies, waits for them, and re-layouts  22.2 us (5%)
  other arithmetic  18.5 us (4%)
  between operations  15.1 us (3%)
    all_to_all x2, waiting for transfers between devices, per_device(): lax.all_to_all(outgoing, ('seq', 'exp'), split_axis=0, concat_axis=0, til...  73.4 us
    all_to_all x2, waiting for transfers between devices, per_device(): lax.all_to_all(part_sum.astype(jnp.bfloat16), ('seq', 'exp'), split_axis=...  72 us
    all_gather x1, waiting for transfers between devices, per_device(): group_normed = lax.all_gather(normed, 'seq', axis=0, tiled=True)  67 us
    dot_general x4, matrix products, share_part(): jnp.einsum('scd,gfd->scgf', rows, pair, preferred_element_type=jnp.float32)  30.5 us
    all_to_all x1, waiting for transfers between devices, per_device(): lax.all_to_all(jnp.broadcast_to(own_part[None], (seq_count,) + own_part.s...  26.4 us
    all_to_all x1, blocking collectives, per_device(): lax.all_to_all(outgoing_rows, ('seq', 'exp'), split_axis=0, concat_axis=0...  19.4 us
    all_to_all x1, blocking collectives, per_device(): lax.all_to_all(heads_flat, 'seq', split_axis=0, concat_axis=1, tiled=True)  18.4 us
    ppermute x1, waiting for transfers between devices, per_device(): lax.ppermute(seq_part[0], 'exp', [(i, (i + 2 * step) % group_count) for i...  18 us
  transfers between devices with their start and end apart: 10, of which 8 were waited for; matrix products, arithmetic and copies ran while one was open for 21% of the time, Pallas kernels for 0%

profile of v4, /device:TPU:0, one launch (start us, length us, event | category | flops | bytes accessed | tf_op | source)
XLA Modules:
  0.0 471.8 jit_solution(3015130228766579097)
XLA Ops:
  8.5 2.0 fusion.58
  10.7 8.7 %copy.125 = bf16[2048,3,2,128]{0,3,2,1:T(8,128)(2,1)} copy(bf16[2048,3,2,128]{3,2,1,0:T(2,128)(2,1)} %param.15) | data formatting | bytes 6291456 | tf_op args[3]
  19.9 67.0 %all-gather.2.cloned.1.call-done = bf16[1024,2048]{1,0:T(8,128)(2,1)} async-done(((bf16[128,2048]{1,0:T(8,128)(2,1)}), bf16[1024,2048]{1,0:T(8,128)(2,1)}) %all-gather.2.cloned.1.call-update) | async-done | bytes 4194320 | tf_op jit(solution)/shard_map/all_gather | solution.py:90
  86.9 1.6 broadcast_in_dim.68
  88.6 3.7 all-to-all-start
  96.1 6.2 %fusion.199 = f32[1024,768]{0,1:S(1)} fusion(bf16[1024,2048]{1,0:T(8,128)(2,1)} %all-gather.2.cloned.1.call-done, bf16[2048,768]{0,1:T(8,128)(2,1)} %bitcast.227), kind=kOutput, calls=%fused_computation.242 | convolution fusion | flops 3221225472 | bytes 10485760
  106.5 1.6 fusion.188
  108.2 2.5 fusion.53
  111.7 1.9 fusion.183
  113.6 26.4 %all-to-all-done = bf16[8,2,32,2048]{3,2,1,0:T(8,128)(2,1)S(1)} async-done(((bf16[8,2,32,2048]{3,2,1,0:T(8,128)(2,1)}), bf16[8,2,32,2048]{3,2,1,0:T(8,128)(2,1)S(1)}, u32[]{:S(2)}, u32[]{:S(2)}) %all-to-all-start) | async-done | bytes 2097184 | tf_op jit(solution)/shard_map/all_to_all | solution.py:96
  140.0 1.5 collective-permute-start
  141.4 1.5 fusion.52
  143.0 2.3 fusion.182
  145.2 2.1 fusion.54
  147.4 1.6 fusion.55
  149.3 18.4 %all_to_all.54 = bf16[8,128,256]{1,2,0:T(8,128)(2,1)S(1)} all-to-all(bf16[8,128,256]{1,2,0:T(8,128)(2,1)S(1)} %copy.135), channel_id=1, replica_groups=mesh['seq'=8,'exp'=4] {'seq'}, dimensions={0} | all-to-all | bytes 1048576 | tf_op jit(solution)/shard_map/all_to_all | solution.py:148
  167.7 18.0 %collective-permute-done = bf16[16,32,2048]{2,1,0:T(8,128)(2,1)} collective-permute-done((bf16[16,32,2048]{2,1,0:T(8,128)(2,1)S(1)}, bf16[16,32,2048]{2,1,0:T(8,128)(2,1)}, u32[]{:S(2)}, u32[]{:S(2)}) %collective-permute-start) | collective-permute-done | bytes 2097184 | tf_op jit(solution)/shard_map/ppermute | solution.py:108
  185.8 4.0 pad_maximum_fusion
  190.7 1.7 reduce-window.11
  194.4 2.9 collective-permute-done.1
  197.3 2.1 convolution_bitcast_fusion.3
  199.3 2.1 convolution_bitcast_fusion.2
  201.5 2.4 multiply_reduce_fusion
  204.7 2.4 copy.154
  207.1 5.6 %all-to-all-start.4 = ((bf16[32,14,2048]{2,1,0:T(8,128)(2,1)}), bf16[32,14,2048]{2,1,0:T(8,128)(2,1)}, u32[]{:S(2)}, u32[]{:S(2)}) async-start(bf16[32,14,2048]{2,1,0:T(8,128)(2,1)} %copy.154), calls=%async_computation.4 | async-start | bytes 4194304 | tf_op jit(solution)/shard_map/all_to_all | solution.py:207
  213.3 2.3 copy.146
  215.7 45.9 %all-to-all-done.4 = bf16[32,14,2048]{2,1,0:T(8,128)(2,1)} async-done(((bf16[32,14,2048]{2,1,0:T(8,128)(2,1)}), bf16[32,14,2048]{2,1,0:T(8,128)(2,1)}, u32[]{:S(2)}, u32[]{:S(2)}) %all-to-all-start.4) | async-done | bytes 1835040 | tf_op jit(solution)/shard_map/all_to_all | solution.py:207
  261.6 4.3 all-to-all-start.2
  266.3 7.7 %fusion.8 = f32[32,14,2,704]{3,0,2,1:T(8,128)S(1)} fusion(bf16[1,2,704,2048]{3,2,1,0:T(8,128)(2,1)} %param.20, bf16[32,14,2048,1]{2,1,0,3:T(8,128)(2,1)} %bitcast.50), kind=kOutput, calls=%fused_computation.8 | convolution fusion | flops 2583691264 | bytes 10125312 | tf_op jit(solution)/shard_map/scd,gfd->scgf/dot_general | solution.py:193
  274.0 1.6 convolution_convert_fusion.1
  275.7 7.5 %fusion.4 = f32[32,14,2,704]{3,0,1,2:T(8,128)S(1)} fusion(bf16[2,704,2048]{2,1,0:T(8,128)(2,1)} %collective-permute-done.2, bf16[32,14,2048]{2,1,0:T(8,128)(2,1)} %all-to-all-done.4), kind=kOutput, calls=%fused_computation.4 | convolution fusion | flops 2583691264 | bytes 10125312 | tf_op jit(solution)/shard_map/scd,gfd->scgf/dot_general | solution.py:193
  283.2 1.7 add_convert_fusion
  284.9 2.4 copy.159
  287.3 27.5 %all-to-all-done.2 = bf16[32,14,2048]{2,1,0:T(8,128)(2,1)} async-done(((bf16[32,14,2048]{2,1,0:T(8,128)(2,1)}), bf16[32,14,2048]{2,1,0:T(8,128)(2,1)}, u32[]{:S(2)}, u32[]{:S(2)}) %all-to-all-start.2) | async-done | bytes 1835040 | tf_op jit(solution)/shard_map/all_to_all | solution.py:207
  314.8 4.4 all-to-all-start.5
  319.1 7.7 %fusion.10 = f32[32,14,2,704]{3,0,2,1:T(8,128)S(1)} fusion(bf16[1,2,704,2048]{3,2,1,0:T(8,128)(2,1)} %param.20, bf16[32,14,2048,1]{2,1,0,3:T(8,128)(2,1)} %bitcast.38), kind=kOutput, calls=%fused_computation.10 | convolution fusion | flops 2583691264 | bytes 10125312 | tf_op jit(solution)/shard_map/scd,gfd->scgf/dot_general | solution.py:193
  326.8 1.6 convolution_convert_fusion.4
  328.5 7.7 %fusion.6 = f32[32,14,2,704]{3,0,2,1:T(8,128)S(1)} fusion(bf16[2,704,2048]{2,1,0:T(8,128)(2,1)} %collective-permute-done.2, bf16[32,14,2048,1]{2,1,0,3:T(8,128)(2,1)} %bitcast.38), kind=kOutput, calls=%fused_computation.6 | convolution fusion | flops 2583691264 | bytes 10125312 | tf_op jit(solution)/shard_map/scd,gfd->scgf/dot_general | solution.py:193
  336.2 1.7 add_convert_fusion.1
  337.9 2.4 copy.150
  340.2 27.8 %all-to-all-done.5 = bf16[32,14,2048]{2,1,0:T(8,128)(2,1)} async-done(((bf16[32,14,2048]{2,1,0:T(8,128)(2,1)}), bf16[32,14,2048]{2,1,0:T(8,128)(2,1)}, u32[]{:S(2)}, u32[]{:S(2)}) %all-to-all-start.5) | async-done | bytes 1835040 | tf_op jit(solution)/shard_map/all_to_all | solution.py:213
  368.0 4.4 all-to-all-start.3
  373.4 3.6 convolution_bitcast_fusion
  377.0 44.3 %all-to-all-done.3 = bf16[32,14,2048]{2,1,0:T(8,128)(2,1)} async-done(((bf16[32,14,2048]{2,1,0:T(8,128)(2,1)}), bf16[32,14,2048]{2,1,0:T(8,128)(2,1)}, u32[]{:S(2)}, u32[]{:S(2)}) %all-to-all-start.3) | async-done | bytes 1835040 | tf_op jit(solution)/shard_map/all_to_all | solution.py:213
  421.3 3.6 fusion.27
  425.3 19.4 %all_to_all.55 = bf16[32,4,2048]{2,1,0:T(4,128)(2,1)S(1)} all-to-all(bf16[32,4,2048]{2,1,0:T(4,128)(2,1)S(1)} %broadcast_in_dim.86), channel_id=1, replica_groups=mesh['seq'=8,'exp'=4] {'seq','exp'}, dimensions={0} | all-to-all | bytes 1048576 | tf_op jit(solution)/shard_map/all_to_all | solution.py:232
  445.0 8.4 %fusion.198 = (f32[16]{0:T(128)S(1)}, f32[16,3200]{1,0:T(8,128)S(1)}) fusion(bf16[3200,2048]{1,0:T(8,128)(2,1)} %param.23, f32[16,2048]{1,0:T(8,128)S(1)} %reduce_sum.159, f32[2048]{0:T(1024)S(1)} %copy-done.15, f32[16]{0:T(128)S(1)} %add_rsqrt_fusion), kind=kOutput, calls=%fused_computation.241 | convolution fusion | flops 209864688 | bytes 13451392 | tf_op jit(solution)/shard_map/dot_general | solution.py:239
  453.7 10.1 %all_to_all.56 = f32[32,2,16]{2,1,0:T(2,128)S(1)} all-to-all(f32[32,2,16]{2,1,0:T(2,128)S(1)} %broadcast_in_dim.87), channel_id=1, replica_groups=mesh['seq'=8,'exp'=4] {'seq','exp'}, dimensions={0} | all-to-all | bytes 8192 | tf_op jit(solution)/shard_map/all_to_all | solution.py:245
  (129 shorter events, 18.7 us)
Async XLA Ops:
  7.2 12.7 %copy-start = (bf16[2,128,2048]{2,1,0:T(8,128)(2,1)S(1)}, bf16[2,128,2048]{2,1,0:T(8,128)(2,1)}, u32[]{:S(2)}) copy-start(bf16[2,128,2048]{2,1,0:T(8,128)(2,1)} %param.16) | copy-start | bytes 3145732
  7.2 79.7 %all-gather.2.cloned.1.call-start = ((), (), s32[]{:S(2)}) async-start(), calls=%async_computation.8 | async-start | bytes 4718592 | tf_op jit(solution)/shard_map/all_gather | solution.py:90
  10.6 8.8 %copy-start.12 = (s32[1024]{0:T(1024)}, s32[1024]{0:T(1024)S(1)}, u32[]{:S(2)}) copy-start(s32[1024]{0:T(1024)S(1)} %iota.53) | copy-start | bytes 12292
  10.6 8.7 %copy-start.20 = (s32[1,4]{1,0:T(1,128)S(1)}, s32[1,4]{1,0:T(1,128)}, u32[]{:S(2)}) copy-start(s32[1,4]{1,0:T(1,128)} %param.13) | copy-start | bytes 52
  88.6 3.8 slice-start
  88.6 51.4 %all-to-all-start = ((bf16[8,2,32,2048]{3,2,1,0:T(8,128)(2,1)}), bf16[8,2,32,2048]{3,2,1,0:T(8,128)(2,1)S(1)}, u32[]{:S(2)}, u32[]{:S(2)}) async-start(bf16[8,2,32,2048]{3,2,1,0:T(8,128)(2,1)} %broadcast_in_dim.68), calls=%async_computation | async-start | bytes 4194304 | tf_op jit(solution)/shard_map/all_to_all | solution.py:96
  105.1 3.0 copy-start.5
  105.1 3.0 copy-start.6
  105.1 3.0 copy-start.7
  108.2 3.5 copy-start.9
  113.6 29.4 %copy-start.8 = (pred[256,1024]{1,0:T(8,128)(4,1)S(1)}, pred[256,1024]{1,0:T(8,128)(4,1)}, u32[]{:S(2)}) copy-start(pred[256,1024]{1,0:T(8,128)(4,1)} %fusion.61) | copy-start | bytes 786436
  140.0 45.8 %collective-permute-start = (bf16[16,32,2048]{2,1,0:T(8,128)(2,1)S(1)}, bf16[16,32,2048]{2,1,0:T(8,128)(2,1)}, u32[]{:S(2)}, u32[]{:S(2)}) collective-permute-start(bf16[16,32,2048]{2,1,0:T(8,128)(2,1)S(1)} %bitcast.222), channel_id=1, source_target_pairs={{0,2},{1,3},{2,0},{3,1},{4,6},{5,7},{6,4},{7,5},{8,10},{9,11},{10,... | collective-permute-start | bytes 6291464 | tf_op jit(solution)/shard_map/ppermute | solution.py:108
  145.2 2.2 copy-start.21
  147.4 1.7 copy-start.10
  167.7 31.6 %copy-start.3 = (bf16[8,128,256]{1,2,0:T(8,128)(2,1)}, bf16[8,128,256]{1,2,0:T(8,128)(2,1)S(1)}, u32[]{:S(2)}) copy-start(bf16[8,128,256]{1,2,0:T(8,128)(2,1)S(1)} %all_to_all.54) | copy-start | bytes 1572868
  185.8 4.5 copy-start.13
  189.8 7.5 %collective-permute-start.1 = (bf16[2,16,32,2048]{3,2,1,0:T(8,128)(2,1)}, bf16[2,16,32,2048]{3,2,1,0:T(8,128)(2,1)}, u32[]{:S(2)}, u32[]{:S(2)}) collective-permute-start(bf16[2,16,32,2048]{3,2,1,0:T(8,128)(2,1)} %pad_maximum_fusion), channel_id=1, source_target_pairs={{0,1},{1,0},{2,3},{3,2},{4,5},{5,4},{6,7},{7,6},{8,9},{9,8},{10,11... | collective-permute-start | bytes 12582920 | tf_op jit(solution)/shard_map/ppermute | solution.py:52
  189.8 85.9 %collective-permute-start.2 = (bf16[2,704,2048]{2,1,0:T(8,128)(2,1)}, bf16[2,704,2048]{2,1,0:T(8,128)(2,1)}, u32[]{:S(2)}, u32[]{:S(2)}) collective-permute-start(bf16[2,704,2048]{2,1,0:T(8,128)(2,1)} %bitcast.39), channel_id=1, source_target_pairs={{0,1},{1,0},{2,3},{3,2},{4,5},{5,4},{6,7},{7,6},{8,9},{9,8},{10,11... | collective-permute-start | bytes 17301512 | tf_op jit(solution)/shard_map/ppermute | solution.py:52
  199.3 2.1 copy-start.2
  201.5 2.4 copy-start.14
  207.1 54.5 %all-to-all-start.4 = ((bf16[32,14,2048]{2,1,0:T(8,128)(2,1)}), bf16[32,14,2048]{2,1,0:T(8,128)(2,1)}, u32[]{:S(2)}, u32[]{:S(2)}) async-start(bf16[32,14,2048]{2,1,0:T(8,128)(2,1)} %copy.154), calls=%async_computation.4 | async-start | bytes 4194304 | tf_op jit(solution)/shard_map/all_to_all | solution.py:207
  261.6 53.2 %all-to-all-start.2 = ((bf16[32,14,2048]{2,1,0:T(8,128)(2,1)}), bf16[32,14,2048]{2,1,0:T(8,128)(2,1)}, u32[]{:S(2)}, u32[]{:S(2)}) async-start(bf16[32,14,2048]{2,1,0:T(8,128)(2,1)} %copy.146), calls=%async_computation.2 | async-start | bytes 4194304 | tf_op jit(solution)/shard_map/all_to_all | solution.py:207
  265.9 17.3 %collective-permute-start.3 = (bf16[704,2048]{1,0:T(8,128)(2,1)}, bf16[704,2048]{1,0:T(8,128)(2,1)S(1)}, u32[]{:S(2)}, u32[]{:S(2)}) collective-permute-start(bf16[704,2048]{1,0:T(8,128)(2,1)} %bitcast.245), channel_id=1, source_target_pairs={{0,1},{1,0},{2,3},{3,2},{4,5},{5,4},{6,7},{7,6},{8,9},{9,8},{10,11... | collective-permute-start | bytes 8650760 | tf_op jit(solution)/shard_map/ppermute | solution.py:52
  266.3 7.7 %copy-start.16 = (bf16[1,704,2048]{2,1,0:T(8,128)(2,1)S(1)}, bf16[1,704,2048]{2,1,0:T(8,128)(2,1)}, u32[]{:S(2)}) copy-start(bf16[1,704,2048]{2,1,0:T(8,128)(2,1)} %param.21) | copy-start | bytes 8650756
  283.2 1.7 copy-start.18
  314.8 53.2 %all-to-all-start.5 = ((bf16[32,14,2048]{2,1,0:T(8,128)(2,1)}), bf16[32,14,2048]{2,1,0:T(8,128)(2,1)}, u32[]{:S(2)}, u32[]{:S(2)}) async-start(bf16[32,14,2048]{2,1,0:T(8,128)(2,1)} %copy.159), calls=%async_computation.5 | async-start | bytes 4194304 | tf_op jit(solution)/shard_map/all_to_all | solution.py:213
  319.1 7.7 %copy-start.17 = (bf16[1,704,2048]{2,1,0:T(8,128)(2,1)S(1)}, bf16[1,704,2048]{2,1,0:T(8,128)(2,1)}, u32[]{:S(2)}) copy-start(bf16[1,704,2048]{2,1,0:T(8,128)(2,1)} %param.21) | copy-start | bytes 8650756
  328.5 7.7 %copy-start.19 = (bf16[704,2048]{1,0:T(8,128)(2,1)S(1)}, bf16[704,2048]{1,0:T(8,128)(2,1)}, u32[]{:S(2)}) copy-start(bf16[704,2048]{1,0:T(8,128)(2,1)} %copy-done.18) | copy-start | bytes 8650756
  340.2 32.2 %copy-start.11 = (bf16[2048,16]{0,1:T(8,128)(2,1)S(1)}, bf16[2048,16]{0,1:T(8,128)(2,1)}, u32[]{:S(2)}) copy-start(bf16[2048,16]{0,1:T(8,128)(2,1)} %param.18) | copy-start | bytes 196612
  368.0 53.3 %all-to-all-start.3 = ((bf16[32,14,2048]{2,1,0:T(8,128)(2,1)}), bf16[32,14,2048]{2,1,0:T(8,128)(2,1)}, u32[]{:S(2)}, u32[]{:S(2)}) async-start(bf16[32,14,2048]{2,1,0:T(8,128)(2,1)} %copy.150), calls=%async_computation.3 | async-start | bytes 4194304 | tf_op jit(solution)/shard_map/all_to_all | solution.py:213
  424.8 20.0 %copy-start.4 = (bf16[128,2048]{1,0:T(8,128)(2,1)}, bf16[128,2048]{1,0:T(8,128)(2,1)S(1)}, u32[]{:S(2)}) copy-start(bf16[128,2048]{1,0:T(8,128)(2,1)S(1)} %fusion.27) | copy-start | bytes 1572868
  425.3 19.7 %copy-start.15 = (f32[2048]{0:T(1024)S(1)}, f32[2048]{0:T(1024)}, u32[]{:S(2)}) copy-start(f32[2048]{0:T(1024)} %param.22) | copy-start | bytes 24580
  445.0 19.7 %copy-start.1 = (bf16[2,128,2048]{2,1,0:T(8,128)(2,1)S(1)}, bf16[2,128,2048]{2,1,0:T(8,128)(2,1)}, u32[]{:S(2)}) copy-start(bf16[2,128,2048]{2,1,0:T(8,128)(2,1)} %param.16) | copy-start | bytes 3145732
Sparse Core Ops, SparseCore 0:
  10.7 76.1 all-gather.1

commit v5 on v3

--- a/solution.py
+++ b/solution.py
@@ -225,15 +225,23 @@
     here_places = lax.axis_index("seq") * tok_rows + jnp.arange(tok_rows, dtype=jnp.int32)
     select_table = (last_places[:, None] == here_places[None, :]).astype(jnp.bfloat16)
     picked = jnp.dot(select_table, layer_rows, preferred_element_type=jnp.float32)
-    outgoing_rows = jnp.broadcast_to(
-        picked.astype(jnp.bfloat16)[None], (device_count, prompt_count, model_width)
-    )
-    arrived_rows = lax.all_to_all(
-        outgoing_rows, ("seq", "exp"), split_axis=0, concat_axis=0, tiled=True
-    ).astype(jnp.float32)
-    last_rows = jnp.sum(
-        arrived_rows.reshape(seq_count, group_count * prompt_count, model_width), axis=0
-    )
+    group_rows = lax.all_to_all(
+        jnp.broadcast_to(
+            picked.astype(jnp.bfloat16)[None], (seq_count, prompt_count, model_width)
+        ),
+        "seq",
+        split_axis=0,
+        concat_axis=0,
+        tiled=True,
+    )
+    group_rows = jnp.sum(group_rows.astype(jnp.float32), axis=0).astype(jnp.bfloat16)
+    last_rows = lax.all_to_all(
+        jnp.broadcast_to(group_rows[None], (group_count, prompt_count, model_width)),
+        "exp",
+        split_axis=0,
+        concat_axis=0,
+        tiled=True,
+    ).reshape(group_count * prompt_count, model_width).astype(jnp.float32)
     final = rms_scale(last_rows, final_gain).astype(jnp.bfloat16)
     vocab_scores = lax.dot_general(
         final, lm_head, (((1,), (1,)), ((), ())), preferred_element_type=jnp.float32

time: 462 us -> 459 us (level)
    all_to_all x1 -> x2, blocking collectives: 19.4 us -> 17.8 us  [the longest x1 10.6 us: per_device(): lax.all_to_all(jnp.broadcast_to(picked.astype(jnp.bfloat16)[None], (seq_c...]
  transfers between devices with their start and end apart: 11 -> 11, of which waited for: 8 -> 8; matrix products, arithmetic and copies ran while one was open for 23% -> 24% of each run, Pallas kernels for 0% -> 0%
where the time goes in v5:
time: 459 us; the launch traced here: 451 us
  waiting for transfers between devices  245 us (53%)
  matrix products  83.7 us (18%)
  starting transfers between devices  34.6 us (8%)
  blocking collectives  26.8 us (6%)
  local copies, waits for them, and re-layouts  24.3 us (5%)
  other arithmetic  21.2 us (5%)
  between operations  15.1 us (3%)
    all_to_all x1, waiting for transfers between devices, per_device(): lax.all_to_all(jnp.broadcast_to(own_part[None], (seq_count,) + own_part.s...  77.9 us
    all_to_all x2, waiting for transfers between devices, per_device(): lax.all_to_all(outgoing, ('seq', 'exp'), split_axis=0, concat_axis=0, til...  73.4 us
    all_to_all x2, waiting for transfers between devices, per_device(): lax.all_to_all(part_sum.astype(jnp.bfloat16), ('seq', 'exp'), split_axis=...  72 us
    dot_general x4, matrix products, share_part(): jnp.einsum('scd,gfd->scgf', rows, pair, preferred_element_type=jnp.float32)  30.5 us
    all_to_all x1, waiting for transfers between devices, per_device(): lax.all_to_all(heads_flat, 'seq', split_axis=0, concat_axis=1, tiled=True)  11.2 us
    all_to_all x1, blocking collectives, per_device(): lax.all_to_all(jnp.broadcast_to(picked.astype(jnp.bfloat16)[None], (seq_c...  10.6 us
    unnamed x49, local copies, waits for them, and re-layouts  10.6 us
  transfers between devices with their start and end apart: 11, of which 8 were waited for; matrix products, arithmetic and copies ran while one was open for 24% of the time, Pallas kernels for 0%

profile of v5, /device:TPU:0, one launch (start us, length us, event | category | flops | bytes accessed | tf_op | source)
XLA Modules:
  0.0 450.8 jit_solution(2705848047213241272)
XLA Ops:
  8.5 2.0 fusion.58
  10.6 1.6 broadcast_in_dim.70
  12.3 7.4 %all-to-all-start = ((bf16[8,2,32,2048]{3,2,1,0:T(8,128)(2,1)}), bf16[8,2,32,2048]{3,2,1,0:T(8,128)(2,1)S(1)}, u32[]{:S(2)}, u32[]{:S(2)}) async-start(bf16[8,2,32,2048]{3,2,1,0:T(8,128)(2,1)} %broadcast_in_dim.70), calls=%async_computation | async-start | bytes 4194304 | tf_op jit(solution)/shard_map/all_to_all | solution.py:95
  19.9 8.7 %copy.125 = bf16[2048,3,2,128]{0,3,2,1:T(8,128)(2,1)} copy(bf16[2048,3,2,128]{3,2,1,0:T(2,128)(2,1)} %param.15) | data formatting | bytes 6291456 | tf_op args[3]
  31.8 1.8 multiply_cosine_fusion
  33.6 77.9 %all-to-all-done = bf16[8,2,32,2048]{3,2,1,0:T(8,128)(2,1)S(1)} async-done(((bf16[8,2,32,2048]{3,2,1,0:T(8,128)(2,1)}), bf16[8,2,32,2048]{3,2,1,0:T(8,128)(2,1)S(1)}, u32[]{:S(2)}, u32[]{:S(2)}) %all-to-all-start) | async-done | bytes 2097184 | tf_op jit(solution)/shard_map/all_to_all | solution.py:95
  113.1 7.6 %all-gather.2.cloned.1.call-done = bf16[1024,2048]{1,0:T(8,128)(2,1)} async-done(((bf16[128,2048]{1,0:T(8,128)(2,1)}), bf16[1024,2048]{1,0:T(8,128)(2,1)}) %all-gather.2.cloned.1.call-update) | async-done | bytes 4194320 | tf_op jit(solution)/shard_map/all_gather | solution.py:90
  120.7 6.2 %fusion.199 = f32[1024,768]{0,1:S(1)} fusion(bf16[1024,2048]{1,0:T(8,128)(2,1)} %all-gather.2.cloned.1.call-done, bf16[2048,768]{0,1:T(8,128)(2,1)} %bitcast.226), kind=kOutput, calls=%fused_computation.242 | convolution fusion | flops 3221225472 | bytes 10485760
  129.8 1.7 fusion.188
  131.9 3.3 convert.18
  137.8 2.4 fusion.53
  140.2 2.9 fusion.183
  143.1 2.3 fusion.182
  145.4 2.1 fusion.54
  147.6 1.6 fusion.55
  149.3 2.9 collective-permute-done
  152.2 4.0 pad_maximum_fusion
  158.0 8.0 %all-to-all-start.1 = ((bf16[8,128,256]{1,2,0:T(8,128)(2,1)}), bf16[8,128,256]{1,2,0:T(8,128)(2,1)S(1)}, u32[]{:S(2)}, u32[]{:S(2)}) async-start(bf16[8,128,256]{1,2,0:T(8,128)(2,1)} %copy.135), calls=%async_computation.1 | async-start | bytes 1048576 | tf_op jit(solution)/shard_map/all_to_all | solution.py:148
  166.2 1.7 reduce-window.11
  169.4 11.2 %all-to-all-done.1 = bf16[8,128,256]{1,2,0:T(8,128)(2,1)S(1)} async-done(((bf16[8,128,256]{1,2,0:T(8,128)(2,1)}), bf16[8,128,256]{1,2,0:T(8,128)(2,1)S(1)}, u32[]{:S(2)}, u32[]{:S(2)}) %all-to-all-start.1) | async-done | bytes 524320 | tf_op jit(solution)/shard_map/all_to_all | solution.py:148
  181.1 2.1 convolution_bitcast_fusion.3
  183.2 2.1 convolution_bitcast_fusion.2
  185.3 2.4 multiply_reduce_fusion
  188.5 2.4 copy.154
  190.9 3.6 all-to-all-start.4
  195.2 2.3 copy.146
  197.5 45.9 %all-to-all-done.4 = bf16[32,14,2048]{2,1,0:T(8,128)(2,1)} async-done(((bf16[32,14,2048]{2,1,0:T(8,128)(2,1)}), bf16[32,14,2048]{2,1,0:T(8,128)(2,1)}, u32[]{:S(2)}, u32[]{:S(2)}) %all-to-all-start.4) | async-done | bytes 1835040 | tf_op jit(solution)/shard_map/all_to_all | solution.py:206
  243.4 4.3 all-to-all-start.2
  248.2 7.7 %fusion.8 = f32[32,14,2,704]{3,0,2,1:T(8,128)S(1)} fusion(bf16[1,2,704,2048]{3,2,1,0:T(8,128)(2,1)} %param.20, bf16[32,14,2048,1]{2,1,0,3:T(8,128)(2,1)} %bitcast.50), kind=kOutput, calls=%fused_computation.8 | convolution fusion | flops 2583691264 | bytes 10125312 | tf_op jit(solution)/shard_map/scd,gfd->scgf/dot_general | solution.py:192
  257.5 7.5 %fusion.4 = f32[32,14,2,704]{3,0,1,2:T(8,128)S(1)} fusion(bf16[2,704,2048]{2,1,0:T(8,128)(2,1)} %collective-permute-done.2, bf16[32,14,2048]{2,1,0:T(8,128)(2,1)} %all-to-all-done.4), kind=kOutput, calls=%fused_computation.4 | convolution fusion | flops 2583691264 | bytes 10125312 | tf_op jit(solution)/shard_map/scd,gfd->scgf/dot_general | solution.py:192
  265.0 1.7 add_convert_fusion
  266.7 2.4 copy.159
  269.1 27.5 %all-to-all-done.2 = bf16[32,14,2048]{2,1,0:T(8,128)(2,1)} async-done(((bf16[32,14,2048]{2,1,0:T(8,128)(2,1)}), bf16[32,14,2048]{2,1,0:T(8,128)(2,1)}, u32[]{:S(2)}, u32[]{:S(2)}) %all-to-all-start.2) | async-done | bytes 1835040 | tf_op jit(solution)/shard_map/all_to_all | solution.py:206
  296.6 4.4 all-to-all-start.5
  301.0 7.7 %fusion.10 = f32[32,14,2,704]{3,0,2,1:T(8,128)S(1)} fusion(bf16[1,2,704,2048]{3,2,1,0:T(8,128)(2,1)} %param.20, bf16[32,14,2048,1]{2,1,0,3:T(8,128)(2,1)} %bitcast.38), kind=kOutput, calls=%fused_computation.10 | convolution fusion | flops 2583691264 | bytes 10125312 | tf_op jit(solution)/shard_map/scd,gfd->scgf/dot_general | solution.py:192
  308.7 1.6 convolution_convert_fusion.4
  310.3 7.7 %fusion.6 = f32[32,14,2,704]{3,0,2,1:T(8,128)S(1)} fusion(bf16[2,704,2048]{2,1,0:T(8,128)(2,1)} %collective-permute-done.2, bf16[32,14,2048,1]{2,1,0,3:T(8,128)(2,1)} %bitcast.38), kind=kOutput, calls=%fused_computation.6 | convolution fusion | flops 2583691264 | bytes 10125312 | tf_op jit(solution)/shard_map/scd,gfd->scgf/dot_general | solution.py:192
  318.0 1.7 add_convert_fusion.1
  319.7 2.4 copy.150
  322.0 27.8 %all-to-all-done.5 = bf16[32,14,2048]{2,1,0:T(8,128)(2,1)} async-done(((bf16[32,14,2048]{2,1,0:T(8,128)(2,1)}), bf16[32,14,2048]{2,1,0:T(8,128)(2,1)}, u32[]{:S(2)}, u32[]{:S(2)}) %all-to-all-start.5) | async-done | bytes 1835040 | tf_op jit(solution)/shard_map/all_to_all | solution.py:212
  349.8 4.4 all-to-all-start.3
  355.3 3.6 convolution_bitcast_fusion
  358.8 44.3 %all-to-all-done.3 = bf16[32,14,2048]{2,1,0:T(8,128)(2,1)} async-done(((bf16[32,14,2048]{2,1,0:T(8,128)(2,1)}), bf16[32,14,2048]{2,1,0:T(8,128)(2,1)}, u32[]{:S(2)}, u32[]{:S(2)}) %all-to-all-start.3) | async-done | bytes 1835040 | tf_op jit(solution)/shard_map/all_to_all | solution.py:212
  403.1 3.6 fusion.27
  407.0 10.6 %all_to_all.56 = bf16[8,4,2048]{2,1,0:T(4,128)(2,1)S(1)} all-to-all(bf16[8,4,2048]{2,1,0:T(4,128)(2,1)S(1)} %broadcast_in_dim.92), channel_id=1, replica_groups=mesh['seq'=8,'exp'=4] {'seq'}, dimensions={0} | all-to-all | bytes 262144 | tf_op jit(solution)/shard_map/all_to_all | solution.py:228
  417.7 7.2 %all_to_all.57 = bf16[4,4,2048]{2,1,0:T(4,128)(2,1)S(1)} all-to-all(bf16[4,4,2048]{2,1,0:T(4,128)(2,1)S(1)} %broadcast_in_dim.93), channel_id=1, replica_groups=mesh['seq'=8,'exp'=4] {'exp'}, dimensions={0} | all-to-all | bytes 131072 | tf_op jit(solution)/shard_map/all_to_all | solution.py:238
  425.2 8.4 %fusion.198 = (f32[16]{0:T(128)S(1)}, f32[16,3200]{1,0:T(8,128)S(1)}) fusion(bf16[3200,2048]{1,0:T(8,128)(2,1)} %param.23, f32[16,2048]{1,0:T(8,128)S(1)} %reshape.444, f32[2048]{0:T(1024)S(1)} %copy-done.16, f32[16]{0:T(128)S(1)} %rsqrt.30), kind=kOutput, calls=%fused_computation.241 | convolution fusion | flops 209864688 | bytes 13451392 | tf_op jit(solution)/shard_map/dot_general | solution.py:246
  433.9 8.9 %all_to_all.58 = f32[32,2,16]{2,1,0:T(2,128)S(1)} all-to-all(f32[32,2,16]{2,1,0:T(2,128)S(1)} %broadcast_in_dim.94), channel_id=1, replica_groups=mesh['seq'=8,'exp'=4] {'seq','exp'}, dimensions={0} | all-to-all | bytes 8192 | tf_op jit(solution)/shard_map/all_to_all | solution.py:252
  (134 shorter events, 22.1 us)
Async XLA Ops:
  7.2 3.4 copy-start
  7.2 113.5 %all-gather.2.cloned.1.call-start = ((), (), s32[]{:S(2)}) async-start(), calls=%async_computation.9 | async-start | bytes 4718592 | tf_op jit(solution)/shard_map/all_gather | solution.py:90
  12.3 7.4 %copy-start.21 = (s32[1,4]{1,0:T(1,128)S(1)}, s32[1,4]{1,0:T(1,128)}, u32[]{:S(2)}) copy-start(s32[1,4]{1,0:T(1,128)} %param.13) | copy-start | bytes 52
  12.3 99.3 %all-to-all-start = ((bf16[8,2,32,2048]{3,2,1,0:T(8,128)(2,1)}), bf16[8,2,32,2048]{3,2,1,0:T(8,128)(2,1)S(1)}, u32[]{:S(2)}, u32[]{:S(2)}) async-start(bf16[8,2,32,2048]{3,2,1,0:T(8,128)(2,1)} %broadcast_in_dim.70), calls=%async_computation | async-start | bytes 4194304 | tf_op jit(solution)/shard_map/all_to_all | solution.py:95
  111.6 40.6 %collective-permute-start = (bf16[16,32,2048]{2,1,0:T(8,128)(2,1)S(1)}, bf16[16,32,2048]{2,1,0:T(8,128)(2,1)}, u32[]{:S(2)}, u32[]{:S(2)}) collective-permute-start(bf16[16,32,2048]{2,1,0:T(8,128)(2,1)S(1)} %bitcast.221), channel_id=1, source_target_pairs={{0,2},{1,3},{2,0},{3,1},{4,6},{5,7},{6,4},{7,5},{8,10},{9,11},{10,... | collective-permute-start | bytes 6291464 | tf_op jit(solution)/shard_map/ppermute | solution.py:107
  126.8 1.7 copy-start.2
  126.9 1.7 copy-start.9
  126.9 1.7 copy-start.10
  129.8 1.7 copy-start.6
  129.8 1.7 copy-start.7
  129.8 1.7 copy-start.8
  140.2 2.9 copy-start.11
  145.4 2.2 copy-start.22
  147.6 1.7 copy-start.12
  152.2 4.5 %copy-start.14 = (s32[1,128,6]{1,0,2:T(1,128)S(1)}, s32[1,128,6]{1,0,2:T(1,128)}, u32[]{:S(2)}) copy-start(s32[1,128,6]{1,0,2:T(1,128)} %param.19) | copy-start | bytes 9220
  156.2 24.8 %collective-permute-start.1 = (bf16[2,16,32,2048]{3,2,1,0:T(8,128)(2,1)}, bf16[2,16,32,2048]{3,2,1,0:T(8,128)(2,1)}, u32[]{:S(2)}, u32[]{:S(2)}) collective-permute-start(bf16[2,16,32,2048]{3,2,1,0:T(8,128)(2,1)} %pad_maximum_fusion), channel_id=1, source_target_pairs={{0,1},{1,0},{2,3},{3,2},{4,5},{5,4},{6,7},{7,6},{8,9},{9,8},{10,11... | collective-permute-start | bytes 12582920 | tf_op jit(solution)/shard_map/ppermute | solution.py:52
  156.2 101.3 %collective-permute-start.2 = (bf16[2,704,2048]{2,1,0:T(8,128)(2,1)}, bf16[2,704,2048]{2,1,0:T(8,128)(2,1)}, u32[]{:S(2)}, u32[]{:S(2)}) collective-permute-start(bf16[2,704,2048]{2,1,0:T(8,128)(2,1)} %bitcast.39), channel_id=1, source_target_pairs={{0,1},{1,0},{2,3},{3,2},{4,5},{5,4},{6,7},{7,6},{8,9},{9,8},{10,11... | collective-permute-start | bytes 17301512 | tf_op jit(solution)/shard_map/ppermute | solution.py:52
  158.0 22.6 %all-to-all-start.1 = ((bf16[8,128,256]{1,2,0:T(8,128)(2,1)}), bf16[8,128,256]{1,2,0:T(8,128)(2,1)S(1)}, u32[]{:S(2)}, u32[]{:S(2)}) async-start(bf16[8,128,256]{1,2,0:T(8,128)(2,1)} %copy.135), calls=%async_computation.1 | async-start | bytes 1048576 | tf_op jit(solution)/shard_map/all_to_all | solution.py:148
  180.6 2.6 copy-start.4
  183.2 2.1 copy-start.3
  185.3 2.4 copy-start.15
  190.9 52.5 %all-to-all-start.4 = ((bf16[32,14,2048]{2,1,0:T(8,128)(2,1)}), bf16[32,14,2048]{2,1,0:T(8,128)(2,1)}, u32[]{:S(2)}, u32[]{:S(2)}) async-start(bf16[32,14,2048]{2,1,0:T(8,128)(2,1)} %copy.154), calls=%async_computation.4 | async-start | bytes 4194304 | tf_op jit(solution)/shard_map/all_to_all | solution.py:206
  243.4 53.2 %all-to-all-start.2 = ((bf16[32,14,2048]{2,1,0:T(8,128)(2,1)}), bf16[32,14,2048]{2,1,0:T(8,128)(2,1)}, u32[]{:S(2)}, u32[]{:S(2)}) async-start(bf16[32,14,2048]{2,1,0:T(8,128)(2,1)} %copy.146), calls=%async_computation.2 | async-start | bytes 4194304 | tf_op jit(solution)/shard_map/all_to_all | solution.py:206
  247.7 17.3 %collective-permute-start.3 = (bf16[704,2048]{1,0:T(8,128)(2,1)}, bf16[704,2048]{1,0:T(8,128)(2,1)S(1)}, u32[]{:S(2)}, u32[]{:S(2)}) collective-permute-start(bf16[704,2048]{1,0:T(8,128)(2,1)} %bitcast.244), channel_id=1, source_target_pairs={{0,1},{1,0},{2,3},{3,2},{4,5},{5,4},{6,7},{7,6},{8,9},{9,8},{10,11... | collective-permute-start | bytes 8650760 | tf_op jit(solution)/shard_map/ppermute | solution.py:52
  248.2 7.7 %copy-start.17 = (bf16[1,704,2048]{2,1,0:T(8,128)(2,1)S(1)}, bf16[1,704,2048]{2,1,0:T(8,128)(2,1)}, u32[]{:S(2)}) copy-start(bf16[1,704,2048]{2,1,0:T(8,128)(2,1)} %param.21) | copy-start | bytes 8650756
  265.0 1.7 copy-start.19
  296.6 53.2 %all-to-all-start.5 = ((bf16[32,14,2048]{2,1,0:T(8,128)(2,1)}), bf16[32,14,2048]{2,1,0:T(8,128)(2,1)}, u32[]{:S(2)}, u32[]{:S(2)}) async-start(bf16[32,14,2048]{2,1,0:T(8,128)(2,1)} %copy.159), calls=%async_computation.5 | async-start | bytes 4194304 | tf_op jit(solution)/shard_map/all_to_all | solution.py:212
  301.0 7.7 %copy-start.18 = (bf16[1,704,2048]{2,1,0:T(8,128)(2,1)S(1)}, bf16[1,704,2048]{2,1,0:T(8,128)(2,1)}, u32[]{:S(2)}) copy-start(bf16[1,704,2048]{2,1,0:T(8,128)(2,1)} %param.21) | copy-start | bytes 8650756
  310.3 7.7 %copy-start.20 = (bf16[704,2048]{1,0:T(8,128)(2,1)S(1)}, bf16[704,2048]{1,0:T(8,128)(2,1)}, u32[]{:S(2)}) copy-start(bf16[704,2048]{1,0:T(8,128)(2,1)} %copy-done.19) | copy-start | bytes 8650756
  322.0 32.2 %copy-start.13 = (bf16[2048,16]{0,1:T(8,128)(2,1)S(1)}, bf16[2048,16]{0,1:T(8,128)(2,1)}, u32[]{:S(2)}) copy-start(bf16[2048,16]{0,1:T(8,128)(2,1)} %param.18) | copy-start | bytes 196612
  349.8 53.3 %all-to-all-start.3 = ((bf16[32,14,2048]{2,1,0:T(8,128)(2,1)}), bf16[32,14,2048]{2,1,0:T(8,128)(2,1)}, u32[]{:S(2)}, u32[]{:S(2)}) async-start(bf16[32,14,2048]{2,1,0:T(8,128)(2,1)} %copy.150), calls=%async_computation.3 | async-start | bytes 4194304 | tf_op jit(solution)/shard_map/all_to_all | solution.py:212
  403.1 22.0 %copy-start.16 = (f32[2048]{0:T(1024)S(1)}, f32[2048]{0:T(1024)}, u32[]{:S(2)}) copy-start(f32[2048]{0:T(1024)} %param.22) | copy-start | bytes 24580
  406.7 26.9 %copy-start.5 = (bf16[128,2048]{1,0:T(8,128)(2,1)}, bf16[128,2048]{1,0:T(8,128)(2,1)S(1)}, u32[]{:S(2)}) copy-start(bf16[128,2048]{1,0:T(8,128)(2,1)S(1)} %fusion.27) | copy-start | bytes 1572868
  425.1 18.5 %copy-start.1 = (bf16[2,128,2048]{2,1,0:T(8,128)(2,1)S(1)}, bf16[2,128,2048]{2,1,0:T(8,128)(2,1)}, u32[]{:S(2)}) copy-start(bf16[2,128,2048]{2,1,0:T(8,128)(2,1)} %param.16) | copy-start | bytes 3145732
Sparse Core Ops, SparseCore 0:
  10.7 109.8 all-gather.1

commit v6 on v5

--- a/solution.py
+++ b/solution.py
@@ -87,18 +87,15 @@
     prompt_lengths = lengths[0]
     segment, offset = segment_layout(prompt_lengths, group_tokens)
     normed = rms_scale(token_rows, attn_gain).astype(jnp.bfloat16)
-    group_normed = lax.all_gather(normed, "seq", axis=0, tiled=True)
     part_size = head_size // group_count
     own_part = lax.dynamic_slice_in_dim(
         w_out, lax.axis_index("exp") * part_size, part_size, axis=1
     )
-    seq_part = lax.all_to_all(
-        jnp.broadcast_to(own_part[None], (seq_count,) + own_part.shape),
-        "seq",
-        split_axis=0,
-        concat_axis=0,
-        tiled=True,
-    ).reshape((1, -1) + own_part.shape[1:])
+    part_rows = own_part.shape[0] * part_size
+    joined_rows = jnp.concatenate([normed, own_part.reshape(part_rows, model_width)], axis=0)
+    gathered = lax.all_gather(joined_rows, "seq", axis=0)
+    group_normed = gathered[:, :tok_rows].reshape(group_tokens, model_width)
+    seq_part = gathered[:, tok_rows:].reshape((1, -1) + own_part.shape[1:])
     exp_index = lax.axis_index("exp")
     x_count = group_count // 2
     x_pieces, x_owners = [], []

time: 459 us -> 474 us (1.033)
  waiting for transfers between devices: 245 us -> 270 us
  starting transfers between devices: 34.6 us -> 23.3 us
    all_gather x1, waiting for transfers between devices: 7.56 us -> 88 us  [per_device(): gathered = lax.all_gather(joined_rows, 'seq', axis=0)]
    all_to_all x1 -> x0, waiting for transfers between devices: 77.9 us -> none  [per_device(): lax.all_to_all(jnp.broadcast_to(own_part[None], (seq_count,) + own_part.s...]
    ppermute x1, waiting for transfers between devices: 2.91 us -> 24.7 us  [per_device(): lax.ppermute(seq_part[0], 'exp', [(i, (i + 2 * step) % group_count) for i...]
    all_to_all x1 -> x0, starting transfers between devices: 7.41 us -> none  [per_device(): lax.all_to_all(jnp.broadcast_to(own_part[None], (seq_count,) + own_part.s...]
    unnamed x49 -> x51, local copies, waits for them, and re-layouts: 10.6 us -> 11.2 us
  transfers between devices with their start and end apart: 11 -> 10, of which waited for: 8 -> 7; matrix products, arithmetic and copies ran while one was open for 24% -> 21% of each run, Pallas kernels for 0% -> 0%
where the time goes in v6:
time: 474 us; the launch traced here: 465 us
  waiting for transfers between devices  270 us (57%)
  matrix products  81 us (17%)
  local copies, waits for them, and re-layouts  27.7 us (6%)
  blocking collectives  26.8 us (6%)
  starting transfers between devices  23.3 us (5%)
  other arithmetic  21.3 us (4%)
  between operations  15.3 us (3%)
    all_gather x1, waiting for transfers between devices, per_device(): gathered = lax.all_gather(joined_rows, 'seq', axis=0)  88 us
    all_to_all x2, waiting for transfers between devices, per_device(): lax.all_to_all(outgoing, ('seq', 'exp'), split_axis=0, concat_axis=0, til...  73.4 us
    all_to_all x2, waiting for transfers between devices, per_device(): lax.all_to_all(part_sum.astype(jnp.bfloat16), ('seq', 'exp'), split_axis=...  72.1 us
    dot_general x4, matrix products, share_part(): jnp.einsum('scd,gfd->scgf', rows, pair, preferred_element_type=jnp.float32)  30.5 us
    ppermute x1, waiting for transfers between devices, per_device(): lax.ppermute(seq_part[0], 'exp', [(i, (i + 2 * step) % group_count) for i...  24.7 us
    all_to_all x1, waiting for transfers between devices, per_device(): lax.all_to_all(heads_flat, 'seq', split_axis=0, concat_axis=1, tiled=True)  11.5 us
    unnamed x51, local copies, waits for them, and re-layouts  11.2 us
    all_to_all x1, blocking collectives, per_device(): lax.all_to_all(jnp.broadcast_to(picked.astype(jnp.bfloat16)[None], (seq_c...  10.6 us
  transfers between devices with their start and end apart: 10, of which 7 were waited for; matrix products, arithmetic and copies ran while one was open for 21% of the time, Pallas kernels for 0%

profile of v6, /device:TPU:0, one launch (start us, length us, event | category | flops | bytes accessed | tf_op | source)
XLA Modules:
  0.0 464.9 jit_solution(7154479400449838648)
XLA Ops:
  10.8 8.7 %copy.125 = bf16[2048,3,2,128]{0,3,2,1:T(8,128)(2,1)} copy(bf16[2048,3,2,128]{3,2,1,0:T(2,128)(2,1)} %param.15) | data formatting | bytes 6291456 | tf_op args[3]
  22.9 1.8 multiply_cosine_fusion
  24.7 88.0 %all-gather.3.cloned.1.call-done = bf16[1536,2048]{1,0:T(8,128)(2,1)} async-done(((bf16[192,2048]{1,0:T(8,128)(2,1)}), bf16[1536,2048]{1,0:T(8,128)(2,1)}) %all-gather.3.cloned.1.call-update) | async-done | bytes 6291472 | tf_op jit(solution)/shard_map/all_gather | solution.py:96
  112.7 2.5 slice.215
  115.2 1.9 slice.214
  117.7 3.5 fusion.199
  125.6 1.7 fusion.188
  127.8 3.3 convert.18
  132.1 1.5 fusion.52
  133.6 2.4 fusion.53
  136.1 2.9 fusion.183
  138.9 2.3 fusion.182
  141.2 2.1 fusion.54
  143.4 1.6 fusion.55
  145.1 24.7 %collective-permute-done = bf16[16,32,2048]{2,1,0:T(8,128)(2,1)} collective-permute-done((bf16[16,32,2048]{2,1,0:T(8,128)(2,1)S(1)}, bf16[16,32,2048]{2,1,0:T(8,128)(2,1)}, u32[]{:S(2)}, u32[]{:S(2)}) %collective-permute-start) | collective-permute-done | bytes 2097184 | tf_op jit(solution)/shard_map/ppermute | solution.py:104
  169.8 4.0 pad_maximum_fusion
  175.6 4.0 all-to-all-start
  179.8 1.7 reduce-window.11
  183.0 11.5 %all-to-all-done = bf16[8,128,256]{1,2,0:T(8,128)(2,1)S(1)} async-done(((bf16[8,128,256]{1,2,0:T(8,128)(2,1)}), bf16[8,128,256]{1,2,0:T(8,128)(2,1)S(1)}, u32[]{:S(2)}, u32[]{:S(2)}) %all-to-all-start) | async-done | bytes 524320 | tf_op jit(solution)/shard_map/all_to_all | solution.py:145
  194.9 2.1 convolution_bitcast_fusion.3
  197.0 2.1 convolution_bitcast_fusion.2
  199.2 2.4 multiply_reduce_fusion
  202.4 2.4 copy.154
  204.8 3.7 all-to-all-start.3
  209.2 2.3 copy.146
  211.5 45.9 %all-to-all-done.3 = bf16[32,14,2048]{2,1,0:T(8,128)(2,1)} async-done(((bf16[32,14,2048]{2,1,0:T(8,128)(2,1)}), bf16[32,14,2048]{2,1,0:T(8,128)(2,1)}, u32[]{:S(2)}, u32[]{:S(2)}) %all-to-all-start.3) | async-done | bytes 1835040 | tf_op jit(solution)/shard_map/all_to_all | solution.py:203
  257.4 4.3 all-to-all-start.1
  262.2 7.7 %fusion.8 = f32[32,14,2,704]{3,0,2,1:T(8,128)S(1)} fusion(bf16[1,2,704,2048]{3,2,1,0:T(8,128)(2,1)} %param.20, bf16[32,14,2048,1]{2,1,0,3:T(8,128)(2,1)} %bitcast.53), kind=kOutput, calls=%fused_computation.8 | convolution fusion | flops 2583691264 | bytes 10125312 | tf_op jit(solution)/shard_map/scd,gfd->scgf/dot_general | solution.py:189
  269.8 1.6 convolution_convert_fusion.1
  271.5 7.5 %fusion.4 = f32[32,14,2,704]{3,0,1,2:T(8,128)S(1)} fusion(bf16[2,704,2048]{2,1,0:T(8,128)(2,1)} %collective-permute-done.2, bf16[32,14,2048]{2,1,0:T(8,128)(2,1)} %all-to-all-done.3), kind=kOutput, calls=%fused_computation.4 | convolution fusion | flops 2583691264 | bytes 10125312 | tf_op jit(solution)/shard_map/scd,gfd->scgf/dot_general | solution.py:189
  279.0 1.7 add_convert_fusion
  280.7 2.4 copy.159
  283.1 27.5 %all-to-all-done.1 = bf16[32,14,2048]{2,1,0:T(8,128)(2,1)} async-done(((bf16[32,14,2048]{2,1,0:T(8,128)(2,1)}), bf16[32,14,2048]{2,1,0:T(8,128)(2,1)}, u32[]{:S(2)}, u32[]{:S(2)}) %all-to-all-start.1) | async-done | bytes 1835040 | tf_op jit(solution)/shard_map/all_to_all | solution.py:203
  310.6 4.4 all-to-all-start.4
  315.0 7.7 %fusion.10 = f32[32,14,2,704]{3,0,2,1:T(8,128)S(1)} fusion(bf16[1,2,704,2048]{3,2,1,0:T(8,128)(2,1)} %param.20, bf16[32,14,2048,1]{2,1,0,3:T(8,128)(2,1)} %bitcast.41), kind=kOutput, calls=%fused_computation.10 | convolution fusion | flops 2583691264 | bytes 10125312 | tf_op jit(solution)/shard_map/scd,gfd->scgf/dot_general | solution.py:189
  322.6 1.6 convolution_convert_fusion.4
  324.3 7.7 %fusion.6 = f32[32,14,2,704]{3,0,2,1:T(8,128)S(1)} fusion(bf16[2,704,2048]{2,1,0:T(8,128)(2,1)} %collective-permute-done.2, bf16[32,14,2048,1]{2,1,0,3:T(8,128)(2,1)} %bitcast.41), kind=kOutput, calls=%fused_computation.6 | convolution fusion | flops 2583691264 | bytes 10125312 | tf_op jit(solution)/shard_map/scd,gfd->scgf/dot_general | solution.py:189
  332.0 1.7 add_convert_fusion.1
  333.7 2.4 copy.150
  336.0 27.8 %all-to-all-done.4 = bf16[32,14,2048]{2,1,0:T(8,128)(2,1)} async-done(((bf16[32,14,2048]{2,1,0:T(8,128)(2,1)}), bf16[32,14,2048]{2,1,0:T(8,128)(2,1)}, u32[]{:S(2)}, u32[]{:S(2)}) %all-to-all-start.4) | async-done | bytes 1835040 | tf_op jit(solution)/shard_map/all_to_all | solution.py:209
  363.8 4.4 all-to-all-start.2
  369.3 3.6 convolution_bitcast_fusion
  372.8 44.3 %all-to-all-done.2 = bf16[32,14,2048]{2,1,0:T(8,128)(2,1)} async-done(((bf16[32,14,2048]{2,1,0:T(8,128)(2,1)}), bf16[32,14,2048]{2,1,0:T(8,128)(2,1)}, u32[]{:S(2)}, u32[]{:S(2)}) %all-to-all-start.2) | async-done | bytes 1835040 | tf_op jit(solution)/shard_map/all_to_all | solution.py:209
  417.1 3.6 fusion.27
  421.0 10.6 %all_to_all.51 = bf16[8,4,2048]{2,1,0:T(4,128)(2,1)S(1)} all-to-all(bf16[8,4,2048]{2,1,0:T(4,128)(2,1)S(1)} %broadcast_in_dim.89), channel_id=1, replica_groups=mesh['seq'=8,'exp'=4] {'seq'}, dimensions={0} | all-to-all | bytes 262144 | tf_op jit(solution)/shard_map/all_to_all | solution.py:225
  431.7 7.2 %all_to_all.52 = bf16[4,4,2048]{2,1,0:T(4,128)(2,1)S(1)} all-to-all(bf16[4,4,2048]{2,1,0:T(4,128)(2,1)S(1)} %broadcast_in_dim.90), channel_id=1, replica_groups=mesh['seq'=8,'exp'=4] {'exp'}, dimensions={0} | all-to-all | bytes 131072 | tf_op jit(solution)/shard_map/all_to_all | solution.py:235
  439.1 8.4 %fusion.198 = (f32[16]{0:T(128)S(1)}, f32[16,3200]{1,0:T(8,128)S(1)}) fusion(bf16[3200,2048]{1,0:T(8,128)(2,1)} %param.23, f32[16,2048]{1,0:T(8,128)S(1)} %reshape.451, f32[2048]{0:T(1024)S(1)} %copy-done.17, f32[16]{0:T(128)S(1)} %rsqrt.30), kind=kOutput, calls=%fused_computation.242 | convolution fusion | flops 209864688 | bytes 13451392 | tf_op jit(solution)/shard_map/dot_general | solution.py:243
  447.8 8.9 %all_to_all.53 = f32[32,2,16]{2,1,0:T(2,128)S(1)} all-to-all(f32[32,2,16]{2,1,0:T(2,128)S(1)} %broadcast_in_dim.91), channel_id=1, replica_groups=mesh['seq'=8,'exp'=4] {'seq','exp'}, dimensions={0} | all-to-all | bytes 8192 | tf_op jit(solution)/shard_map/all_to_all | solution.py:249
  (136 shorter events, 21.8 us)
Async XLA Ops:
  7.2 1.4 copy-start
  7.2 105.5 %all-gather.3.cloned.1.call-start = ((), (), s32[]{:S(2)}) async-start(), calls=%async_computation.8 | async-start | bytes 7077888 | tf_op jit(solution)/shard_map/all_gather | solution.py:96
  10.8 8.7 %copy-start.22 = (s32[1,4]{1,0:T(1,128)S(1)}, s32[1,4]{1,0:T(1,128)}, u32[]{:S(2)}) copy-start(s32[1,4]{1,0:T(1,128)} %param.13) | copy-start | bytes 52
  115.2 2.5 copy-start.4
  121.2 1.7 copy-start.2
  121.2 3.1 copy-start.10
  121.2 3.1 copy-start.11
  122.9 47.0 %collective-permute-start = (bf16[16,32,2048]{2,1,0:T(8,128)(2,1)S(1)}, bf16[16,32,2048]{2,1,0:T(8,128)(2,1)}, u32[]{:S(2)}, u32[]{:S(2)}) collective-permute-start(bf16[16,32,2048]{2,1,0:T(8,128)(2,1)S(1)} %bitcast.224), channel_id=1, source_target_pairs={{0,2},{1,3},{2,0},{3,1},{4,6},{5,7},{6,4},{7,5},{8,10},{9,11},{10,... | collective-permute-start | bytes 6291464 | tf_op jit(solution)/shard_map/ppermute | solution.py:104
  125.6 1.7 copy-start.7
  125.6 1.7 copy-start.8
  125.6 1.7 copy-start.9
  136.1 2.9 copy-start.12
  141.2 2.2 copy-start.23
  143.4 1.7 copy-start.13
  169.8 4.5 copy-start.15
  173.8 21.1 %collective-permute-start.1 = (bf16[2,16,32,2048]{3,2,1,0:T(8,128)(2,1)}, bf16[2,16,32,2048]{3,2,1,0:T(8,128)(2,1)}, u32[]{:S(2)}, u32[]{:S(2)}) collective-permute-start(bf16[2,16,32,2048]{3,2,1,0:T(8,128)(2,1)} %pad_maximum_fusion), channel_id=1, source_target_pairs={{0,1},{1,0},{2,3},{3,2},{4,5},{5,4},{6,7},{7,6},{8,9},{9,8},{10,11... | collective-permute-start | bytes 12582920 | tf_op jit(solution)/shard_map/ppermute | solution.py:52
  173.8 97.6 %collective-permute-start.2 = (bf16[2,704,2048]{2,1,0:T(8,128)(2,1)}, bf16[2,704,2048]{2,1,0:T(8,128)(2,1)}, u32[]{:S(2)}, u32[]{:S(2)}) collective-permute-start(bf16[2,704,2048]{2,1,0:T(8,128)(2,1)} %bitcast.42), channel_id=1, source_target_pairs={{0,1},{1,0},{2,3},{3,2},{4,5},{5,4},{6,7},{7,6},{8,9},{9,8},{10,11... | collective-permute-start | bytes 17301512 | tf_op jit(solution)/shard_map/ppermute | solution.py:52
  175.6 18.9 %all-to-all-start = ((bf16[8,128,256]{1,2,0:T(8,128)(2,1)}), bf16[8,128,256]{1,2,0:T(8,128)(2,1)S(1)}, u32[]{:S(2)}, u32[]{:S(2)}) async-start(bf16[8,128,256]{1,2,0:T(8,128)(2,1)} %copy.135), calls=%async_computation | async-start | bytes 1048576 | tf_op jit(solution)/shard_map/all_to_all | solution.py:145
  194.5 2.6 copy-start.5
  197.0 2.1 copy-start.3
  199.2 2.4 copy-start.16
  204.8 52.6 %all-to-all-start.3 = ((bf16[32,14,2048]{2,1,0:T(8,128)(2,1)}), bf16[32,14,2048]{2,1,0:T(8,128)(2,1)}, u32[]{:S(2)}, u32[]{:S(2)}) async-start(bf16[32,14,2048]{2,1,0:T(8,128)(2,1)} %copy.154), calls=%async_computation.3 | async-start | bytes 4194304 | tf_op jit(solution)/shard_map/all_to_all | solution.py:203
  257.4 53.2 %all-to-all-start.1 = ((bf16[32,14,2048]{2,1,0:T(8,128)(2,1)}), bf16[32,14,2048]{2,1,0:T(8,128)(2,1)}, u32[]{:S(2)}, u32[]{:S(2)}) async-start(bf16[32,14,2048]{2,1,0:T(8,128)(2,1)} %copy.146), calls=%async_computation.1 | async-start | bytes 4194304 | tf_op jit(solution)/shard_map/all_to_all | solution.py:203
  261.7 17.3 %collective-permute-start.3 = (bf16[704,2048]{1,0:T(8,128)(2,1)}, bf16[704,2048]{1,0:T(8,128)(2,1)S(1)}, u32[]{:S(2)}, u32[]{:S(2)}) collective-permute-start(bf16[704,2048]{1,0:T(8,128)(2,1)} %bitcast.251), channel_id=1, source_target_pairs={{0,1},{1,0},{2,3},{3,2},{4,5},{5,4},{6,7},{7,6},{8,9},{9,8},{10,11... | collective-permute-start | bytes 8650760 | tf_op jit(solution)/shard_map/ppermute | solution.py:52
  262.2 7.7 %copy-start.18 = (bf16[1,704,2048]{2,1,0:T(8,128)(2,1)S(1)}, bf16[1,704,2048]{2,1,0:T(8,128)(2,1)}, u32[]{:S(2)}) copy-start(bf16[1,704,2048]{2,1,0:T(8,128)(2,1)} %param.21) | copy-start | bytes 8650756
  279.0 1.7 copy-start.20
  310.6 53.2 %all-to-all-start.4 = ((bf16[32,14,2048]{2,1,0:T(8,128)(2,1)}), bf16[32,14,2048]{2,1,0:T(8,128)(2,1)}, u32[]{:S(2)}, u32[]{:S(2)}) async-start(bf16[32,14,2048]{2,1,0:T(8,128)(2,1)} %copy.159), calls=%async_computation.4 | async-start | bytes 4194304 | tf_op jit(solution)/shard_map/all_to_all | solution.py:209
  315.0 7.7 %copy-start.19 = (bf16[1,704,2048]{2,1,0:T(8,128)(2,1)S(1)}, bf16[1,704,2048]{2,1,0:T(8,128)(2,1)}, u32[]{:S(2)}) copy-start(bf16[1,704,2048]{2,1,0:T(8,128)(2,1)} %param.21) | copy-start | bytes 8650756
  324.3 7.7 %copy-start.21 = (bf16[704,2048]{1,0:T(8,128)(2,1)S(1)}, bf16[704,2048]{1,0:T(8,128)(2,1)}, u32[]{:S(2)}) copy-start(bf16[704,2048]{1,0:T(8,128)(2,1)} %copy-done.20) | copy-start | bytes 8650756
  336.0 32.2 %copy-start.14 = (bf16[2048,16]{0,1:T(8,128)(2,1)S(1)}, bf16[2048,16]{0,1:T(8,128)(2,1)}, u32[]{:S(2)}) copy-start(bf16[2048,16]{0,1:T(8,128)(2,1)} %param.18) | copy-start | bytes 196612
  363.8 53.3 %all-to-all-start.2 = ((bf16[32,14,2048]{2,1,0:T(8,128)(2,1)}), bf16[32,14,2048]{2,1,0:T(8,128)(2,1)}, u32[]{:S(2)}, u32[]{:S(2)}) async-start(bf16[32,14,2048]{2,1,0:T(8,128)(2,1)} %copy.150), calls=%async_computation.2 | async-start | bytes 4194304 | tf_op jit(solution)/shard_map/all_to_all | solution.py:209
  417.1 22.0 %copy-start.17 = (f32[2048]{0:T(1024)S(1)}, f32[2048]{0:T(1024)}, u32[]{:S(2)}) copy-start(f32[2048]{0:T(1024)} %param.22) | copy-start | bytes 24580
  420.7 26.9 %copy-start.6 = (bf16[128,2048]{1,0:T(8,128)(2,1)}, bf16[128,2048]{1,0:T(8,128)(2,1)S(1)}, u32[]{:S(2)}) copy-start(bf16[128,2048]{1,0:T(8,128)(2,1)S(1)} %fusion.27) | copy-start | bytes 1572868
  439.1 18.5 %copy-start.1 = (bf16[2,128,2048]{2,1,0:T(8,128)(2,1)S(1)}, bf16[2,128,2048]{2,1,0:T(8,128)(2,1)}, u32[]{:S(2)}) copy-start(bf16[2,128,2048]{2,1,0:T(8,128)(2,1)} %param.16) | copy-start | bytes 3145732
Sparse Core Ops, SparseCore 0:
  10.9 101.7 all-gather.2

commit v7 on v5

--- a/solution.py
+++ b/solution.py
@@ -147,8 +147,7 @@
     heads_flat = blocks.reshape(group_tokens, head_count * head_size)
     regrouped = lax.all_to_all(heads_flat, "seq", split_axis=0, concat_axis=1, tiled=True)
     pieces, owners = [seq_part[0]] + x_pieces, [exp_index] + x_owners
-    partner_pieces = pair_swap(jnp.stack(pieces))
-    pieces = pieces + [partner_pieces[step] for step in range(x_count)]
+    pieces = pieces + [pair_swap(piece) for piece in pieces]
     owners = owners + [owner ^ 1 for owner in owners]
     regrouped = regrouped.reshape(tok_rows, -1, group_count, part_size)
     mixed = jnp.zeros((tok_rows, model_width), jnp.float32)

time: 459 us -> 455 us (level)
    another operation x6 -> x5, other arithmetic: 10.5 us -> 6.47 us
  transfers between devices with their start and end apart: 11 -> 12, of which waited for: 8 -> 8; matrix products, arithmetic and copies ran while one was open for 24% -> 24% of each run, Pallas kernels for 0% -> 0%
where the time goes in v7:
time: 455 us; the launch traced here: 447 us
  waiting for transfers between devices  245 us (54%)
  matrix products  83.7 us (18%)
  starting transfers between devices  34.6 us (8%)
  blocking collectives  26.8 us (6%)
  local copies, waits for them, and re-layouts  24.3 us (5%)
  other arithmetic  17.2 us (4%)
  between operations  15.1 us (3%)
    all_to_all x1, waiting for transfers between devices, per_device(): lax.all_to_all(jnp.broadcast_to(own_part[None], (seq_count,) + own_part.s...  78 us
    all_to_all x2, waiting for transfers between devices, per_device(): lax.all_to_all(outgoing, ('seq', 'exp'), split_axis=0, concat_axis=0, til...  73.4 us
    all_to_all x2, waiting for transfers between devices, per_device(): lax.all_to_all(part_sum.astype(jnp.bfloat16), ('seq', 'exp'), split_axis=...  72 us
    dot_general x4, matrix products, share_part(): jnp.einsum('scd,gfd->scgf', rows, pair, preferred_element_type=jnp.float32)  30.5 us
    all_to_all x1, waiting for transfers between devices, per_device(): lax.all_to_all(heads_flat, 'seq', split_axis=0, concat_axis=1, tiled=True)  11.2 us
    all_to_all x1, blocking collectives, per_device(): lax.all_to_all(jnp.broadcast_to(picked.astype(jnp.bfloat16)[None], (seq_c...  10.6 us
    unnamed x49, local copies, waits for them, and re-layouts  10.6 us
  transfers between devices with their start and end apart: 12, of which 8 were waited for; matrix products, arithmetic and copies ran while one was open for 24% of the time, Pallas kernels for 0%

profile of v7, /device:TPU:0, one launch (start us, length us, event | category | flops | bytes accessed | tf_op | source)
XLA Modules:
  0.0 446.8 jit_solution(1451306591706699209)
XLA Ops:
  8.5 2.0 fusion.58
  10.6 1.6 broadcast_in_dim.70
  12.3 7.4 %all-to-all-start = ((bf16[8,2,32,2048]{3,2,1,0:T(8,128)(2,1)}), bf16[8,2,32,2048]{3,2,1,0:T(8,128)(2,1)S(1)}, u32[]{:S(2)}, u32[]{:S(2)}) async-start(bf16[8,2,32,2048]{3,2,1,0:T(8,128)(2,1)} %broadcast_in_dim.70), calls=%async_computation | async-start | bytes 4194304 | tf_op jit(solution)/shard_map/all_to_all | solution.py:95
  19.9 8.7 %copy.125 = bf16[2048,3,2,128]{0,3,2,1:T(8,128)(2,1)} copy(bf16[2048,3,2,128]{3,2,1,0:T(2,128)(2,1)} %param.15) | data formatting | bytes 6291456 | tf_op args[3]
  31.8 1.8 multiply_cosine_fusion
  33.6 78.0 %all-to-all-done = bf16[8,2,32,2048]{3,2,1,0:T(8,128)(2,1)S(1)} async-done(((bf16[8,2,32,2048]{3,2,1,0:T(8,128)(2,1)}), bf16[8,2,32,2048]{3,2,1,0:T(8,128)(2,1)S(1)}, u32[]{:S(2)}, u32[]{:S(2)}) %all-to-all-start) | async-done | bytes 2097184 | tf_op jit(solution)/shard_map/all_to_all | solution.py:95
  113.1 7.6 %all-gather.2.cloned.1.call-done = bf16[1024,2048]{1,0:T(8,128)(2,1)} async-done(((bf16[128,2048]{1,0:T(8,128)(2,1)}), bf16[1024,2048]{1,0:T(8,128)(2,1)}) %all-gather.2.cloned.1.call-update) | async-done | bytes 4194320 | tf_op jit(solution)/shard_map/all_gather | solution.py:90
  120.7 6.2 %fusion.199 = f32[1024,768]{0,1:S(1)} fusion(bf16[1024,2048]{1,0:T(8,128)(2,1)} %all-gather.2.cloned.1.call-done, bf16[2048,768]{0,1:T(8,128)(2,1)} %bitcast.220), kind=kOutput, calls=%fused_computation.239 | convolution fusion | flops 3221225472 | bytes 10485760
  129.8 1.7 fusion.188
  131.9 3.3 convert.18
  135.2 2.4 fusion.53
  138.7 2.9 fusion.183
  141.6 2.3 fusion.182
  143.9 2.1 fusion.54
  146.0 1.6 fusion.55
  149.3 2.9 collective-permute-done
  154.0 8.0 %all-to-all-start.1 = ((bf16[8,128,256]{1,2,0:T(8,128)(2,1)}), bf16[8,128,256]{1,2,0:T(8,128)(2,1)S(1)}, u32[]{:S(2)}, u32[]{:S(2)}) async-start(bf16[8,128,256]{1,2,0:T(8,128)(2,1)} %copy.135), calls=%async_computation.1 | async-start | bytes 1048576 | tf_op jit(solution)/shard_map/all_to_all | solution.py:148
  162.2 1.7 reduce-window.11
  165.4 11.2 %all-to-all-done.1 = bf16[8,128,256]{1,2,0:T(8,128)(2,1)S(1)} async-done(((bf16[8,128,256]{1,2,0:T(8,128)(2,1)}), bf16[8,128,256]{1,2,0:T(8,128)(2,1)S(1)}, u32[]{:S(2)}, u32[]{:S(2)}) %all-to-all-start.1) | async-done | bytes 524320 | tf_op jit(solution)/shard_map/all_to_all | solution.py:148
  177.1 2.1 convolution_bitcast_fusion.3
  179.2 2.1 convolution_bitcast_fusion.2
  181.3 2.4 multiply_reduce_fusion
  184.5 2.4 copy.154
  186.9 3.6 all-to-all-start.4
  191.2 2.3 copy.146
  193.5 45.9 %all-to-all-done.4 = bf16[32,14,2048]{2,1,0:T(8,128)(2,1)} async-done(((bf16[32,14,2048]{2,1,0:T(8,128)(2,1)}), bf16[32,14,2048]{2,1,0:T(8,128)(2,1)}, u32[]{:S(2)}, u32[]{:S(2)}) %all-to-all-start.4) | async-done | bytes 1835040 | tf_op jit(solution)/shard_map/all_to_all | solution.py:205
  239.4 4.3 all-to-all-start.2
  244.2 7.7 %fusion.8 = f32[32,14,2,704]{3,0,2,1:T(8,128)S(1)} fusion(bf16[1,2,704,2048]{3,2,1,0:T(8,128)(2,1)} %param.20, bf16[32,14,2048,1]{2,1,0,3:T(8,128)(2,1)} %bitcast.46), kind=kOutput, calls=%fused_computation.8 | convolution fusion | flops 2583691264 | bytes 10125312 | tf_op jit(solution)/shard_map/scd,gfd->scgf/dot_general | solution.py:191
  251.8 1.6 convolution_convert_fusion.1
  253.5 7.5 %fusion.4 = f32[32,14,2,704]{3,0,1,2:T(8,128)S(1)} fusion(bf16[2,704,2048]{2,1,0:T(8,128)(2,1)} %collective-permute-done.3, bf16[32,14,2048]{2,1,0:T(8,128)(2,1)} %all-to-all-done.4), kind=kOutput, calls=%fused_computation.4 | convolution fusion | flops 2583691264 | bytes 10125312 | tf_op jit(solution)/shard_map/scd,gfd->scgf/dot_general | solution.py:191
  261.0 1.7 add_convert_fusion
  262.7 2.4 copy.159
  265.1 27.5 %all-to-all-done.2 = bf16[32,14,2048]{2,1,0:T(8,128)(2,1)} async-done(((bf16[32,14,2048]{2,1,0:T(8,128)(2,1)}), bf16[32,14,2048]{2,1,0:T(8,128)(2,1)}, u32[]{:S(2)}, u32[]{:S(2)}) %all-to-all-start.2) | async-done | bytes 1835040 | tf_op jit(solution)/shard_map/all_to_all | solution.py:205
  292.6 4.4 all-to-all-start.5
  297.0 7.7 %fusion.10 = f32[32,14,2,704]{3,0,2,1:T(8,128)S(1)} fusion(bf16[1,2,704,2048]{3,2,1,0:T(8,128)(2,1)} %param.20, bf16[32,14,2048,1]{2,1,0,3:T(8,128)(2,1)} %bitcast.34), kind=kOutput, calls=%fused_computation.10 | convolution fusion | flops 2583691264 | bytes 10125312 | tf_op jit(solution)/shard_map/scd,gfd->scgf/dot_general | solution.py:191
  304.7 1.6 convolution_convert_fusion.4
  306.3 7.7 %fusion.6 = f32[32,14,2,704]{3,0,2,1:T(8,128)S(1)} fusion(bf16[2,704,2048]{2,1,0:T(8,128)(2,1)} %collective-permute-done.3, bf16[32,14,2048,1]{2,1,0,3:T(8,128)(2,1)} %bitcast.34), kind=kOutput, calls=%fused_computation.6 | convolution fusion | flops 2583691264 | bytes 10125312 | tf_op jit(solution)/shard_map/scd,gfd->scgf/dot_general | solution.py:191
  314.0 1.7 add_convert_fusion.1
  315.7 2.4 copy.150
  318.0 27.8 %all-to-all-done.5 = bf16[32,14,2048]{2,1,0:T(8,128)(2,1)} async-done(((bf16[32,14,2048]{2,1,0:T(8,128)(2,1)}), bf16[32,14,2048]{2,1,0:T(8,128)(2,1)}, u32[]{:S(2)}, u32[]{:S(2)}) %all-to-all-start.5) | async-done | bytes 1835040 | tf_op jit(solution)/shard_map/all_to_all | solution.py:211
  345.8 4.4 all-to-all-start.3
  351.3 3.6 convolution_bitcast_fusion
  354.8 44.3 %all-to-all-done.3 = bf16[32,14,2048]{2,1,0:T(8,128)(2,1)} async-done(((bf16[32,14,2048]{2,1,0:T(8,128)(2,1)}), bf16[32,14,2048]{2,1,0:T(8,128)(2,1)}, u32[]{:S(2)}, u32[]{:S(2)}) %all-to-all-start.3) | async-done | bytes 1835040 | tf_op jit(solution)/shard_map/all_to_all | solution.py:211
  399.1 3.6 fusion.27
  403.0 10.6 %all_to_all.56 = bf16[8,4,2048]{2,1,0:T(4,128)(2,1)S(1)} all-to-all(bf16[8,4,2048]{2,1,0:T(4,128)(2,1)S(1)} %broadcast_in_dim.92), channel_id=1, replica_groups=mesh['seq'=8,'exp'=4] {'seq'}, dimensions={0} | all-to-all | bytes 262144 | tf_op jit(solution)/shard_map/all_to_all | solution.py:227
  413.7 7.2 %all_to_all.57 = bf16[4,4,2048]{2,1,0:T(4,128)(2,1)S(1)} all-to-all(bf16[4,4,2048]{2,1,0:T(4,128)(2,1)S(1)} %broadcast_in_dim.93), channel_id=1, replica_groups=mesh['seq'=8,'exp'=4] {'exp'}, dimensions={0} | all-to-all | bytes 131072 | tf_op jit(solution)/shard_map/all_to_all | solution.py:237
  421.2 8.4 %fusion.198 = (f32[16]{0:T(128)S(1)}, f32[16,3200]{1,0:T(8,128)S(1)}) fusion(bf16[3200,2048]{1,0:T(8,128)(2,1)} %param.23, f32[16,2048]{1,0:T(8,128)S(1)} %reshape.444, f32[2048]{0:T(1024)S(1)} %copy-done.16, f32[16]{0:T(128)S(1)} %rsqrt.30), kind=kOutput, calls=%fused_computation.238 | convolution fusion | flops 209864688 | bytes 13451392 | tf_op jit(solution)/shard_map/dot_general | solution.py:245
  429.9 8.9 %all_to_all.58 = f32[32,2,16]{2,1,0:T(2,128)S(1)} all-to-all(f32[32,2,16]{2,1,0:T(2,128)S(1)} %broadcast_in_dim.94), channel_id=1, replica_groups=mesh['seq'=8,'exp'=4] {'seq','exp'}, dimensions={0} | all-to-all | bytes 8192 | tf_op jit(solution)/shard_map/all_to_all | solution.py:251
  (135 shorter events, 20.5 us)
Async XLA Ops:
  7.2 3.4 copy-start
  7.2 113.5 %all-gather.2.cloned.1.call-start = ((), (), s32[]{:S(2)}) async-start(), calls=%async_computation.9 | async-start | bytes 4718592 | tf_op jit(solution)/shard_map/all_gather | solution.py:90
  12.3 7.4 %copy-start.21 = (s32[1,4]{1,0:T(1,128)S(1)}, s32[1,4]{1,0:T(1,128)}, u32[]{:S(2)}) copy-start(s32[1,4]{1,0:T(1,128)} %param.13) | copy-start | bytes 52
  12.3 99.3 %all-to-all-start = ((bf16[8,2,32,2048]{3,2,1,0:T(8,128)(2,1)}), bf16[8,2,32,2048]{3,2,1,0:T(8,128)(2,1)S(1)}, u32[]{:S(2)}, u32[]{:S(2)}) async-start(bf16[8,2,32,2048]{3,2,1,0:T(8,128)(2,1)} %broadcast_in_dim.70), calls=%async_computation | async-start | bytes 4194304 | tf_op jit(solution)/shard_map/all_to_all | solution.py:95
  111.6 40.6 %collective-permute-start = (bf16[16,32,2048]{2,1,0:T(8,128)(2,1)S(1)}, bf16[16,32,2048]{2,1,0:T(8,128)(2,1)}, u32[]{:S(2)}, u32[]{:S(2)}) collective-permute-start(bf16[16,32,2048]{2,1,0:T(8,128)(2,1)S(1)} %bitcast.217), channel_id=1, source_target_pairs={{0,2},{1,3},{2,0},{3,1},{4,6},{5,7},{6,4},{7,5},{8,10},{9,11},{10,... | collective-permute-start | bytes 6291464 | tf_op jit(solution)/shard_map/ppermute | solution.py:107
  113.1 64.0 %collective-permute-start.1 = (bf16[16,32,2048]{2,1,0:T(8,128)(2,1)S(1)}, bf16[16,32,2048]{2,1,0:T(8,128)(2,1)}, u32[]{:S(2)}, u32[]{:S(2)}) collective-permute-start(bf16[16,32,2048]{2,1,0:T(8,128)(2,1)S(1)} %bitcast.218), channel_id=1, source_target_pairs={{0,1},{1,0},{2,3},{3,2},{4,5},{5,4},{6,7},{7,6},{8,9},{9,8},{10,11... | collective-permute-start | bytes 6291464 | tf_op jit(solution)/shard_map/ppermute | solution.py:52
  126.8 1.7 copy-start.2
  126.9 1.7 copy-start.9
  126.9 1.7 copy-start.10
  129.8 1.7 copy-start.6
  129.8 1.7 copy-start.7
  129.8 1.7 copy-start.8
  138.7 2.9 copy-start.11
  143.9 2.2 copy-start.22
  147.7 1.6 copy-start.12
  147.7 5.1 %copy-start.14 = (s32[1,128,6]{1,0,2:T(1,128)S(1)}, s32[1,128,6]{1,0,2:T(1,128)}, u32[]{:S(2)}) copy-start(s32[1,128,6]{1,0,2:T(1,128)} %param.19) | copy-start | bytes 9220
  152.2 26.9 %collective-permute-start.2 = (bf16[16,32,2048]{2,1,0:T(8,128)(2,1)}, bf16[16,32,2048]{2,1,0:T(8,128)(2,1)}, u32[]{:S(2)}, u32[]{:S(2)}) collective-permute-start(bf16[16,32,2048]{2,1,0:T(8,128)(2,1)} %collective-permute-done), channel_id=1, source_target_pairs={{0,1},{1,0},{2,3},{3,2},{4,5},{5,4},{6,7},{7,6},{8,9},{9,8},{10,11... | collective-permute-start | bytes 6291464 | tf_op jit(solution)/shard_map/ppermute | solution.py:52
  152.2 101.3 %collective-permute-start.3 = (bf16[2,704,2048]{2,1,0:T(8,128)(2,1)}, bf16[2,704,2048]{2,1,0:T(8,128)(2,1)}, u32[]{:S(2)}, u32[]{:S(2)}) collective-permute-start(bf16[2,704,2048]{2,1,0:T(8,128)(2,1)} %bitcast.238), channel_id=1, source_target_pairs={{0,1},{1,0},{2,3},{3,2},{4,5},{5,4},{6,7},{7,6},{8,9},{9,8},{10,11... | collective-permute-start | bytes 17301512 | tf_op jit(solution)/shard_map/ppermute | solution.py:52
  154.0 22.6 %all-to-all-start.1 = ((bf16[8,128,256]{1,2,0:T(8,128)(2,1)}), bf16[8,128,256]{1,2,0:T(8,128)(2,1)S(1)}, u32[]{:S(2)}, u32[]{:S(2)}) async-start(bf16[8,128,256]{1,2,0:T(8,128)(2,1)} %copy.135), calls=%async_computation.1 | async-start | bytes 1048576 | tf_op jit(solution)/shard_map/all_to_all | solution.py:148
  176.6 2.6 copy-start.4
  179.1 2.2 copy-start.3
  181.3 2.4 copy-start.15
  186.9 52.5 %all-to-all-start.4 = ((bf16[32,14,2048]{2,1,0:T(8,128)(2,1)}), bf16[32,14,2048]{2,1,0:T(8,128)(2,1)}, u32[]{:S(2)}, u32[]{:S(2)}) async-start(bf16[32,14,2048]{2,1,0:T(8,128)(2,1)} %copy.154), calls=%async_computation.4 | async-start | bytes 4194304 | tf_op jit(solution)/shard_map/all_to_all | solution.py:205
  239.4 53.2 %all-to-all-start.2 = ((bf16[32,14,2048]{2,1,0:T(8,128)(2,1)}), bf16[32,14,2048]{2,1,0:T(8,128)(2,1)}, u32[]{:S(2)}, u32[]{:S(2)}) async-start(bf16[32,14,2048]{2,1,0:T(8,128)(2,1)} %copy.146), calls=%async_computation.2 | async-start | bytes 4194304 | tf_op jit(solution)/shard_map/all_to_all | solution.py:205
  243.7 17.3 %collective-permute-start.4 = (bf16[704,2048]{1,0:T(8,128)(2,1)}, bf16[704,2048]{1,0:T(8,128)(2,1)S(1)}, u32[]{:S(2)}, u32[]{:S(2)}) collective-permute-start(bf16[704,2048]{1,0:T(8,128)(2,1)} %bitcast.239), channel_id=1, source_target_pairs={{0,1},{1,0},{2,3},{3,2},{4,5},{5,4},{6,7},{7,6},{8,9},{9,8},{10,11... | collective-permute-start | bytes 8650760 | tf_op jit(solution)/shard_map/ppermute | solution.py:52
  244.2 7.7 %copy-start.17 = (bf16[1,704,2048]{2,1,0:T(8,128)(2,1)S(1)}, bf16[1,704,2048]{2,1,0:T(8,128)(2,1)}, u32[]{:S(2)}) copy-start(bf16[1,704,2048]{2,1,0:T(8,128)(2,1)} %param.21) | copy-start | bytes 8650756
  261.0 1.7 copy-start.19
  292.6 53.2 %all-to-all-start.5 = ((bf16[32,14,2048]{2,1,0:T(8,128)(2,1)}), bf16[32,14,2048]{2,1,0:T(8,128)(2,1)}, u32[]{:S(2)}, u32[]{:S(2)}) async-start(bf16[32,14,2048]{2,1,0:T(8,128)(2,1)} %copy.159), calls=%async_computation.5 | async-start | bytes 4194304 | tf_op jit(solution)/shard_map/all_to_all | solution.py:211
  297.0 7.7 %copy-start.18 = (bf16[1,704,2048]{2,1,0:T(8,128)(2,1)S(1)}, bf16[1,704,2048]{2,1,0:T(8,128)(2,1)}, u32[]{:S(2)}) copy-start(bf16[1,704,2048]{2,1,0:T(8,128)(2,1)} %param.21) | copy-start | bytes 8650756
  306.3 7.7 %copy-start.20 = (bf16[704,2048]{1,0:T(8,128)(2,1)S(1)}, bf16[704,2048]{1,0:T(8,128)(2,1)}, u32[]{:S(2)}) copy-start(bf16[704,2048]{1,0:T(8,128)(2,1)} %copy-done.19) | copy-start | bytes 8650756
  318.0 32.2 %copy-start.13 = (bf16[2048,16]{0,1:T(8,128)(2,1)S(1)}, bf16[2048,16]{0,1:T(8,128)(2,1)}, u32[]{:S(2)}) copy-start(bf16[2048,16]{0,1:T(8,128)(2,1)} %param.18) | copy-start | bytes 196612
  345.8 53.3 %all-to-all-start.3 = ((bf16[32,14,2048]{2,1,0:T(8,128)(2,1)}), bf16[32,14,2048]{2,1,0:T(8,128)(2,1)}, u32[]{:S(2)}, u32[]{:S(2)}) async-start(bf16[32,14,2048]{2,1,0:T(8,128)(2,1)} %copy.150), calls=%async_computation.3 | async-start | bytes 4194304 | tf_op jit(solution)/shard_map/all_to_all | solution.py:211
  399.1 22.0 %copy-start.16 = (f32[2048]{0:T(1024)S(1)}, f32[2048]{0:T(1024)}, u32[]{:S(2)}) copy-start(f32[2048]{0:T(1024)} %param.22) | copy-start | bytes 24580
  402.7 26.9 %copy-start.5 = (bf16[128,2048]{1,0:T(8,128)(2,1)}, bf16[128,2048]{1,0:T(8,128)(2,1)S(1)}, u32[]{:S(2)}) copy-start(bf16[128,2048]{1,0:T(8,128)(2,1)S(1)} %fusion.27) | copy-start | bytes 1572868
  421.1 18.5 %copy-start.1 = (bf16[2,128,2048]{2,1,0:T(8,128)(2,1)S(1)}, bf16[2,128,2048]{2,1,0:T(8,128)(2,1)}, u32[]{:S(2)}) copy-start(bf16[2,128,2048]{2,1,0:T(8,128)(2,1)} %param.16) | copy-start | bytes 3145732
Sparse Core Ops, SparseCore 0:
  10.7 109.8 all-gather.1

commit v8 on v7

--- a/solution.py
+++ b/solution.py
@@ -193,7 +193,8 @@
         part = jnp.einsum("scf,fd->scd", act, down, preferred_element_type=jnp.float32)
         return part.astype(jnp.bfloat16).astype(jnp.float32)
 
-    cuts = [0, per_dest // 2, per_dest]
+    first_cut = 16 if per_dest > 16 else per_dest // 2
+    cuts = [0, first_cut, per_dest]
     routed = jnp.zeros((tok_rows, model_width), jnp.float32)
     for low, high in zip(cuts[:-1], cuts[1:]):
         outgoing = jnp.einsum(

time: 455 us -> 458 us (level)
  local copies, waits for them, and re-layouts: 24.3 us -> 32.2 us
    all_to_all x2, waiting for transfers between devices: 72 us -> 64.8 us  [per_device(): lax.all_to_all(part_sum.astype(jnp.bfloat16), ('seq', 'exp'), split_axis=...]
    unnamed x49 -> x61, local copies, waits for them, and re-layouts: 10.6 us -> 16.5 us
    dot_general x4, matrix products: 30.5 us -> 25.6 us  [share_part(): jnp.einsum('scd,gfd->scgf', rows, pair, preferred_element_type=jnp.float32)]
where the time goes in v8:
time: 458 us; the launch traced here: 449 us
  waiting for transfers between devices  241 us (53%)
  matrix products  81.6 us (18%)
  starting transfers between devices  34 us (7%)
  local copies, waits for them, and re-layouts  32.2 us (7%)
  blocking collectives  26.8 us (6%)
  other arithmetic  18.9 us (4%)
  between operations  15.1 us (3%)
    all_to_all x1, waiting for transfers between devices, per_device(): lax.all_to_all(jnp.broadcast_to(own_part[None], (seq_count,) + own_part.s...  78 us
    all_to_all x2, waiting for transfers between devices, per_device(): lax.all_to_all(outgoing, ('seq', 'exp'), split_axis=0, concat_axis=0, til...  76.1 us
    all_to_all x2, waiting for transfers between devices, per_device(): lax.all_to_all(part_sum.astype(jnp.bfloat16), ('seq', 'exp'), split_axis=...  64.8 us
    dot_general x4, matrix products, share_part(): jnp.einsum('scd,gfd->scgf', rows, pair, preferred_element_type=jnp.float32)  25.6 us
    unnamed x61, local copies, waits for them, and re-layouts  16.5 us
    all_to_all x1, waiting for transfers between devices, per_device(): lax.all_to_all(heads_flat, 'seq', split_axis=0, concat_axis=1, tiled=True)  11.3 us
    all_to_all x1, blocking collectives, per_device(): lax.all_to_all(jnp.broadcast_to(picked.astype(jnp.bfloat16)[None], (seq_c...  10.6 us
  transfers between devices with their start and end apart: 12, of which 8 were waited for; matrix products, arithmetic and copies ran while one was open for 24% of the time, Pallas kernels for 0%

profile of v8, /device:TPU:0, one launch (start us, length us, event | category | flops | bytes accessed | tf_op | source)
XLA Modules:
  0.0 449.2 jit_solution(15572790358818891264)
XLA Ops:
  8.5 2.0 fusion.65
  10.6 1.6 broadcast_in_dim.70
  12.3 7.4 %all-to-all-start = ((bf16[8,2,32,2048]{3,2,1,0:T(8,128)(2,1)}), bf16[8,2,32,2048]{3,2,1,0:T(8,128)(2,1)S(1)}, u32[]{:S(2)}, u32[]{:S(2)}) async-start(bf16[8,2,32,2048]{3,2,1,0:T(8,128)(2,1)} %broadcast_in_dim.70), calls=%async_computation | async-start | bytes 4194304 | tf_op jit(solution)/shard_map/all_to_all | solution.py:95
  19.9 8.7 %copy.117 = bf16[2048,3,2,128]{0,3,2,1:T(8,128)(2,1)} copy(bf16[2048,3,2,128]{3,2,1,0:T(2,128)(2,1)} %param.15) | data formatting | bytes 6291456 | tf_op args[3]
  31.8 1.8 multiply_cosine_fusion
  33.5 78.0 %all-to-all-done = bf16[8,2,32,2048]{3,2,1,0:T(8,128)(2,1)S(1)} async-done(((bf16[8,2,32,2048]{3,2,1,0:T(8,128)(2,1)}), bf16[8,2,32,2048]{3,2,1,0:T(8,128)(2,1)S(1)}, u32[]{:S(2)}, u32[]{:S(2)}) %all-to-all-start) | async-done | bytes 2097184 | tf_op jit(solution)/shard_map/all_to_all | solution.py:95
  113.1 7.6 %all-gather.2.cloned.1.call-done = bf16[1024,2048]{1,0:T(8,128)(2,1)} async-done(((bf16[128,2048]{1,0:T(8,128)(2,1)}), bf16[1024,2048]{1,0:T(8,128)(2,1)}) %all-gather.2.cloned.1.call-update) | async-done | bytes 4194320 | tf_op jit(solution)/shard_map/all_gather | solution.py:90
  120.6 6.2 %fusion.201 = f32[1024,768]{0,1:S(1)} fusion(bf16[1024,2048]{1,0:T(8,128)(2,1)} %all-gather.2.cloned.1.call-done, bf16[2048,768]{0,1:T(8,128)(2,1)} %bitcast.224), kind=kOutput, calls=%fused_computation.237 | convolution fusion | flops 3221225472 | bytes 10485760
  129.8 1.7 fusion.190
  131.9 3.3 convert.18
  135.3 2.4 fusion.58
  138.8 2.8 fusion.185
  141.6 2.3 fusion.184
  143.9 2.1 fusion.59
  146.1 1.6 fusion.60
  149.4 2.8 collective-permute-done
  153.2 8.0 %all-to-all-start.1 = ((bf16[8,128,256]{1,2,0:T(8,128)(2,1)}), bf16[8,128,256]{1,2,0:T(8,128)(2,1)S(1)}, u32[]{:S(2)}, u32[]{:S(2)}) async-start(bf16[8,128,256]{1,2,0:T(8,128)(2,1)} %copy.127), calls=%async_computation.1 | async-start | bytes 1048576 | tf_op jit(solution)/shard_map/all_to_all | solution.py:148
  161.9 1.7 reduce-window.11
  165.0 11.3 %all-to-all-done.1 = bf16[8,128,256]{1,2,0:T(8,128)(2,1)S(1)} async-done(((bf16[8,128,256]{1,2,0:T(8,128)(2,1)}), bf16[8,128,256]{1,2,0:T(8,128)(2,1)S(1)}, u32[]{:S(2)}, u32[]{:S(2)}) %all-to-all-start.1) | async-done | bytes 524320 | tf_op jit(solution)/shard_map/all_to_all | solution.py:148
  176.8 2.1 convolution_bitcast_fusion.3
  178.9 2.1 convolution_bitcast_fusion.2
  181.0 2.4 multiply_reduce_fusion
  184.2 2.2 copy.144
  186.4 3.6 all-to-all-start.4
  190.1 2.0 convolution_convert_fusion.2
  192.1 46.9 %all-to-all-done.4 = bf16[32,12,2048]{2,1,0:T(8,128)(2,1)} async-done(((bf16[32,12,2048]{2,1,0:T(8,128)(2,1)}), bf16[32,12,2048]{2,1,0:T(8,128)(2,1)}, u32[]{:S(2)}, u32[]{:S(2)}) %all-to-all-start.4) | async-done | bytes 1572896 | tf_op jit(solution)/shard_map/all_to_all | solution.py:206
  238.9 4.2 all-to-all-start.2
  243.5 7.0 %fusion.8 = f32[32,12,2,704]{3,0,2,1:T(8,128)S(1)} fusion(bf16[1,2,704,2048]{3,2,1,0:T(8,128)(2,1)} %param.20, bf16[32,12,2048,1]{2,1,0,3:T(8,128)(2,1)} %bitcast.47), kind=kOutput, calls=%fused_computation.8 | convolution fusion | flops 2214592512 | bytes 9502720 | tf_op jit(solution)/shard_map/scd,gfd->scgf/dot_general | solution.py:191
  252.0 6.9 %fusion.4 = f32[32,12,2,704]{3,0,2,1:T(8,128)S(1)} fusion(bf16[2,704,2048]{2,1,0:T(8,128)(2,1)} %collective-permute-done.3, bf16[32,12,2048,1]{2,1,0,3:T(8,128)(2,1)} %bitcast.47), kind=kOutput, calls=%fused_computation.4 | convolution fusion | flops 2214592512 | bytes 9502720 | tf_op jit(solution)/shard_map/scd,gfd->scgf/dot_general | solution.py:191
  260.5 2.2 copy.148
  262.7 29.3 %all-to-all-done.2 = bf16[32,16,2048]{2,1,0:T(8,128)(2,1)S(1)} async-done(((bf16[32,16,2048]{2,1,0:T(8,128)(2,1)}), bf16[32,16,2048]{2,1,0:T(8,128)(2,1)S(1)}, u32[]{:S(2)}, u32[]{:S(2)}) %all-to-all-start.2) | async-done | bytes 2097184 | tf_op jit(solution)/shard_map/all_to_all | solution.py:206
  293.3 4.2 all-to-all-start.5
  297.5 6.2 %fusion.6 = f32[32,16,2,704]{3,1,2,0:T(8,128)S(1)} fusion(bf16[2,704,2048]{2,1,0:T(8,128)(2,1)} %collective-permute-done.3, bf16[32,16,2048]{2,1,0:T(8,128)(2,1)} %copy-done.8), kind=kOutput, calls=%fused_computation.6 | convolution fusion | flops 2952790016 | bytes 10747904 | tf_op jit(solution)/shard_map/scd,gfd->scgf/dot_general | solution.py:191
  305.3 5.5 %fusion.10 = f32[32,16,2,704]{3,1,2,0:T(8,128)S(1)} fusion(bf16[1,2,704,2048]{3,2,1,0:T(8,128)(2,1)} %param.20, bf16[32,16,2048]{2,1,0:T(8,128)(2,1)S(1)} %copy-done.9), kind=kOutput, calls=%fused_computation.10 | convolution fusion | flops 2952790016 | bytes 10747904 | tf_op jit(solution)/shard_map/scd,gfd->scgf/dot_general | solution.py:191
  312.6 1.8 convolution_convert_fusion.1
  314.5 1.8 add_convert_fusion
  316.3 2.4 copy.140
  318.8 27.6 %all-to-all-done.5 = bf16[32,12,2048]{2,1,0:T(8,128)(2,1)S(1)} async-done(((bf16[32,12,2048]{2,1,0:T(8,128)(2,1)}), bf16[32,12,2048]{2,1,0:T(8,128)(2,1)S(1)}, u32[]{:S(2)}, u32[]{:S(2)}) %all-to-all-start.5) | async-done | bytes 1572896 | tf_op jit(solution)/shard_map/all_to_all | solution.py:212
  347.8 4.3 all-to-all-start.3
  354.6 2.0 copy.134
  356.6 1.8 reshape.441
  359.4 4.4 convolution_bitcast_fusion
  363.8 37.1 %all-to-all-done.3 = bf16[32,16,2048]{2,1,0:T(8,128)(2,1)S(1)} async-done(((bf16[32,16,2048]{2,1,0:T(8,128)(2,1)}), bf16[32,16,2048]{2,1,0:T(8,128)(2,1)S(1)}, u32[]{:S(2)}, u32[]{:S(2)}) %all-to-all-start.3) | async-done | bytes 2097184 | tf_op jit(solution)/shard_map/all_to_all | solution.py:212
  400.9 3.4 fusion.35
  405.4 10.6 %all_to_all.56 = bf16[8,4,2048]{2,1,0:T(4,128)(2,1)S(1)} all-to-all(bf16[8,4,2048]{2,1,0:T(4,128)(2,1)S(1)} %broadcast_in_dim.92), channel_id=1, replica_groups=mesh['seq'=8,'exp'=4] {'seq'}, dimensions={0} | all-to-all | bytes 262144 | tf_op jit(solution)/shard_map/all_to_all | solution.py:228
  416.0 7.2 %all_to_all.57 = bf16[4,4,2048]{2,1,0:T(4,128)(2,1)S(1)} all-to-all(bf16[4,4,2048]{2,1,0:T(4,128)(2,1)S(1)} %broadcast_in_dim.93), channel_id=1, replica_groups=mesh['seq'=8,'exp'=4] {'exp'}, dimensions={0} | all-to-all | bytes 131072 | tf_op jit(solution)/shard_map/all_to_all | solution.py:238
  423.5 8.4 %fusion.200 = (f32[16]{0:T(128)S(1)}, f32[16,3200]{1,0:T(8,128)S(1)}) fusion(bf16[3200,2048]{1,0:T(8,128)(2,1)} %param.23, f32[16,2048]{1,0:T(8,128)S(1)} %reshape.444, f32[2048]{0:T(1024)S(1)} %copy-done.22, f32[16]{0:T(128)S(1)} %rsqrt.30), kind=kOutput, calls=%fused_computation.236 | convolution fusion | flops 209864688 | bytes 13451392 | tf_op jit(solution)/shard_map/dot_general | solution.py:246
  432.2 8.9 %all_to_all.58 = f32[32,2,16]{2,1,0:T(2,128)S(1)} all-to-all(f32[32,2,16]{2,1,0:T(2,128)S(1)} %broadcast_in_dim.94), channel_id=1, replica_groups=mesh['seq'=8,'exp'=4] {'seq','exp'}, dimensions={0} | all-to-all | bytes 8192 | tf_op jit(solution)/shard_map/all_to_all | solution.py:252
  (151 shorter events, 32.0 us)
Async XLA Ops:
  7.2 3.4 copy-start
  7.2 113.4 %all-gather.2.cloned.1.call-start = ((), (), s32[]{:S(2)}) async-start(), calls=%async_computation.9 | async-start | bytes 4718592 | tf_op jit(solution)/shard_map/all_gather | solution.py:90
  12.3 7.4 %copy-start.27 = (s32[1,4]{1,0:T(1,128)S(1)}, s32[1,4]{1,0:T(1,128)}, u32[]{:S(2)}) copy-start(s32[1,4]{1,0:T(1,128)} %param.13) | copy-start | bytes 52
  12.3 99.3 %all-to-all-start = ((bf16[8,2,32,2048]{3,2,1,0:T(8,128)(2,1)}), bf16[8,2,32,2048]{3,2,1,0:T(8,128)(2,1)S(1)}, u32[]{:S(2)}, u32[]{:S(2)}) async-start(bf16[8,2,32,2048]{3,2,1,0:T(8,128)(2,1)} %broadcast_in_dim.70), calls=%async_computation | async-start | bytes 4194304 | tf_op jit(solution)/shard_map/all_to_all | solution.py:95
  111.6 40.6 %collective-permute-start = (bf16[16,32,2048]{2,1,0:T(8,128)(2,1)S(1)}, bf16[16,32,2048]{2,1,0:T(8,128)(2,1)}, u32[]{:S(2)}, u32[]{:S(2)}) collective-permute-start(bf16[16,32,2048]{2,1,0:T(8,128)(2,1)S(1)} %bitcast.221), channel_id=1, source_target_pairs={{0,2},{1,3},{2,0},{3,1},{4,6},{5,7},{6,4},{7,5},{8,10},{9,11},{10,... | collective-permute-start | bytes 6291464 | tf_op jit(solution)/shard_map/ppermute | solution.py:107
  113.1 63.7 %collective-permute-start.1 = (bf16[16,32,2048]{2,1,0:T(8,128)(2,1)S(1)}, bf16[16,32,2048]{2,1,0:T(8,128)(2,1)}, u32[]{:S(2)}, u32[]{:S(2)}) collective-permute-start(bf16[16,32,2048]{2,1,0:T(8,128)(2,1)S(1)} %bitcast.222), channel_id=1, source_target_pairs={{0,1},{1,0},{2,3},{3,2},{4,5},{5,4},{6,7},{7,6},{8,9},{9,8},{10,11... | collective-permute-start | bytes 6291464 | tf_op jit(solution)/shard_map/ppermute | solution.py:52
  126.8 1.7 copy-start.2
  126.8 1.7 copy-start.13
  126.8 1.7 copy-start.14
  129.8 1.7 copy-start.10
  129.8 1.7 copy-start.11
  129.8 1.7 copy-start.12
  138.8 2.9 copy-start.17
  143.9 2.2 copy-start.28
  147.7 1.6 copy-start.18
  149.3 12.2 %copy-start.20 = (s32[1,128,6]{1,0,2:T(1,128)S(1)}, s32[1,128,6]{1,0,2:T(1,128)}, u32[]{:S(2)}) copy-start(s32[1,128,6]{1,0,2:T(1,128)} %param.19) | copy-start | bytes 9220
  152.2 26.7 %collective-permute-start.2 = (bf16[16,32,2048]{2,1,0:T(8,128)(2,1)}, bf16[16,32,2048]{2,1,0:T(8,128)(2,1)}, u32[]{:S(2)}, u32[]{:S(2)}) collective-permute-start(bf16[16,32,2048]{2,1,0:T(8,128)(2,1)} %collective-permute-done), channel_id=1, source_target_pairs={{0,1},{1,0},{2,3},{3,2},{4,5},{5,4},{6,7},{7,6},{8,9},{9,8},{10,11... | collective-permute-start | bytes 6291464 | tf_op jit(solution)/shard_map/ppermute | solution.py:52
  153.2 23.1 %all-to-all-start.1 = ((bf16[8,128,256]{1,2,0:T(8,128)(2,1)}), bf16[8,128,256]{1,2,0:T(8,128)(2,1)S(1)}, u32[]{:S(2)}, u32[]{:S(2)}) async-start(bf16[8,128,256]{1,2,0:T(8,128)(2,1)} %copy.127), calls=%async_computation.1 | async-start | bytes 1048576 | tf_op jit(solution)/shard_map/all_to_all | solution.py:148
  161.2 90.8 %collective-permute-start.3 = (bf16[2,704,2048]{2,1,0:T(8,128)(2,1)}, bf16[2,704,2048]{2,1,0:T(8,128)(2,1)}, u32[]{:S(2)}, u32[]{:S(2)}) collective-permute-start(bf16[2,704,2048]{2,1,0:T(8,128)(2,1)} %bitcast.242), channel_id=1, source_target_pairs={{0,1},{1,0},{2,3},{3,2},{4,5},{5,4},{6,7},{7,6},{8,9},{9,8},{10,11... | collective-permute-start | bytes 17301512 | tf_op jit(solution)/shard_map/ppermute | solution.py:52
  165.0 13.9 %copy-start.15 = (pred[128,32,28]{0,2,1:T(8,128)(4,1)}, pred[128,32,28]{0,2,1:T(8,128)(4,1)S(1)}, u32[]{:S(2)}) copy-start(pred[128,32,28]{0,2,1:T(8,128)(4,1)S(1)} %reshape.442) | copy-start | bytes 344068
  176.3 2.6 copy-start.6
  178.9 2.2 copy-start.5
  181.0 2.4 copy-start.21
  181.0 2.6 slice-start.1
  183.6 6.4 %copy-start.3 = (bf16[128,2048]{1,0:T(8,128)(2,1)}, bf16[128,2048]{1,0:T(8,128)(2,1)S(1)}, u32[]{:S(2)}) copy-start(bf16[128,2048]{1,0:T(8,128)(2,1)S(1)} %multiply_convert_fusion) | copy-start | bytes 1572868
  186.4 3.7 copy-start.16
  186.4 52.5 %all-to-all-start.4 = ((bf16[32,12,2048]{2,1,0:T(8,128)(2,1)}), bf16[32,12,2048]{2,1,0:T(8,128)(2,1)}, u32[]{:S(2)}, u32[]{:S(2)}) async-start(bf16[32,12,2048]{2,1,0:T(8,128)(2,1)} %copy.144), calls=%async_computation.4 | async-start | bytes 4194304 | tf_op jit(solution)/shard_map/all_to_all | solution.py:206
  238.9 53.1 %all-to-all-start.2 = ((bf16[32,16,2048]{2,1,0:T(8,128)(2,1)}), bf16[32,16,2048]{2,1,0:T(8,128)(2,1)S(1)}, u32[]{:S(2)}, u32[]{:S(2)}) async-start(bf16[32,16,2048]{2,1,0:T(8,128)(2,1)} %convolution_convert_fusion.2), calls=%async_computation.2 | async-start | bytes 4194304 | tf_op jit(solution)/shard_map/all_to_all | solution.py:206
  243.1 15.8 %collective-permute-start.4 = (bf16[704,2048]{1,0:T(8,128)(2,1)}, bf16[704,2048]{1,0:T(8,128)(2,1)S(1)}, u32[]{:S(2)}, u32[]{:S(2)}) collective-permute-start(bf16[704,2048]{1,0:T(8,128)(2,1)} %bitcast.243), channel_id=1, source_target_pairs={{0,1},{1,0},{2,3},{3,2},{4,5},{5,4},{6,7},{7,6},{8,9},{9,8},{10,11... | collective-permute-start | bytes 8650760 | tf_op jit(solution)/shard_map/ppermute | solution.py:52
  243.5 7.0 %copy-start.23 = (bf16[1,704,2048]{2,1,0:T(8,128)(2,1)S(1)}, bf16[1,704,2048]{2,1,0:T(8,128)(2,1)}, u32[]{:S(2)}) copy-start(bf16[1,704,2048]{2,1,0:T(8,128)(2,1)} %param.21) | copy-start | bytes 8650756
  258.9 1.6 copy-start.25
  292.0 1.3 copy-start.8
  293.3 53.1 %all-to-all-start.5 = ((bf16[32,12,2048]{2,1,0:T(8,128)(2,1)}), bf16[32,12,2048]{2,1,0:T(8,128)(2,1)S(1)}, u32[]{:S(2)}, u32[]{:S(2)}) async-start(bf16[32,12,2048]{2,1,0:T(8,128)(2,1)} %copy.148), calls=%async_computation.5 | async-start | bytes 4194304 | tf_op jit(solution)/shard_map/all_to_all | solution.py:212
  303.7 1.6 copy-start.9
  310.8 1.8 copy-start.24
  312.6 1.8 copy-start.26
  318.8 33.3 %copy-start.19 = (bf16[2048,16]{0,1:T(8,128)(2,1)S(1)}, bf16[2048,16]{0,1:T(8,128)(2,1)}, u32[]{:S(2)}) copy-start(bf16[2048,16]{0,1:T(8,128)(2,1)} %param.18) | copy-start | bytes 196612
  346.4 1.4 copy-start.4
  347.8 53.2 %all-to-all-start.3 = ((bf16[32,16,2048]{2,1,0:T(8,128)(2,1)}), bf16[32,16,2048]{2,1,0:T(8,128)(2,1)S(1)}, u32[]{:S(2)}, u32[]{:S(2)}) async-start(bf16[32,16,2048]{2,1,0:T(8,128)(2,1)} %copy.140), calls=%async_computation.3 | async-start | bytes 4194304 | tf_op jit(solution)/shard_map/all_to_all | solution.py:212
  358.4 42.5 %slice-start = ((f32[128,32,28]{0,2,1:T(8,128)}), f32[128,32,16]{0,2,1:T(8,128)S(1)}, s32[]{:S(2)}) async-start(f32[128,32,28]{0,2,1:T(8,128)} %reshape.441), calls=%async_computation.10 | async-start | bytes 524288 | tf_op jit(solution)/shard_map/slice | solution.py:217
  363.8 59.7 %copy-start.22 = (f32[2048]{0:T(1024)S(1)}, f32[2048]{0:T(1024)}, u32[]{:S(2)}) copy-start(f32[2048]{0:T(1024)} %param.22) | copy-start | bytes 24580
  404.3 0.8 copy-start.7
  423.5 18.5 %copy-start.1 = (bf16[2,128,2048]{2,1,0:T(8,128)(2,1)S(1)}, bf16[2,128,2048]{2,1,0:T(8,128)(2,1)}, u32[]{:S(2)}) copy-start(bf16[2,128,2048]{2,1,0:T(8,128)(2,1)} %param.16) | copy-start | bytes 3145732
Sparse Core Ops, SparseCore 0:
  10.7 109.8 all-gather.1

commit v9 on v7

--- a/solution.py
+++ b/solution.py
@@ -88,6 +88,13 @@
     segment, offset = segment_layout(prompt_lengths, group_tokens)
     normed = rms_scale(token_rows, attn_gain).astype(jnp.bfloat16)
     group_normed = lax.all_gather(normed, "seq", axis=0, tiled=True)
+    gate_up = w_gate_up[0]
+    down_weight = w_down[0]
+    other_gate_up = pair_swap(gate_up)
+    other_down = pair_swap(down_weight)
+    other_gate_up, other_down, group_normed = lax.optimization_barrier(
+        (other_gate_up, other_down, group_normed)
+    )
     part_size = head_size // group_count
     own_part = lax.dynamic_slice_in_dim(
         w_out, lax.axis_index("exp") * part_size, part_size, axis=1
@@ -182,10 +189,6 @@
     dispatch_table = dispatch_table.reshape(tok_rows, device_count, per_dest)
     slot_weights = jnp.sum(jnp.where(placed, gates[:, :, None], 0.0), axis=1)
     slot_weights = slot_weights.reshape(tok_rows, device_count, per_dest)
-    gate_up = w_gate_up[0]
-    down_weight = w_down[0]
-    other_gate_up = pair_swap(gate_up)
-    other_down = pair_swap(down_weight)
 
     def share_part(rows, pair, down):
         both = jnp.einsum("scd,gfd->scgf", rows, pair, preferred_element_type=jnp.float32)

time: 455 us -> 455 us (level)
    unnamed x49 -> x45, local copies, waits for them, and re-layouts: 10.6 us -> 10.6 us
  transfers between devices with their start and end apart: 12 -> 12, of which waited for: 8 -> 8; matrix products, arithmetic and copies ran while one was open for 24% -> 23% of each run, Pallas kernels for 0% -> 0%
where the time goes in v9:
time: 455 us; the launch traced here: 446 us
  waiting for transfers between devices  245 us (54%)
  matrix products  87.1 us (19%)
  starting transfers between devices  30.6 us (7%)
  blocking collectives  26.8 us (6%)
  local copies, waits for them, and re-layouts  24.3 us (5%)
  other arithmetic  17.2 us (4%)
  between operations  15.1 us (3%)
    all_to_all x1, waiting for transfers between devices, per_device(): lax.all_to_all(jnp.broadcast_to(own_part[None], (seq_count,) + own_part.s...  76 us
    all_to_all x2, waiting for transfers between devices, per_device(): lax.all_to_all(outgoing, ('seq', 'exp'), split_axis=0, concat_axis=0, til...  72 us
    all_to_all x2, waiting for transfers between devices, per_device(): lax.all_to_all(part_sum.astype(jnp.bfloat16), ('seq', 'exp'), split_axis=...  70.4 us
    dot_general x4, matrix products, share_part(): jnp.einsum('scd,gfd->scgf', rows, pair, preferred_element_type=jnp.float32)  30.3 us
    all_to_all x1, waiting for transfers between devices, per_device(): lax.all_to_all(heads_flat, 'seq', split_axis=0, concat_axis=1, tiled=True)  11.7 us
    unnamed x45, local copies, waits for them, and re-layouts  10.6 us
    all_to_all x1, blocking collectives, per_device(): lax.all_to_all(jnp.broadcast_to(picked.astype(jnp.bfloat16)[None], (seq_c...  10.6 us
    dot_general x4, matrix products, share_part(): jnp.einsum('scf,fd->scd', act, down, preferred_element_type=jnp.float32)  10.3 us
  transfers between devices with their start and end apart: 12, of which 8 were waited for; matrix products, arithmetic and copies ran while one was open for 23% of the time, Pallas kernels for 0%

profile of v9, /device:TPU:0, one launch (start us, length us, event | category | flops | bytes accessed | tf_op | source)
XLA Modules:
  0.0 446.2 jit_solution(3004119255045885575)
XLA Ops:
  8.5 2.0 fusion.58
  11.1 1.6 broadcast_in_dim.70
  12.7 7.0 %all-to-all-start = ((bf16[8,2,32,2048]{3,2,1,0:T(8,128)(2,1)}), bf16[8,2,32,2048]{3,2,1,0:T(8,128)(2,1)S(1)}, u32[]{:S(2)}, u32[]{:S(2)}) async-start(bf16[8,2,32,2048]{3,2,1,0:T(8,128)(2,1)} %broadcast_in_dim.70), calls=%async_computation | async-start | bytes 4194304 | tf_op jit(solution)/shard_map/all_to_all | solution.py:102
  20.1 8.8 %copy.125 = bf16[2048,3,2,128]{0,3,2,1:T(8,128)(2,1)} copy(bf16[2048,3,2,128]{3,2,1,0:T(2,128)(2,1)} %param.15) | data formatting | bytes 6291456 | tf_op args[3]
  32.0 1.8 multiply_cosine_fusion
  33.8 76.0 %all-to-all-done = bf16[8,2,32,2048]{3,2,1,0:T(8,128)(2,1)S(1)} async-done(((bf16[8,2,32,2048]{3,2,1,0:T(8,128)(2,1)}), bf16[8,2,32,2048]{3,2,1,0:T(8,128)(2,1)S(1)}, u32[]{:S(2)}, u32[]{:S(2)}) %all-to-all-start) | async-done | bytes 2097184 | tf_op jit(solution)/shard_map/all_to_all | solution.py:102
  111.3 9.9 %all-gather.2.cloned.1.call-done = bf16[1024,2048]{1,0:T(8,128)(2,1)} async-done(((bf16[128,2048]{1,0:T(8,128)(2,1)}), bf16[1024,2048]{1,0:T(8,128)(2,1)}) %all-gather.2.cloned.1.call-update) | async-done | bytes 4194320 | tf_op jit(solution)/shard_map/all_gather | solution.py:90
  121.3 6.2 %fusion.199 = f32[1024,768]{0,1:S(1)} fusion(bf16[1024,2048]{1,0:T(8,128)(2,1)} %all-gather.2.cloned.1.call-done, bf16[2048,768]{0,1:T(8,128)(2,1)} %bitcast.220), kind=kOutput, calls=%fused_computation.239 | convolution fusion | flops 3221225472 | bytes 10485760
  130.5 1.7 fusion.188
  132.6 3.3 convert.18
  135.9 2.4 fusion.53
  139.4 2.9 fusion.183
  142.3 2.2 fusion.182
  144.5 2.1 fusion.54
  146.7 1.6 fusion.55
  150.0 5.1 %collective-permute-done = bf16[16,32,2048]{2,1,0:T(8,128)(2,1)} collective-permute-done((bf16[16,32,2048]{2,1,0:T(8,128)(2,1)S(1)}, bf16[16,32,2048]{2,1,0:T(8,128)(2,1)}, u32[]{:S(2)}, u32[]{:S(2)}) %collective-permute-start) | collective-permute-done | bytes 2097184 | tf_op jit(solution)/shard_map/ppermute | solution.py:114
  156.4 4.4 all-to-all-start.1
  161.0 1.7 reduce-window.11
  164.2 11.7 %all-to-all-done.1 = bf16[8,128,256]{1,2,0:T(8,128)(2,1)S(1)} async-done(((bf16[8,128,256]{1,2,0:T(8,128)(2,1)}), bf16[8,128,256]{1,2,0:T(8,128)(2,1)S(1)}, u32[]{:S(2)}, u32[]{:S(2)}) %all-to-all-start.1) | async-done | bytes 524320 | tf_op jit(solution)/shard_map/all_to_all | solution.py:155
  176.4 2.1 convolution_bitcast_fusion.3
  178.5 2.1 convolution_bitcast_fusion.2
  180.6 2.4 multiply_reduce_fusion
  183.8 2.3 copy.154
  186.2 3.8 all-to-all-start.4
  190.6 2.3 copy.146
  193.0 45.9 %all-to-all-done.4 = bf16[32,14,2048]{2,1,0:T(8,128)(2,1)} async-done(((bf16[32,14,2048]{2,1,0:T(8,128)(2,1)}), bf16[32,14,2048]{2,1,0:T(8,128)(2,1)}, u32[]{:S(2)}, u32[]{:S(2)}) %all-to-all-start.4) | async-done | bytes 1835040 | tf_op jit(solution)/shard_map/all_to_all | solution.py:208
  238.9 4.3 all-to-all-start.2
  243.2 7.7 %fusion.8 = f32[32,14,2,704]{3,0,2,1:T(8,128)S(1)} fusion(bf16[1,2,704,2048]{3,2,1,0:T(8,128)(2,1)} %param.20, bf16[32,14,2048,1]{2,1,0,3:T(8,128)(2,1)} %bitcast.46), kind=kOutput, calls=%fused_computation.8 | convolution fusion | flops 2583691264 | bytes 10125312 | tf_op jit(solution)/shard_map/scd,gfd->scgf/dot_general | solution.py:194
  250.9 1.6 convolution_convert_fusion.1
  252.5 7.5 %fusion.4 = f32[32,14,2,704]{3,0,1,2:T(8,128)S(1)} fusion(bf16[2,704,2048]{2,1,0:T(8,128)(2,1)} %collective-permute-done.1, bf16[32,14,2048]{2,1,0:T(8,128)(2,1)} %all-to-all-done.4), kind=kOutput, calls=%fused_computation.4 | convolution fusion | flops 2583691264 | bytes 10125312 | tf_op jit(solution)/shard_map/scd,gfd->scgf/dot_general | solution.py:194
  260.0 3.5 add_convert_fusion
  263.5 2.4 copy.159
  265.9 26.1 %all-to-all-done.2 = bf16[32,14,2048]{2,1,0:T(8,128)(2,1)} async-done(((bf16[32,14,2048]{2,1,0:T(8,128)(2,1)}), bf16[32,14,2048]{2,1,0:T(8,128)(2,1)}, u32[]{:S(2)}, u32[]{:S(2)}) %all-to-all-start.2) | async-done | bytes 1835040 | tf_op jit(solution)/shard_map/all_to_all | solution.py:208
  292.0 4.4 all-to-all-start.5
  296.4 7.7 %fusion.10 = f32[32,14,2,704]{3,0,2,1:T(8,128)S(1)} fusion(bf16[1,2,704,2048]{3,2,1,0:T(8,128)(2,1)} %param.20, bf16[32,14,2048,1]{2,1,0,3:T(8,128)(2,1)} %bitcast.36), kind=kOutput, calls=%fused_computation.10 | convolution fusion | flops 2583691264 | bytes 10125312 | tf_op jit(solution)/shard_map/scd,gfd->scgf/dot_general | solution.py:194
  304.1 1.6 convolution_convert_fusion.4
  305.7 7.5 %fusion.6 = f32[32,14,2,704]{3,0,2,1:T(8,128)S(1)} fusion(bf16[2,704,2048]{2,1,0:T(8,128)(2,1)} %collective-permute-done.1, bf16[32,14,2048,1]{2,1,0,3:T(8,128)(2,1)} %bitcast.36), kind=kOutput, calls=%fused_computation.6 | convolution fusion | flops 2583691264 | bytes 10125312 | tf_op jit(solution)/shard_map/scd,gfd->scgf/dot_general | solution.py:194
  313.3 3.5 add_convert_fusion.1
  316.8 2.4 copy.150
  319.1 26.1 %all-to-all-done.5 = bf16[32,14,2048]{2,1,0:T(8,128)(2,1)} async-done(((bf16[32,14,2048]{2,1,0:T(8,128)(2,1)}), bf16[32,14,2048]{2,1,0:T(8,128)(2,1)}, u32[]{:S(2)}, u32[]{:S(2)}) %all-to-all-start.5) | async-done | bytes 1835040 | tf_op jit(solution)/shard_map/all_to_all | solution.py:214
  345.3 4.4 all-to-all-start.3
  350.7 3.6 convolution_bitcast_fusion
  354.3 44.3 %all-to-all-done.3 = bf16[32,14,2048]{2,1,0:T(8,128)(2,1)} async-done(((bf16[32,14,2048]{2,1,0:T(8,128)(2,1)}), bf16[32,14,2048]{2,1,0:T(8,128)(2,1)}, u32[]{:S(2)}, u32[]{:S(2)}) %all-to-all-start.3) | async-done | bytes 1835040 | tf_op jit(solution)/shard_map/all_to_all | solution.py:214
  398.5 3.6 fusion.27
  402.4 10.6 %all_to_all.56 = bf16[8,4,2048]{2,1,0:T(4,128)(2,1)S(1)} all-to-all(bf16[8,4,2048]{2,1,0:T(4,128)(2,1)S(1)} %broadcast_in_dim.92), channel_id=1, replica_groups=mesh['seq'=8,'exp'=4] {'seq'}, dimensions={0} | all-to-all | bytes 262144 | tf_op jit(solution)/shard_map/all_to_all | solution.py:230
  413.1 7.2 %all_to_all.57 = bf16[4,4,2048]{2,1,0:T(4,128)(2,1)S(1)} all-to-all(bf16[4,4,2048]{2,1,0:T(4,128)(2,1)S(1)} %broadcast_in_dim.93), channel_id=1, replica_groups=mesh['seq'=8,'exp'=4] {'exp'}, dimensions={0} | all-to-all | bytes 131072 | tf_op jit(solution)/shard_map/all_to_all | solution.py:240
  420.6 8.4 %fusion.198 = (f32[16]{0:T(128)S(1)}, f32[16,3200]{1,0:T(8,128)S(1)}) fusion(bf16[3200,2048]{1,0:T(8,128)(2,1)} %param.23, f32[16,2048]{1,0:T(8,128)S(1)} %reshape.444, f32[2048]{0:T(1024)S(1)} %copy-done.16, f32[16]{0:T(128)S(1)} %rsqrt.30), kind=kOutput, calls=%fused_computation.238 | convolution fusion | flops 209864688 | bytes 13451392 | tf_op jit(solution)/shard_map/dot_general | solution.py:248
  429.3 8.9 %all_to_all.58 = f32[32,2,16]{2,1,0:T(2,128)S(1)} all-to-all(f32[32,2,16]{2,1,0:T(2,128)S(1)} %broadcast_in_dim.94), channel_id=1, replica_groups=mesh['seq'=8,'exp'=4] {'seq','exp'}, dimensions={0} | all-to-all | bytes 8192 | tf_op jit(solution)/shard_map/all_to_all | solution.py:254
  (131 shorter events, 20.4 us)
Async XLA Ops:
  7.2 4.0 copy-start
  7.2 114.1 %all-gather.2.cloned.1.call-start = ((), (), s32[]{:S(2)}) async-start(), calls=%async_computation.9 | async-start | bytes 4718592 | tf_op jit(solution)/shard_map/all_gather | solution.py:90
  10.6 100.7 %collective-permute-start.1 = (bf16[2,704,2048]{2,1,0:T(8,128)(2,1)}, bf16[2,704,2048]{2,1,0:T(8,128)(2,1)}, u32[]{:S(2)}, u32[]{:S(2)}) collective-permute-start(bf16[2,704,2048]{2,1,0:T(8,128)(2,1)} %bitcast.238), channel_id=1, source_target_pairs={{0,1},{1,0},{2,3},{3,2},{4,5},{5,4},{6,7},{7,6},{8,9},{9,8},{10,11... | collective-permute-start | bytes 17301512 | tf_op jit(solution)/shard_map/ppermute | solution.py:52
  12.7 7.2 %copy-start.19 = (s32[1,4]{1,0:T(1,128)S(1)}, s32[1,4]{1,0:T(1,128)}, u32[]{:S(2)}) copy-start(s32[1,4]{1,0:T(1,128)} %param.13) | copy-start | bytes 52
  12.7 97.1 %all-to-all-start = ((bf16[8,2,32,2048]{3,2,1,0:T(8,128)(2,1)}), bf16[8,2,32,2048]{3,2,1,0:T(8,128)(2,1)S(1)}, u32[]{:S(2)}, u32[]{:S(2)}) async-start(bf16[8,2,32,2048]{3,2,1,0:T(8,128)(2,1)} %broadcast_in_dim.70), calls=%async_computation | async-start | bytes 4194304 | tf_op jit(solution)/shard_map/all_to_all | solution.py:102
  19.7 91.6 %collective-permute-start.2 = (bf16[704,2048]{1,0:T(8,128)(2,1)}, bf16[704,2048]{1,0:T(8,128)(2,1)}, u32[]{:S(2)}, u32[]{:S(2)}) collective-permute-start(bf16[704,2048]{1,0:T(8,128)(2,1)} %bitcast.239), channel_id=1, source_target_pairs={{0,1},{1,0},{2,3},{3,2},{4,5},{5,4},{6,7},{7,6},{8,9},{9,8},{10,11... | collective-permute-start | bytes 8650760 | tf_op jit(solution)/shard_map/ppermute | solution.py:52
  109.8 45.3 %collective-permute-start = (bf16[16,32,2048]{2,1,0:T(8,128)(2,1)S(1)}, bf16[16,32,2048]{2,1,0:T(8,128)(2,1)}, u32[]{:S(2)}, u32[]{:S(2)}) collective-permute-start(bf16[16,32,2048]{2,1,0:T(8,128)(2,1)S(1)} %bitcast.217), channel_id=1, source_target_pairs={{0,2},{1,3},{2,0},{3,1},{4,6},{5,7},{6,4},{7,5},{8,10},{9,11},{10,... | collective-permute-start | bytes 6291464 | tf_op jit(solution)/shard_map/ppermute | solution.py:114
  111.3 65.1 %collective-permute-start.3 = (bf16[16,32,2048]{2,1,0:T(8,128)(2,1)S(1)}, bf16[16,32,2048]{2,1,0:T(8,128)(2,1)}, u32[]{:S(2)}, u32[]{:S(2)}) collective-permute-start(bf16[16,32,2048]{2,1,0:T(8,128)(2,1)S(1)} %bitcast.218), channel_id=1, source_target_pairs={{0,1},{1,0},{2,3},{3,2},{4,5},{5,4},{6,7},{7,6},{8,9},{9,8},{10,11... | collective-permute-start | bytes 6291464 | tf_op jit(solution)/shard_map/ppermute | solution.py:52
  127.5 1.7 copy-start.2
  127.5 1.7 copy-start.9
  127.5 1.7 copy-start.10
  130.5 1.7 copy-start.6
  130.5 1.7 copy-start.7
  130.5 1.7 copy-start.8
  139.4 2.9 copy-start.11
  144.5 2.2 copy-start.20
  148.3 1.6 copy-start.12
  148.3 6.8 %copy-start.14 = (s32[1,128,6]{1,0,2:T(1,128)S(1)}, s32[1,128,6]{1,0,2:T(1,128)}, u32[]{:S(2)}) copy-start(s32[1,128,6]{1,0,2:T(1,128)} %param.19) | copy-start | bytes 9220
  155.1 23.3 %collective-permute-start.4 = (bf16[16,32,2048]{2,1,0:T(8,128)(2,1)}, bf16[16,32,2048]{2,1,0:T(8,128)(2,1)}, u32[]{:S(2)}, u32[]{:S(2)}) collective-permute-start(bf16[16,32,2048]{2,1,0:T(8,128)(2,1)} %collective-permute-done), channel_id=1, source_target_pairs={{0,1},{1,0},{2,3},{3,2},{4,5},{5,4},{6,7},{7,6},{8,9},{9,8},{10,11... | collective-permute-start | bytes 6291464 | tf_op jit(solution)/shard_map/ppermute | solution.py:52
  156.4 19.5 %all-to-all-start.1 = ((bf16[8,128,256]{1,2,0:T(8,128)(2,1)}), bf16[8,128,256]{1,2,0:T(8,128)(2,1)S(1)}, u32[]{:S(2)}, u32[]{:S(2)}) async-start(bf16[8,128,256]{1,2,0:T(8,128)(2,1)} %copy.135), calls=%async_computation.1 | async-start | bytes 1048576 | tf_op jit(solution)/shard_map/all_to_all | solution.py:155
  175.9 2.6 copy-start.4
  178.5 2.2 copy-start.3
  180.6 2.4 copy-start.15
  186.2 52.7 %all-to-all-start.4 = ((bf16[32,14,2048]{2,1,0:T(8,128)(2,1)}), bf16[32,14,2048]{2,1,0:T(8,128)(2,1)}, u32[]{:S(2)}, u32[]{:S(2)}) async-start(bf16[32,14,2048]{2,1,0:T(8,128)(2,1)} %copy.154), calls=%async_computation.4 | async-start | bytes 4194304 | tf_op jit(solution)/shard_map/all_to_all | solution.py:208
  238.9 53.2 %all-to-all-start.2 = ((bf16[32,14,2048]{2,1,0:T(8,128)(2,1)}), bf16[32,14,2048]{2,1,0:T(8,128)(2,1)}, u32[]{:S(2)}, u32[]{:S(2)}) async-start(bf16[32,14,2048]{2,1,0:T(8,128)(2,1)} %copy.146), calls=%async_computation.2 | async-start | bytes 4194304 | tf_op jit(solution)/shard_map/all_to_all | solution.py:208
  243.2 7.7 %copy-start.17 = (bf16[1,704,2048]{2,1,0:T(8,128)(2,1)S(1)}, bf16[1,704,2048]{2,1,0:T(8,128)(2,1)}, u32[]{:S(2)}) copy-start(bf16[1,704,2048]{2,1,0:T(8,128)(2,1)} %param.21) | copy-start | bytes 8650756
  292.0 53.2 %all-to-all-start.5 = ((bf16[32,14,2048]{2,1,0:T(8,128)(2,1)}), bf16[32,14,2048]{2,1,0:T(8,128)(2,1)}, u32[]{:S(2)}, u32[]{:S(2)}) async-start(bf16[32,14,2048]{2,1,0:T(8,128)(2,1)} %copy.159), calls=%async_computation.5 | async-start | bytes 4194304 | tf_op jit(solution)/shard_map/all_to_all | solution.py:214
  296.4 7.7 %copy-start.18 = (bf16[1,704,2048]{2,1,0:T(8,128)(2,1)S(1)}, bf16[1,704,2048]{2,1,0:T(8,128)(2,1)}, u32[]{:S(2)}) copy-start(bf16[1,704,2048]{2,1,0:T(8,128)(2,1)} %param.21) | copy-start | bytes 8650756
  319.1 30.6 %copy-start.13 = (bf16[2048,16]{0,1:T(8,128)(2,1)S(1)}, bf16[2048,16]{0,1:T(8,128)(2,1)}, u32[]{:S(2)}) copy-start(bf16[2048,16]{0,1:T(8,128)(2,1)} %param.18) | copy-start | bytes 196612
  345.3 53.3 %all-to-all-start.3 = ((bf16[32,14,2048]{2,1,0:T(8,128)(2,1)}), bf16[32,14,2048]{2,1,0:T(8,128)(2,1)}, u32[]{:S(2)}, u32[]{:S(2)}) async-start(bf16[32,14,2048]{2,1,0:T(8,128)(2,1)} %copy.150), calls=%async_computation.3 | async-start | bytes 4194304 | tf_op jit(solution)/shard_map/all_to_all | solution.py:214
  398.5 22.0 %copy-start.16 = (f32[2048]{0:T(1024)S(1)}, f32[2048]{0:T(1024)}, u32[]{:S(2)}) copy-start(f32[2048]{0:T(1024)} %param.22) | copy-start | bytes 24580
  402.1 26.9 %copy-start.5 = (bf16[128,2048]{1,0:T(8,128)(2,1)}, bf16[128,2048]{1,0:T(8,128)(2,1)S(1)}, u32[]{:S(2)}) copy-start(bf16[128,2048]{1,0:T(8,128)(2,1)S(1)} %fusion.27) | copy-start | bytes 1572868
  420.6 18.5 %copy-start.1 = (bf16[2,128,2048]{2,1,0:T(8,128)(2,1)S(1)}, bf16[2,128,2048]{2,1,0:T(8,128)(2,1)}, u32[]{:S(2)}) copy-start(bf16[2,128,2048]{2,1,0:T(8,128)(2,1)} %param.16) | copy-start | bytes 3145732
Sparse Core Ops, SparseCore 0:
  10.7 110.5 all-gather.1

commit v10 on v9

--- a/solution.py
+++ b/solution.py
@@ -150,9 +150,9 @@
         ).astype(jnp.bfloat16)
 
     blocks = jnp.concatenate([one_block(index) for index in range(block_count)], axis=0)
-    x_pieces, blocks = lax.optimization_barrier((x_pieces, blocks))
     heads_flat = blocks.reshape(group_tokens, head_count * head_size)
     regrouped = lax.all_to_all(heads_flat, "seq", split_axis=0, concat_axis=1, tiled=True)
+    x_pieces, regrouped = lax.optimization_barrier((x_pieces, regrouped))
     pieces, owners = [seq_part[0]] + x_pieces, [exp_index] + x_owners
     pieces = pieces + [pair_swap(piece) for piece in pieces]
     owners = owners + [owner ^ 1 for owner in owners]

time: 455 us -> 449 us (0.987)
    unnamed x45 -> x51, local copies, waits for them, and re-layouts: 10.6 us -> 9.97 us
where the time goes in v10:
time: 449 us; the launch traced here: 440 us
  waiting for transfers between devices  243 us (54%)
  matrix products  87.2 us (19%)
  starting transfers between devices  30.4 us (7%)
  blocking collectives  26.8 us (6%)
  local copies, waits for them, and re-layouts  23.6 us (5%)
  between operations  15.1 us (3%)
  other arithmetic  14.4 us (3%)
    all_to_all x1, waiting for transfers between devices, per_device(): lax.all_to_all(jnp.broadcast_to(own_part[None], (seq_count,) + own_part.s...  76 us
    all_to_all x2, waiting for transfers between devices, per_device(): lax.all_to_all(outgoing, ('seq', 'exp'), split_axis=0, concat_axis=0, til...  72 us
    all_to_all x2, waiting for transfers between devices, per_device(): lax.all_to_all(part_sum.astype(jnp.bfloat16), ('seq', 'exp'), split_axis=...  70.4 us
    dot_general x4, matrix products, share_part(): jnp.einsum('scd,gfd->scgf', rows, pair, preferred_element_type=jnp.float32)  30.3 us
    all_to_all x1, waiting for transfers between devices, per_device(): lax.all_to_all(heads_flat, 'seq', split_axis=0, concat_axis=1, tiled=True)  11.3 us
    all_to_all x1, blocking collectives, per_device(): lax.all_to_all(jnp.broadcast_to(picked.astype(jnp.bfloat16)[None], (seq_c...  10.6 us
    dot_general x4, matrix products, share_part(): jnp.einsum('scf,fd->scd', act, down, preferred_element_type=jnp.float32)  10.3 us
    unnamed x51, local copies, waits for them, and re-layouts  9.97 us
  transfers between devices with their start and end apart: 12, of which 8 were waited for; matrix products, arithmetic and copies ran while one was open for 23% of the time, Pallas kernels for 0%

profile of v10, /device:TPU:0, one launch (start us, length us, event | category | flops | bytes accessed | tf_op | source)
XLA Modules:
  0.0 440.5 jit_solution(16440977384542799258)
XLA Ops:
  8.5 2.0 fusion.58
  11.1 1.6 broadcast_in_dim.70
  12.7 7.0 %all-to-all-start = ((bf16[8,2,32,2048]{3,2,1,0:T(8,128)(2,1)}), bf16[8,2,32,2048]{3,2,1,0:T(8,128)(2,1)S(1)}, u32[]{:S(2)}, u32[]{:S(2)}) async-start(bf16[8,2,32,2048]{3,2,1,0:T(8,128)(2,1)} %broadcast_in_dim.70), calls=%async_computation | async-start | bytes 4194304 | tf_op jit(solution)/shard_map/all_to_all | solution.py:102
  20.1 8.8 %copy.125 = bf16[2048,3,2,128]{0,3,2,1:T(8,128)(2,1)} copy(bf16[2048,3,2,128]{3,2,1,0:T(2,128)(2,1)} %param.15) | data formatting | bytes 6291456 | tf_op args[3]
  32.0 1.8 multiply_cosine_fusion
  33.8 76.0 %all-to-all-done = bf16[8,2,32,2048]{3,2,1,0:T(8,128)(2,1)S(1)} async-done(((bf16[8,2,32,2048]{3,2,1,0:T(8,128)(2,1)}), bf16[8,2,32,2048]{3,2,1,0:T(8,128)(2,1)S(1)}, u32[]{:S(2)}, u32[]{:S(2)}) %all-to-all-start) | async-done | bytes 2097184 | tf_op jit(solution)/shard_map/all_to_all | solution.py:102
  111.3 9.9 %all-gather.2.cloned.1.call-done = bf16[1024,2048]{1,0:T(8,128)(2,1)} async-done(((bf16[128,2048]{1,0:T(8,128)(2,1)}), bf16[1024,2048]{1,0:T(8,128)(2,1)}) %all-gather.2.cloned.1.call-update) | async-done | bytes 4194320 | tf_op jit(solution)/shard_map/all_gather | solution.py:90
  121.3 6.2 %fusion.199 = f32[1024,768]{0,1:S(1)} fusion(bf16[1024,2048]{1,0:T(8,128)(2,1)} %all-gather.2.cloned.1.call-done, bf16[2048,768]{0,1:T(8,128)(2,1)} %bitcast.221), kind=kOutput, calls=%fused_computation.239 | convolution fusion | flops 3221225472 | bytes 10485760
  132.8 1.6 fusion.188
  134.5 1.9 fusion.183
  136.4 1.8 fusion.53
  138.2 2.2 fusion.52
  140.4 2.3 fusion.182
  142.7 2.1 fusion.54
  144.8 1.6 fusion.55
  147.6 4.0 all-to-all-start.1
  151.7 3.4 collective-permute-done
  155.1 11.3 %all-to-all-done.1 = bf16[8,128,256]{1,2,0:T(8,128)(2,1)S(1)} async-done(((bf16[8,128,256]{1,2,0:T(8,128)(2,1)}), bf16[8,128,256]{1,2,0:T(8,128)(2,1)S(1)}, u32[]{:S(2)}, u32[]{:S(2)}) %all-to-all-start.1) | async-done | bytes 524320 | tf_op jit(solution)/shard_map/all_to_all | solution.py:154
  166.9 1.7 reduce-window.11
  170.6 2.1 convolution_bitcast_fusion.3
  172.7 2.1 convolution_bitcast_fusion.2
  174.8 2.4 multiply_reduce_fusion
  178.0 2.3 copy.154
  180.3 3.9 all-to-all-start.4
  184.9 2.3 copy.146
  187.2 45.9 %all-to-all-done.4 = bf16[32,14,2048]{2,1,0:T(8,128)(2,1)} async-done(((bf16[32,14,2048]{2,1,0:T(8,128)(2,1)}), bf16[32,14,2048]{2,1,0:T(8,128)(2,1)}, u32[]{:S(2)}, u32[]{:S(2)}) %all-to-all-start.4) | async-done | bytes 1835040 | tf_op jit(solution)/shard_map/all_to_all | solution.py:208
  233.1 4.3 all-to-all-start.2
  237.5 7.7 %fusion.8 = f32[32,14,2,704]{3,0,2,1:T(8,128)S(1)} fusion(bf16[1,2,704,2048]{3,2,1,0:T(8,128)(2,1)} %param.20, bf16[32,14,2048,1]{2,1,0,3:T(8,128)(2,1)} %bitcast.46), kind=kOutput, calls=%fused_computation.8 | convolution fusion | flops 2583691264 | bytes 10125312 | tf_op jit(solution)/shard_map/scd,gfd->scgf/dot_general | solution.py:194
  245.1 1.6 convolution_convert_fusion.1
  246.8 7.5 %fusion.4 = f32[32,14,2,704]{3,0,1,2:T(8,128)S(1)} fusion(bf16[2,704,2048]{2,1,0:T(8,128)(2,1)} %collective-permute-done.1, bf16[32,14,2048]{2,1,0:T(8,128)(2,1)} %all-to-all-done.4), kind=kOutput, calls=%fused_computation.4 | convolution fusion | flops 2583691264 | bytes 10125312 | tf_op jit(solution)/shard_map/scd,gfd->scgf/dot_general | solution.py:194
  254.3 3.5 add_convert_fusion
  257.8 2.4 copy.159
  260.2 26.1 %all-to-all-done.2 = bf16[32,14,2048]{2,1,0:T(8,128)(2,1)} async-done(((bf16[32,14,2048]{2,1,0:T(8,128)(2,1)}), bf16[32,14,2048]{2,1,0:T(8,128)(2,1)}, u32[]{:S(2)}, u32[]{:S(2)}) %all-to-all-start.2) | async-done | bytes 1835040 | tf_op jit(solution)/shard_map/all_to_all | solution.py:208
  286.3 4.4 all-to-all-start.5
  290.7 7.7 %fusion.10 = f32[32,14,2,704]{3,0,2,1:T(8,128)S(1)} fusion(bf16[1,2,704,2048]{3,2,1,0:T(8,128)(2,1)} %param.20, bf16[32,14,2048,1]{2,1,0,3:T(8,128)(2,1)} %bitcast.36), kind=kOutput, calls=%fused_computation.10 | convolution fusion | flops 2583691264 | bytes 10125312 | tf_op jit(solution)/shard_map/scd,gfd->scgf/dot_general | solution.py:194
  298.4 1.6 convolution_convert_fusion.4
  300.0 7.5 %fusion.6 = f32[32,14,2,704]{3,0,2,1:T(8,128)S(1)} fusion(bf16[2,704,2048]{2,1,0:T(8,128)(2,1)} %collective-permute-done.1, bf16[32,14,2048,1]{2,1,0,3:T(8,128)(2,1)} %bitcast.36), kind=kOutput, calls=%fused_computation.6 | convolution fusion | flops 2583691264 | bytes 10125312 | tf_op jit(solution)/shard_map/scd,gfd->scgf/dot_general | solution.py:194
  307.5 3.5 add_convert_fusion.1
  311.0 2.4 copy.150
  313.4 26.1 %all-to-all-done.5 = bf16[32,14,2048]{2,1,0:T(8,128)(2,1)} async-done(((bf16[32,14,2048]{2,1,0:T(8,128)(2,1)}), bf16[32,14,2048]{2,1,0:T(8,128)(2,1)}, u32[]{:S(2)}, u32[]{:S(2)}) %all-to-all-start.5) | async-done | bytes 1835040 | tf_op jit(solution)/shard_map/all_to_all | solution.py:214
  339.5 4.4 all-to-all-start.3
  345.0 3.6 convolution_bitcast_fusion
  348.5 44.3 %all-to-all-done.3 = bf16[32,14,2048]{2,1,0:T(8,128)(2,1)} async-done(((bf16[32,14,2048]{2,1,0:T(8,128)(2,1)}), bf16[32,14,2048]{2,1,0:T(8,128)(2,1)}, u32[]{:S(2)}, u32[]{:S(2)}) %all-to-all-start.3) | async-done | bytes 1835040 | tf_op jit(solution)/shard_map/all_to_all | solution.py:214
  392.8 3.6 fusion.27
  396.7 10.6 %all_to_all.59 = bf16[8,4,2048]{2,1,0:T(4,128)(2,1)S(1)} all-to-all(bf16[8,4,2048]{2,1,0:T(4,128)(2,1)S(1)} %broadcast_in_dim.92), channel_id=1, replica_groups=mesh['seq'=8,'exp'=4] {'seq'}, dimensions={0} | all-to-all | bytes 262144 | tf_op jit(solution)/shard_map/all_to_all | solution.py:230
  407.4 7.2 %all_to_all.60 = bf16[4,4,2048]{2,1,0:T(4,128)(2,1)S(1)} all-to-all(bf16[4,4,2048]{2,1,0:T(4,128)(2,1)S(1)} %broadcast_in_dim.93), channel_id=1, replica_groups=mesh['seq'=8,'exp'=4] {'exp'}, dimensions={0} | all-to-all | bytes 131072 | tf_op jit(solution)/shard_map/all_to_all | solution.py:240
  414.9 8.4 %fusion.198 = (f32[16]{0:T(128)S(1)}, f32[16,3200]{1,0:T(8,128)S(1)}) fusion(bf16[3200,2048]{1,0:T(8,128)(2,1)} %param.23, f32[16,2048]{1,0:T(8,128)S(1)} %reshape.443, f32[2048]{0:T(1024)S(1)} %copy-done.19, f32[16]{0:T(128)S(1)} %rsqrt.30), kind=kOutput, calls=%fused_computation.238 | convolution fusion | flops 209864688 | bytes 13451392 | tf_op jit(solution)/shard_map/dot_general | solution.py:248
  423.6 8.9 %all_to_all.61 = f32[32,2,16]{2,1,0:T(2,128)S(1)} all-to-all(f32[32,2,16]{2,1,0:T(2,128)S(1)} %broadcast_in_dim.94), channel_id=1, replica_groups=mesh['seq'=8,'exp'=4] {'seq','exp'}, dimensions={0} | all-to-all | bytes 8192 | tf_op jit(solution)/shard_map/all_to_all | solution.py:254
  (137 shorter events, 19.8 us)
Async XLA Ops:
  7.2 4.0 copy-start
  7.2 114.1 %all-gather.2.cloned.1.call-start = ((), (), s32[]{:S(2)}) async-start(), calls=%async_computation.9 | async-start | bytes 4718592 | tf_op jit(solution)/shard_map/all_gather | solution.py:90
  10.6 100.7 %collective-permute-start.1 = (bf16[2,704,2048]{2,1,0:T(8,128)(2,1)}, bf16[2,704,2048]{2,1,0:T(8,128)(2,1)}, u32[]{:S(2)}, u32[]{:S(2)}) collective-permute-start(bf16[2,704,2048]{2,1,0:T(8,128)(2,1)} %bitcast.239), channel_id=1, source_target_pairs={{0,1},{1,0},{2,3},{3,2},{4,5},{5,4},{6,7},{7,6},{8,9},{9,8},{10,11... | collective-permute-start | bytes 17301512 | tf_op jit(solution)/shard_map/ppermute | solution.py:52
  12.7 7.2 %copy-start.22 = (s32[1,4]{1,0:T(1,128)S(1)}, s32[1,4]{1,0:T(1,128)}, u32[]{:S(2)}) copy-start(s32[1,4]{1,0:T(1,128)} %param.13) | copy-start | bytes 52
  12.7 97.1 %all-to-all-start = ((bf16[8,2,32,2048]{3,2,1,0:T(8,128)(2,1)}), bf16[8,2,32,2048]{3,2,1,0:T(8,128)(2,1)S(1)}, u32[]{:S(2)}, u32[]{:S(2)}) async-start(bf16[8,2,32,2048]{3,2,1,0:T(8,128)(2,1)} %broadcast_in_dim.70), calls=%async_computation | async-start | bytes 4194304 | tf_op jit(solution)/shard_map/all_to_all | solution.py:102
  19.7 91.6 %collective-permute-start.2 = (bf16[704,2048]{1,0:T(8,128)(2,1)}, bf16[704,2048]{1,0:T(8,128)(2,1)}, u32[]{:S(2)}, u32[]{:S(2)}) collective-permute-start(bf16[704,2048]{1,0:T(8,128)(2,1)} %bitcast.240), channel_id=1, source_target_pairs={{0,1},{1,0},{2,3},{3,2},{4,5},{5,4},{6,7},{7,6},{8,9},{9,8},{10,11... | collective-permute-start | bytes 8650760 | tf_op jit(solution)/shard_map/ppermute | solution.py:52
  109.8 45.3 %collective-permute-start = (bf16[16,32,2048]{2,1,0:T(8,128)(2,1)S(1)}, bf16[16,32,2048]{2,1,0:T(8,128)(2,1)}, u32[]{:S(2)}, u32[]{:S(2)}) collective-permute-start(bf16[16,32,2048]{2,1,0:T(8,128)(2,1)S(1)} %bitcast.218), channel_id=1, source_target_pairs={{0,2},{1,3},{2,0},{3,1},{4,6},{5,7},{6,4},{7,5},{8,10},{9,11},{10,... | collective-permute-start | bytes 6291464 | tf_op jit(solution)/shard_map/ppermute | solution.py:114
  127.6 1.5 copy-start.11
  127.6 1.5 copy-start.12
  129.5 0.7 copy-start.5
  129.5 0.8 copy-start.7
  129.5 0.9 copy-start.9
  131.4 3.0 copy-start.6
  131.4 3.0 copy-start.8
  131.4 3.1 copy-start.10
  131.4 3.1 copy-start.14
  138.2 2.2 copy-start.13
  142.7 2.2 copy-start.23
  144.8 1.7 copy-start.15
  146.5 20.0 %copy-start.17 = (s32[1,128,6]{1,0,2:T(1,128)S(1)}, s32[1,128,6]{1,0,2:T(1,128)}, u32[]{:S(2)}) copy-start(s32[1,128,6]{1,0,2:T(1,128)} %param.19) | copy-start | bytes 9220
  147.6 18.9 %all-to-all-start.1 = ((bf16[8,128,256]{1,2,0:T(8,128)(2,1)}), bf16[8,128,256]{1,2,0:T(8,128)(2,1)S(1)}, u32[]{:S(2)}, u32[]{:S(2)}) async-start(bf16[8,128,256]{1,2,0:T(8,128)(2,1)} %copy.135), calls=%async_computation.1 | async-start | bytes 1048576 | tf_op jit(solution)/shard_map/all_to_all | solution.py:154
  151.6 19.0 %collective-permute-start.3 = (bf16[16,32,2048]{2,1,0:T(8,128)(2,1)S(1)}, bf16[16,32,2048]{2,1,0:T(8,128)(2,1)}, u32[]{:S(2)}, u32[]{:S(2)}) collective-permute-start(bf16[16,32,2048]{2,1,0:T(8,128)(2,1)S(1)} %bitcast.219), channel_id=1, source_target_pairs={{0,1},{1,0},{2,3},{3,2},{4,5},{5,4},{6,7},{7,6},{8,9},{9,8},{10,11... | collective-permute-start | bytes 6291464 | tf_op jit(solution)/shard_map/ppermute | solution.py:52
  166.5 6.2 %copy-start.3 = (bf16[8,128,256]{1,2,0:T(8,128)(2,1)}, bf16[8,128,256]{1,2,0:T(8,128)(2,1)S(1)}, u32[]{:S(2)}) copy-start(bf16[8,128,256]{1,2,0:T(8,128)(2,1)S(1)} %all-to-all-done.1) | copy-start | bytes 1572868
  166.5 6.2 %collective-permute-start.4 = (bf16[16,32,2048]{2,1,0:T(8,128)(2,1)}, bf16[16,32,2048]{2,1,0:T(8,128)(2,1)}, u32[]{:S(2)}, u32[]{:S(2)}) collective-permute-start(bf16[16,32,2048]{2,1,0:T(8,128)(2,1)} %collective-permute-done), channel_id=1, source_target_pairs={{0,1},{1,0},{2,3},{3,2},{4,5},{5,4},{6,7},{7,6},{8,9},{9,8},{10,11... | collective-permute-start | bytes 6291464 | tf_op jit(solution)/shard_map/ppermute | solution.py:52
  172.6 2.2 copy-start.2
  174.8 2.4 copy-start.18
  180.3 52.8 %all-to-all-start.4 = ((bf16[32,14,2048]{2,1,0:T(8,128)(2,1)}), bf16[32,14,2048]{2,1,0:T(8,128)(2,1)}, u32[]{:S(2)}, u32[]{:S(2)}) async-start(bf16[32,14,2048]{2,1,0:T(8,128)(2,1)} %copy.154), calls=%async_computation.4 | async-start | bytes 4194304 | tf_op jit(solution)/shard_map/all_to_all | solution.py:208
  233.1 53.2 %all-to-all-start.2 = ((bf16[32,14,2048]{2,1,0:T(8,128)(2,1)}), bf16[32,14,2048]{2,1,0:T(8,128)(2,1)}, u32[]{:S(2)}, u32[]{:S(2)}) async-start(bf16[32,14,2048]{2,1,0:T(8,128)(2,1)} %copy.146), calls=%async_computation.2 | async-start | bytes 4194304 | tf_op jit(solution)/shard_map/all_to_all | solution.py:208
  237.4 7.7 %copy-start.20 = (bf16[1,704,2048]{2,1,0:T(8,128)(2,1)S(1)}, bf16[1,704,2048]{2,1,0:T(8,128)(2,1)}, u32[]{:S(2)}) copy-start(bf16[1,704,2048]{2,1,0:T(8,128)(2,1)} %param.21) | copy-start | bytes 8650756
  286.3 53.2 %all-to-all-start.5 = ((bf16[32,14,2048]{2,1,0:T(8,128)(2,1)}), bf16[32,14,2048]{2,1,0:T(8,128)(2,1)}, u32[]{:S(2)}, u32[]{:S(2)}) async-start(bf16[32,14,2048]{2,1,0:T(8,128)(2,1)} %copy.159), calls=%async_computation.5 | async-start | bytes 4194304 | tf_op jit(solution)/shard_map/all_to_all | solution.py:214
  290.7 7.7 %copy-start.21 = (bf16[1,704,2048]{2,1,0:T(8,128)(2,1)S(1)}, bf16[1,704,2048]{2,1,0:T(8,128)(2,1)}, u32[]{:S(2)}) copy-start(bf16[1,704,2048]{2,1,0:T(8,128)(2,1)} %param.21) | copy-start | bytes 8650756
  313.4 30.6 %copy-start.16 = (bf16[2048,16]{0,1:T(8,128)(2,1)S(1)}, bf16[2048,16]{0,1:T(8,128)(2,1)}, u32[]{:S(2)}) copy-start(bf16[2048,16]{0,1:T(8,128)(2,1)} %param.18) | copy-start | bytes 196612
  339.5 53.3 %all-to-all-start.3 = ((bf16[32,14,2048]{2,1,0:T(8,128)(2,1)}), bf16[32,14,2048]{2,1,0:T(8,128)(2,1)}, u32[]{:S(2)}, u32[]{:S(2)}) async-start(bf16[32,14,2048]{2,1,0:T(8,128)(2,1)} %copy.150), calls=%async_computation.3 | async-start | bytes 4194304 | tf_op jit(solution)/shard_map/all_to_all | solution.py:214
  392.8 22.0 %copy-start.19 = (f32[2048]{0:T(1024)S(1)}, f32[2048]{0:T(1024)}, u32[]{:S(2)}) copy-start(f32[2048]{0:T(1024)} %param.22) | copy-start | bytes 24580
  396.4 26.9 %copy-start.4 = (bf16[128,2048]{1,0:T(8,128)(2,1)}, bf16[128,2048]{1,0:T(8,128)(2,1)S(1)}, u32[]{:S(2)}) copy-start(bf16[128,2048]{1,0:T(8,128)(2,1)S(1)} %fusion.27) | copy-start | bytes 1572868
  414.9 18.5 %copy-start.1 = (bf16[2,128,2048]{2,1,0:T(8,128)(2,1)S(1)}, bf16[2,128,2048]{2,1,0:T(8,128)(2,1)}, u32[]{:S(2)}) copy-start(bf16[2,128,2048]{2,1,0:T(8,128)(2,1)} %param.16) | copy-start | bytes 3145732
Sparse Core Ops, SparseCore 0:
  10.7 110.5 all-gather.1

commit v11 on v10

--- a/solution.py
+++ b/solution.py
@@ -92,8 +92,13 @@
     down_weight = w_down[0]
     other_gate_up = pair_swap(gate_up)
     other_down = pair_swap(down_weight)
-    other_gate_up, other_down, group_normed = lax.optimization_barrier(
-        (other_gate_up, other_down, group_normed)
+    early_flat = (
+        routes[0].reshape(-1, 1) == jnp.arange(router.shape[1], dtype=jnp.int32)[None, :]
+    ).astype(jnp.int32)
+    early_count = jnp.cumsum(early_flat, axis=0) - early_flat
+    early_slots = jnp.sum(early_count * early_flat, axis=1)
+    other_gate_up, other_down, early_slots, group_normed = lax.optimization_barrier(
+        (other_gate_up, other_down, early_slots, group_normed)
     )
     part_size = head_size // group_count
     own_part = lax.dynamic_slice_in_dim(
@@ -176,10 +181,9 @@
     chosen = jnp.sum(jnp.where(chosen_mask, logits[:, None, :], 0.0), axis=2)
     gates = jax.nn.softmax(chosen, axis=-1)
     capacity = max(2, tok_rows * top_count * 7 // (6 * expert_count))
-    flat_mask = chosen_mask.reshape(tok_rows * top_count, expert_count).astype(jnp.int32)
-    earlier_count = jnp.cumsum(flat_mask, axis=0) - flat_mask
-    slot_index = jnp.sum(earlier_count * flat_mask, axis=1)
+    slot_index = early_slots
     target = (token_routes.reshape(-1) * capacity + slot_index).reshape(tok_rows, top_count)
+    target, chosen_mask = lax.optimization_barrier((target, chosen_mask))
     slot_total = expert_count * capacity
     placed = target[:, :, None] == jnp.arange(slot_total, dtype=jnp.int32)[None, None, :]
     shares = device_count // expert_count

time: 449 us -> 451 us (level)
    unnamed x51 -> x58, local copies, waits for them, and re-layouts: 9.97 us -> 11.9 us
where the time goes in v11:
time: 451 us; the launch traced here: 443 us
  waiting for transfers between devices  241 us (53%)
  matrix products  87.6 us (19%)
  starting transfers between devices  30.2 us (7%)
  blocking collectives  26.8 us (6%)
  local copies, waits for them, and re-layouts  25.5 us (6%)
  other arithmetic  16.4 us (4%)
  between operations  15 us (3%)
    all_to_all x1, waiting for transfers between devices, per_device(): lax.all_to_all(jnp.broadcast_to(own_part[None], (seq_count,) + own_part.s...  73.5 us
    all_to_all x2, waiting for transfers between devices, per_device(): lax.all_to_all(outgoing, ('seq', 'exp'), split_axis=0, concat_axis=0, til...  72 us
    all_to_all x2, waiting for transfers between devices, per_device(): lax.all_to_all(part_sum.astype(jnp.bfloat16), ('seq', 'exp'), split_axis=...  70.4 us
    dot_general x4, matrix products, share_part(): jnp.einsum('scd,gfd->scgf', rows, pair, preferred_element_type=jnp.float32)  30.3 us
    all_to_all x1, waiting for transfers between devices, per_device(): lax.all_to_all(heads_flat, 'seq', split_axis=0, concat_axis=1, tiled=True)  14.8 us
    unnamed x58, local copies, waits for them, and re-layouts  11.9 us
    all_to_all x1, blocking collectives, per_device(): lax.all_to_all(jnp.broadcast_to(picked.astype(jnp.bfloat16)[None], (seq_c...  10.6 us
    dot_general x4, matrix products, share_part(): jnp.einsum('scf,fd->scd', act, down, preferred_element_type=jnp.float32)  10.3 us
  transfers between devices with their start and end apart: 12, of which 8 were waited for; matrix products, arithmetic and copies ran while one was open for 23% of the time, Pallas kernels for 0%

profile of v11, /device:TPU:0, one launch (start us, length us, event | category | flops | bytes accessed | tf_op | source)
XLA Modules:
  0.0 442.9 jit_solution(15187390229727615877)
XLA Ops:
  8.5 2.0 fusion.58
  11.1 1.6 broadcast_in_dim.70
  12.7 7.0 %all-to-all-start = ((bf16[8,2,32,2048]{3,2,1,0:T(8,128)(2,1)}), bf16[8,2,32,2048]{3,2,1,0:T(8,128)(2,1)S(1)}, u32[]{:S(2)}, u32[]{:S(2)}) async-start(bf16[8,2,32,2048]{3,2,1,0:T(8,128)(2,1)} %broadcast_in_dim.70), calls=%async_computation | async-start | bytes 4194304 | tf_op jit(solution)/shard_map/all_to_all | solution.py:107
  20.3 1.7 reduce-window.10
  22.3 8.7 %copy.125 = bf16[2048,3,2,128]{0,3,2,1:T(8,128)(2,1)} copy(bf16[2048,3,2,128]{3,2,1,0:T(2,128)(2,1)} %param.15) | data formatting | bytes 6291456 | tf_op args[3]
  34.5 1.8 multiply_cosine_fusion
  36.3 73.5 %all-to-all-done = bf16[8,2,32,2048]{3,2,1,0:T(8,128)(2,1)S(1)} async-done(((bf16[8,2,32,2048]{3,2,1,0:T(8,128)(2,1)}), bf16[8,2,32,2048]{3,2,1,0:T(8,128)(2,1)S(1)}, u32[]{:S(2)}, u32[]{:S(2)}) %all-to-all-start) | async-done | bytes 2097184 | tf_op jit(solution)/shard_map/all_to_all | solution.py:107
  111.3 9.9 %all-gather.2.cloned.1.call-done = bf16[1024,2048]{1,0:T(8,128)(2,1)} async-done(((bf16[128,2048]{1,0:T(8,128)(2,1)}), bf16[1024,2048]{1,0:T(8,128)(2,1)}) %all-gather.2.cloned.1.call-update) | async-done | bytes 4194320 | tf_op jit(solution)/shard_map/all_gather | solution.py:90
  121.3 6.2 %fusion.198 = f32[1024,768]{0,1:S(1)} fusion(bf16[1024,2048]{1,0:T(8,128)(2,1)} %all-gather.2.cloned.1.call-done, bf16[2048,768]{0,1:T(8,128)(2,1)} %bitcast.217), kind=kOutput, calls=%fused_computation.238 | convolution fusion | flops 3221225472 | bytes 10485760
  131.5 1.9 fusion.192
  133.4 3.4 convert.18
  137.7 2.5 fusion.182
  140.2 2.4 fusion.53
  142.6 1.6 fusion.52
  144.2 2.8 fusion.181
  147.0 2.1 fusion.54
  149.2 1.6 fusion.55
  151.9 4.0 all-to-all-start.1
  156.0 14.8 %all-to-all-done.1 = bf16[8,128,256]{1,2,0:T(8,128)(2,1)S(1)} async-done(((bf16[8,128,256]{1,2,0:T(8,128)(2,1)}), bf16[8,128,256]{1,2,0:T(8,128)(2,1)S(1)}, u32[]{:S(2)}, u32[]{:S(2)}) %all-to-all-start.1) | async-done | bytes 524320 | tf_op jit(solution)/shard_map/all_to_all | solution.py:159
  172.4 2.1 convolution_bitcast_fusion.3
  175.3 2.1 convolution_bitcast_fusion.2
  177.4 2.4 multiply_reduce_fusion
  180.6 2.3 copy.149
  182.9 3.8 all-to-all-start.4
  187.3 2.3 copy.141
  189.7 45.9 %all-to-all-done.4 = bf16[32,14,2048]{2,1,0:T(8,128)(2,1)} async-done(((bf16[32,14,2048]{2,1,0:T(8,128)(2,1)}), bf16[32,14,2048]{2,1,0:T(8,128)(2,1)}, u32[]{:S(2)}, u32[]{:S(2)}) %all-to-all-start.4) | async-done | bytes 1835040 | tf_op jit(solution)/shard_map/all_to_all | solution.py:212
  235.6 4.3 all-to-all-start.2
  239.9 7.7 %fusion.8 = f32[32,14,2,704]{3,0,2,1:T(8,128)S(1)} fusion(bf16[1,2,704,2048]{3,2,1,0:T(8,128)(2,1)} %param.20, bf16[32,14,2048,1]{2,1,0,3:T(8,128)(2,1)} %bitcast.44), kind=kOutput, calls=%fused_computation.8 | convolution fusion | flops 2583691264 | bytes 10125312 | tf_op jit(solution)/shard_map/scd,gfd->scgf/dot_general | solution.py:198
  247.6 1.6 convolution_convert_fusion.1
  249.2 7.5 %fusion.4 = f32[32,14,2,704]{3,0,1,2:T(8,128)S(1)} fusion(bf16[2,704,2048]{2,1,0:T(8,128)(2,1)} %collective-permute-done.1, bf16[32,14,2048]{2,1,0:T(8,128)(2,1)} %all-to-all-done.4), kind=kOutput, calls=%fused_computation.4 | convolution fusion | flops 2583691264 | bytes 10125312 | tf_op jit(solution)/shard_map/scd,gfd->scgf/dot_general | solution.py:198
  256.7 3.5 add_convert_fusion
  260.2 2.4 copy.154
  262.7 26.1 %all-to-all-done.2 = bf16[32,14,2048]{2,1,0:T(8,128)(2,1)} async-done(((bf16[32,14,2048]{2,1,0:T(8,128)(2,1)}), bf16[32,14,2048]{2,1,0:T(8,128)(2,1)}, u32[]{:S(2)}, u32[]{:S(2)}) %all-to-all-start.2) | async-done | bytes 1835040 | tf_op jit(solution)/shard_map/all_to_all | solution.py:212
  288.7 4.4 all-to-all-start.5
  293.1 7.7 %fusion.10 = f32[32,14,2,704]{3,0,2,1:T(8,128)S(1)} fusion(bf16[1,2,704,2048]{3,2,1,0:T(8,128)(2,1)} %param.20, bf16[32,14,2048,1]{2,1,0,3:T(8,128)(2,1)} %bitcast.34), kind=kOutput, calls=%fused_computation.10 | convolution fusion | flops 2583691264 | bytes 10125312 | tf_op jit(solution)/shard_map/scd,gfd->scgf/dot_general | solution.py:198
  300.8 1.6 convolution_convert_fusion.4
  302.4 7.5 %fusion.6 = f32[32,14,2,704]{3,0,2,1:T(8,128)S(1)} fusion(bf16[2,704,2048]{2,1,0:T(8,128)(2,1)} %collective-permute-done.1, bf16[32,14,2048,1]{2,1,0,3:T(8,128)(2,1)} %bitcast.34), kind=kOutput, calls=%fused_computation.6 | convolution fusion | flops 2583691264 | bytes 10125312 | tf_op jit(solution)/shard_map/scd,gfd->scgf/dot_general | solution.py:198
  310.0 3.5 add_convert_fusion.1
  313.5 2.4 copy.145
  315.8 26.1 %all-to-all-done.5 = bf16[32,14,2048]{2,1,0:T(8,128)(2,1)} async-done(((bf16[32,14,2048]{2,1,0:T(8,128)(2,1)}), bf16[32,14,2048]{2,1,0:T(8,128)(2,1)}, u32[]{:S(2)}, u32[]{:S(2)}) %all-to-all-start.5) | async-done | bytes 1835040 | tf_op jit(solution)/shard_map/all_to_all | solution.py:218
  342.0 4.4 all-to-all-start.3
  347.4 3.6 convolution_bitcast_fusion
  351.0 44.3 %all-to-all-done.3 = bf16[32,14,2048]{2,1,0:T(8,128)(2,1)} async-done(((bf16[32,14,2048]{2,1,0:T(8,128)(2,1)}), bf16[32,14,2048]{2,1,0:T(8,128)(2,1)}, u32[]{:S(2)}, u32[]{:S(2)}) %all-to-all-start.3) | async-done | bytes 1835040 | tf_op jit(solution)/shard_map/all_to_all | solution.py:218
  395.2 3.6 fusion.27
  399.1 10.6 %all_to_all.59 = bf16[8,4,2048]{2,1,0:T(4,128)(2,1)S(1)} all-to-all(bf16[8,4,2048]{2,1,0:T(4,128)(2,1)S(1)} %broadcast_in_dim.88), channel_id=1, replica_groups=mesh['seq'=8,'exp'=4] {'seq'}, dimensions={0} | all-to-all | bytes 262144 | tf_op jit(solution)/shard_map/all_to_all | solution.py:234
  409.8 7.2 %all_to_all.60 = bf16[4,4,2048]{2,1,0:T(4,128)(2,1)S(1)} all-to-all(bf16[4,4,2048]{2,1,0:T(4,128)(2,1)S(1)} %broadcast_in_dim.93), channel_id=1, replica_groups=mesh['seq'=8,'exp'=4] {'exp'}, dimensions={0} | all-to-all | bytes 131072 | tf_op jit(solution)/shard_map/all_to_all | solution.py:244
  417.3 8.4 %fusion.197 = (f32[16]{0:T(128)S(1)}, f32[16,3200]{1,0:T(8,128)S(1)}) fusion(bf16[3200,2048]{1,0:T(8,128)(2,1)} %param.23, f32[16,2048]{1,0:T(8,128)S(1)} %reshape.438, f32[2048]{0:T(1024)S(1)} %copy-done.21, f32[16]{0:T(128)S(1)} %rsqrt.30), kind=kOutput, calls=%fused_computation.237 | convolution fusion | flops 209864688 | bytes 13451392 | tf_op jit(solution)/shard_map/dot_general | solution.py:252
  426.0 8.9 %all_to_all.61 = f32[32,2,16]{2,1,0:T(2,128)S(1)} all-to-all(f32[32,2,16]{2,1,0:T(2,128)S(1)} %broadcast_in_dim.94), channel_id=1, replica_groups=mesh['seq'=8,'exp'=4] {'seq','exp'}, dimensions={0} | all-to-all | bytes 8192 | tf_op jit(solution)/shard_map/all_to_all | solution.py:258
  (143 shorter events, 20.3 us)
Async XLA Ops:
  7.2 4.0 copy-start
  7.2 114.1 %all-gather.2.cloned.1.call-start = ((), (), s32[]{:S(2)}) async-start(), calls=%async_computation.9 | async-start | bytes 4718592 | tf_op jit(solution)/shard_map/all_gather | solution.py:90
  10.6 100.7 %collective-permute-start.1 = (bf16[2,704,2048]{2,1,0:T(8,128)(2,1)}, bf16[2,704,2048]{2,1,0:T(8,128)(2,1)}, u32[]{:S(2)}, u32[]{:S(2)}) collective-permute-start(bf16[2,704,2048]{2,1,0:T(8,128)(2,1)} %bitcast.235), channel_id=1, source_target_pairs={{0,1},{1,0},{2,3},{3,2},{4,5},{5,4},{6,7},{7,6},{8,9},{9,8},{10,11... | collective-permute-start | bytes 17301512 | tf_op jit(solution)/shard_map/ppermute | solution.py:52
  12.7 7.2 %copy-start.19 = (s32[1,128,6]{1,0,2:T(1,128)S(1)}, s32[1,128,6]{1,0,2:T(1,128)}, u32[]{:S(2)}) copy-start(s32[1,128,6]{1,0,2:T(1,128)} %param.19) | copy-start | bytes 9220
  12.7 97.1 %all-to-all-start = ((bf16[8,2,32,2048]{3,2,1,0:T(8,128)(2,1)}), bf16[8,2,32,2048]{3,2,1,0:T(8,128)(2,1)S(1)}, u32[]{:S(2)}, u32[]{:S(2)}) async-start(bf16[8,2,32,2048]{3,2,1,0:T(8,128)(2,1)} %broadcast_in_dim.70), calls=%async_computation | async-start | bytes 4194304 | tf_op jit(solution)/shard_map/all_to_all | solution.py:107
  19.7 91.6 %collective-permute-start.2 = (bf16[704,2048]{1,0:T(8,128)(2,1)}, bf16[704,2048]{1,0:T(8,128)(2,1)}, u32[]{:S(2)}, u32[]{:S(2)}) collective-permute-start(bf16[704,2048]{1,0:T(8,128)(2,1)} %bitcast.236), channel_id=1, source_target_pairs={{0,1},{1,0},{2,3},{3,2},{4,5},{5,4},{6,7},{7,6},{8,9},{9,8},{10,11... | collective-permute-start | bytes 8650760 | tf_op jit(solution)/shard_map/ppermute | solution.py:52
  22.3 8.8 %copy-start.24 = (s32[1,4]{1,0:T(1,128)S(1)}, s32[1,4]{1,0:T(1,128)}, u32[]{:S(2)}) copy-start(s32[1,4]{1,0:T(1,128)} %param.13) | copy-start | bytes 52
  109.8 46.2 %collective-permute-start = (bf16[16,32,2048]{2,1,0:T(8,128)(2,1)S(1)}, bf16[16,32,2048]{2,1,0:T(8,128)(2,1)}, u32[]{:S(2)}, u32[]{:S(2)}) collective-permute-start(bf16[16,32,2048]{2,1,0:T(8,128)(2,1)S(1)} %bitcast.214), channel_id=1, source_target_pairs={{0,2},{1,3},{2,0},{3,1},{4,6},{5,7},{6,4},{7,5},{8,10},{9,11},{10,... | collective-permute-start | bytes 6291464 | tf_op jit(solution)/shard_map/ppermute | solution.py:119
  127.5 1.7 copy-start.2
  127.5 1.7 copy-start.12
  127.5 1.7 copy-start.13
  129.5 0.7 copy-start.6
  129.5 0.8 copy-start.8
  129.6 0.9 copy-start.10
  133.4 3.4 copy-start.7
  133.4 3.4 copy-start.9
  133.4 3.4 copy-start.11
  133.4 3.4 copy-start.16
  136.8 0.9 copy-start.15
  142.6 1.6 copy-start.14
  147.0 2.2 copy-start.25
  147.0 2.2 copy-start.26
  149.2 1.7 copy-start.17
  151.9 18.9 %all-to-all-start.1 = ((bf16[8,128,256]{1,2,0:T(8,128)(2,1)}), bf16[8,128,256]{1,2,0:T(8,128)(2,1)S(1)}, u32[]{:S(2)}, u32[]{:S(2)}) async-start(bf16[8,128,256]{1,2,0:T(8,128)(2,1)} %copy.135), calls=%async_computation.1 | async-start | bytes 1048576 | tf_op jit(solution)/shard_map/all_to_all | solution.py:159
  155.9 16.4 %collective-permute-start.3 = (bf16[16,32,2048]{2,1,0:T(8,128)(2,1)S(1)}, bf16[16,32,2048]{2,1,0:T(8,128)(2,1)}, u32[]{:S(2)}, u32[]{:S(2)}) collective-permute-start(bf16[16,32,2048]{2,1,0:T(8,128)(2,1)S(1)} %bitcast.215), channel_id=1, source_target_pairs={{0,1},{1,0},{2,3},{3,2},{4,5},{5,4},{6,7},{7,6},{8,9},{9,8},{10,11... | collective-permute-start | bytes 6291464 | tf_op jit(solution)/shard_map/ppermute | solution.py:52
  170.8 4.5 %copy-start.4 = (bf16[8,128,256]{1,2,0:T(8,128)(2,1)}, bf16[8,128,256]{1,2,0:T(8,128)(2,1)S(1)}, u32[]{:S(2)}) copy-start(bf16[8,128,256]{1,2,0:T(8,128)(2,1)S(1)} %all-to-all-done.1) | copy-start | bytes 1572868
  170.8 4.5 %collective-permute-start.4 = (bf16[16,32,2048]{2,1,0:T(8,128)(2,1)}, bf16[16,32,2048]{2,1,0:T(8,128)(2,1)}, u32[]{:S(2)}, u32[]{:S(2)}) collective-permute-start(bf16[16,32,2048]{2,1,0:T(8,128)(2,1)} %collective-permute-done), channel_id=1, source_target_pairs={{0,1},{1,0},{2,3},{3,2},{4,5},{5,4},{6,7},{7,6},{8,9},{9,8},{10,11... | collective-permute-start | bytes 6291464 | tf_op jit(solution)/shard_map/ppermute | solution.py:52
  174.4 2.9 copy-start.3
  177.4 2.4 copy-start.20
  182.9 52.6 %all-to-all-start.4 = ((bf16[32,14,2048]{2,1,0:T(8,128)(2,1)}), bf16[32,14,2048]{2,1,0:T(8,128)(2,1)}, u32[]{:S(2)}, u32[]{:S(2)}) async-start(bf16[32,14,2048]{2,1,0:T(8,128)(2,1)} %copy.149), calls=%async_computation.4 | async-start | bytes 4194304 | tf_op jit(solution)/shard_map/all_to_all | solution.py:212
  235.6 53.2 %all-to-all-start.2 = ((bf16[32,14,2048]{2,1,0:T(8,128)(2,1)}), bf16[32,14,2048]{2,1,0:T(8,128)(2,1)}, u32[]{:S(2)}, u32[]{:S(2)}) async-start(bf16[32,14,2048]{2,1,0:T(8,128)(2,1)} %copy.141), calls=%async_computation.2 | async-start | bytes 4194304 | tf_op jit(solution)/shard_map/all_to_all | solution.py:212
  239.9 7.7 %copy-start.22 = (bf16[1,704,2048]{2,1,0:T(8,128)(2,1)S(1)}, bf16[1,704,2048]{2,1,0:T(8,128)(2,1)}, u32[]{:S(2)}) copy-start(bf16[1,704,2048]{2,1,0:T(8,128)(2,1)} %param.21) | copy-start | bytes 8650756
  288.7 53.2 %all-to-all-start.5 = ((bf16[32,14,2048]{2,1,0:T(8,128)(2,1)}), bf16[32,14,2048]{2,1,0:T(8,128)(2,1)}, u32[]{:S(2)}, u32[]{:S(2)}) async-start(bf16[32,14,2048]{2,1,0:T(8,128)(2,1)} %copy.154), calls=%async_computation.5 | async-start | bytes 4194304 | tf_op jit(solution)/shard_map/all_to_all | solution.py:218
  293.1 7.7 %copy-start.23 = (bf16[1,704,2048]{2,1,0:T(8,128)(2,1)S(1)}, bf16[1,704,2048]{2,1,0:T(8,128)(2,1)}, u32[]{:S(2)}) copy-start(bf16[1,704,2048]{2,1,0:T(8,128)(2,1)} %param.21) | copy-start | bytes 8650756
  315.8 30.6 %copy-start.18 = (bf16[2048,16]{0,1:T(8,128)(2,1)S(1)}, bf16[2048,16]{0,1:T(8,128)(2,1)}, u32[]{:S(2)}) copy-start(bf16[2048,16]{0,1:T(8,128)(2,1)} %param.18) | copy-start | bytes 196612
  342.0 53.3 %all-to-all-start.3 = ((bf16[32,14,2048]{2,1,0:T(8,128)(2,1)}), bf16[32,14,2048]{2,1,0:T(8,128)(2,1)}, u32[]{:S(2)}, u32[]{:S(2)}) async-start(bf16[32,14,2048]{2,1,0:T(8,128)(2,1)} %copy.145), calls=%async_computation.3 | async-start | bytes 4194304 | tf_op jit(solution)/shard_map/all_to_all | solution.py:218
  395.2 22.0 %copy-start.21 = (f32[2048]{0:T(1024)S(1)}, f32[2048]{0:T(1024)}, u32[]{:S(2)}) copy-start(f32[2048]{0:T(1024)} %param.22) | copy-start | bytes 24580
  398.8 26.9 %copy-start.5 = (bf16[128,2048]{1,0:T(8,128)(2,1)}, bf16[128,2048]{1,0:T(8,128)(2,1)S(1)}, u32[]{:S(2)}) copy-start(bf16[128,2048]{1,0:T(8,128)(2,1)S(1)} %fusion.27) | copy-start | bytes 1572868
  417.3 18.5 %copy-start.1 = (bf16[2,128,2048]{2,1,0:T(8,128)(2,1)S(1)}, bf16[2,128,2048]{2,1,0:T(8,128)(2,1)}, u32[]{:S(2)}) copy-start(bf16[2,128,2048]{2,1,0:T(8,128)(2,1)} %param.16) | copy-start | bytes 3145732
Sparse Core Ops, SparseCore 0:
  10.7 110.5 all-gather.1

commit v12 on v10

--- a/solution.py
+++ b/solution.py
@@ -196,7 +196,8 @@
         part = jnp.einsum("scf,fd->scd", act, down, preferred_element_type=jnp.float32)
         return part.astype(jnp.bfloat16).astype(jnp.float32)
 
-    cuts = [0, per_dest // 2, per_dest]
+    first_cut = per_dest - 16 if per_dest > 16 else per_dest // 2
+    cuts = [0, first_cut, per_dest]
     routed = jnp.zeros((tok_rows, model_width), jnp.float32)
     for low, high in zip(cuts[:-1], cuts[1:]):
         outgoing = jnp.einsum(

time: 449 us -> 449 us (level)
  local copies, waits for them, and re-layouts: 23.6 us -> 28.6 us
    dot_general x4, matrix products: 30.3 us -> 25.8 us  [share_part(): jnp.einsum('scd,gfd->scgf', rows, pair, preferred_element_type=jnp.float32)]
    unnamed x51 -> x57, local copies, waits for them, and re-layouts: 9.97 us -> 12.8 us
where the time goes in v12:
time: 449 us; the launch traced here: 441 us
  waiting for transfers between devices  239 us (53%)
  matrix products  84.5 us (19%)
  starting transfers between devices  30.1 us (7%)
  local copies, waits for them, and re-layouts  28.6 us (6%)
  blocking collectives  26.8 us (6%)
  other arithmetic  16.2 us (4%)
  between operations  15.1 us (3%)
    all_to_all x1, waiting for transfers between devices, per_device(): lax.all_to_all(jnp.broadcast_to(own_part[None], (seq_count,) + own_part.s...  76 us
    all_to_all x2, waiting for transfers between devices, per_device(): lax.all_to_all(outgoing, ('seq', 'exp'), split_axis=0, concat_axis=0, til...  72.3 us
    all_to_all x2, waiting for transfers between devices, per_device(): lax.all_to_all(part_sum.astype(jnp.bfloat16), ('seq', 'exp'), split_axis=...  66.5 us
    dot_general x4, matrix products, share_part(): jnp.einsum('scd,gfd->scgf', rows, pair, preferred_element_type=jnp.float32)  25.8 us
    unnamed x57, local copies, waits for them, and re-layouts  12.8 us
    all_to_all x1, waiting for transfers between devices, per_device(): lax.all_to_all(heads_flat, 'seq', split_axis=0, concat_axis=1, tiled=True)  11.3 us
    all_to_all x1, blocking collectives, per_device(): lax.all_to_all(jnp.broadcast_to(picked.astype(jnp.bfloat16)[None], (seq_c...  10.6 us
    dot_general x4, matrix products, share_part(): jnp.einsum('scf,fd->scd', act, down, preferred_element_type=jnp.float32)  10.2 us
  transfers between devices with their start and end apart: 12, of which 8 were waited for; matrix products, arithmetic and copies ran while one was open for 23% of the time, Pallas kernels for 0%

profile of v12, /device:TPU:0, one launch (start us, length us, event | category | flops | bytes accessed | tf_op | source)
XLA Modules:
  0.0 440.7 jit_solution(14400899907311674315)
XLA Ops:
  8.5 2.0 fusion.65
  12.7 7.0 %all-to-all-start = ((bf16[8,2,32,2048]{3,2,1,0:T(8,128)(2,1)}), bf16[8,2,32,2048]{3,2,1,0:T(8,128)(2,1)S(1)}, u32[]{:S(2)}, u32[]{:S(2)}) async-start(bf16[8,2,32,2048]{3,2,1,0:T(8,128)(2,1)} %broadcast_in_dim.70), calls=%async_computation | async-start | bytes 4194304 | tf_op jit(solution)/shard_map/all_to_all | solution.py:102
  20.1 8.8 %copy.117 = bf16[2048,3,2,128]{0,3,2,1:T(8,128)(2,1)} copy(bf16[2048,3,2,128]{3,2,1,0:T(2,128)(2,1)} %param.15) | data formatting | bytes 6291456 | tf_op args[3]
  32.0 1.8 multiply_cosine_fusion
  33.8 76.0 %all-to-all-done = bf16[8,2,32,2048]{3,2,1,0:T(8,128)(2,1)S(1)} async-done(((bf16[8,2,32,2048]{3,2,1,0:T(8,128)(2,1)}), bf16[8,2,32,2048]{3,2,1,0:T(8,128)(2,1)S(1)}, u32[]{:S(2)}, u32[]{:S(2)}) %all-to-all-start) | async-done | bytes 2097184 | tf_op jit(solution)/shard_map/all_to_all | solution.py:102
  111.3 9.9 %all-gather.2.cloned.1.call-done = bf16[1024,2048]{1,0:T(8,128)(2,1)} async-done(((bf16[128,2048]{1,0:T(8,128)(2,1)}), bf16[1024,2048]{1,0:T(8,128)(2,1)}) %all-gather.2.cloned.1.call-update) | async-done | bytes 4194320 | tf_op jit(solution)/shard_map/all_gather | solution.py:90
  121.3 6.2 %fusion.201 = f32[1024,768]{0,1:S(1)} fusion(bf16[1024,2048]{1,0:T(8,128)(2,1)} %all-gather.2.cloned.1.call-done, bf16[2048,768]{0,1:T(8,128)(2,1)} %bitcast.225), kind=kOutput, calls=%fused_computation.237 | convolution fusion | flops 3221225472 | bytes 10485760
  132.8 1.6 fusion.190
  134.5 1.9 fusion.185
  136.4 1.8 fusion.58
  138.2 2.2 fusion.57
  140.4 2.3 fusion.184
  142.7 2.1 fusion.59
  144.8 1.6 fusion.60
  147.6 4.0 all-to-all-start.1
  151.7 3.4 collective-permute-done
  155.1 11.3 %all-to-all-done.1 = bf16[8,128,256]{1,2,0:T(8,128)(2,1)S(1)} async-done(((bf16[8,128,256]{1,2,0:T(8,128)(2,1)}), bf16[8,128,256]{1,2,0:T(8,128)(2,1)S(1)}, u32[]{:S(2)}, u32[]{:S(2)}) %all-to-all-start.1) | async-done | bytes 524320 | tf_op jit(solution)/shard_map/all_to_all | solution.py:154
  166.9 1.7 reduce-window.11
  170.5 2.1 convolution_bitcast_fusion.3
  172.6 2.1 convolution_bitcast_fusion.2
  174.8 2.4 multiply_reduce_fusion
  177.3 2.0 convolution_convert_fusion.2
  179.3 3.9 all-to-all-start.4
  183.8 2.3 copy.138
  186.1 46.0 %all-to-all-done.4 = bf16[32,16,2048]{2,1,0:T(8,128)(2,1)} async-done(((bf16[32,16,2048]{2,1,0:T(8,128)(2,1)}), bf16[32,16,2048]{2,1,0:T(8,128)(2,1)}, u32[]{:S(2)}, u32[]{:S(2)}) %all-to-all-start.4) | async-done | bytes 2097184 | tf_op jit(solution)/shard_map/all_to_all | solution.py:209
  232.1 4.2 all-to-all-start.2
  236.3 6.2 %fusion.4 = f32[32,16,2,704]{3,1,2,0:T(8,128)S(1)} fusion(bf16[2,704,2048]{2,1,0:T(8,128)(2,1)} %collective-permute-done.1, bf16[32,16,2048]{2,1,0:T(8,128)(2,1)} %all-to-all-done.4), kind=kOutput, calls=%fused_computation.4 | convolution fusion | flops 2952790016 | bytes 10747904 | tf_op jit(solution)/shard_map/scd,gfd->scgf/dot_general | solution.py:194
  243.0 6.2 %fusion.8 = f32[32,16,2,704]{3,1,2,0:T(8,128)S(1)} fusion(bf16[1,2,704,2048]{3,2,1,0:T(8,128)(2,1)} %param.20, bf16[32,16,2048]{2,1,0:T(8,128)(2,1)} %all-to-all-done.4), kind=kOutput, calls=%fused_computation.8 | convolution fusion | flops 2952790016 | bytes 10747904 | tf_op jit(solution)/shard_map/scd,gfd->scgf/dot_general | solution.py:194
  251.0 1.8 convolution_convert_fusion.1
  252.8 3.6 add_convert_fusion
  256.4 2.5 copy.148
  258.9 26.3 %all-to-all-done.2 = bf16[32,12,2048]{2,1,0:T(8,128)(2,1)S(1)} async-done(((bf16[32,12,2048]{2,1,0:T(8,128)(2,1)}), bf16[32,12,2048]{2,1,0:T(8,128)(2,1)S(1)}, u32[]{:S(2)}, u32[]{:S(2)}) %all-to-all-start.2) | async-done | bytes 1572896 | tf_op jit(solution)/shard_map/all_to_all | solution.py:209
  286.6 4.2 all-to-all-start.5
  290.8 7.0 %fusion.10 = f32[32,12,2,704]{3,0,2,1:T(8,128)S(1)} fusion(bf16[1,2,704,2048]{3,2,1,0:T(8,128)(2,1)} %param.20, bf16[32,12,2048,1]{2,1,0,3:T(8,128)(2,1)} %bitcast.231), kind=kOutput, calls=%fused_computation.10 | convolution fusion | flops 2214592512 | bytes 9502720 | tf_op jit(solution)/shard_map/scd,gfd->scgf/dot_general | solution.py:194
  299.4 6.5 %fusion.6 = f32[32,12,2,704]{3,0,2,1:T(8,128)S(1)} fusion(bf16[2,704,2048]{2,1,0:T(8,128)(2,1)} %collective-permute-done.1, bf16[32,12,2048,1]{2,1,0,3:T(8,128)(2,1)S(1)} %bitcast.232), kind=kOutput, calls=%fused_computation.6 | convolution fusion | flops 2214592512 | bytes 9502720 | tf_op jit(solution)/shard_map/scd,gfd->scgf/dot_general | solution.py:194
  305.9 3.3 add_convert_fusion.1
  309.2 2.2 copy.142
  311.5 28.2 %all-to-all-done.5 = bf16[32,16,2048]{2,1,0:T(8,128)(2,1)S(1)} async-done(((bf16[32,16,2048]{2,1,0:T(8,128)(2,1)}), bf16[32,16,2048]{2,1,0:T(8,128)(2,1)S(1)}, u32[]{:S(2)}, u32[]{:S(2)}) %all-to-all-start.5) | async-done | bytes 2097184 | tf_op jit(solution)/shard_map/all_to_all | solution.py:215
  339.7 4.4 all-to-all-start.3
  346.6 2.0 copy.134
  348.6 1.8 reshape.440
  351.6 3.1 convolution_bitcast_fusion
  354.7 38.3 %all-to-all-done.3 = bf16[32,12,2048]{2,1,0:T(8,128)(2,1)} async-done(((bf16[32,12,2048]{2,1,0:T(8,128)(2,1)}), bf16[32,12,2048]{2,1,0:T(8,128)(2,1)}, u32[]{:S(2)}, u32[]{:S(2)}) %all-to-all-start.3) | async-done | bytes 1572896 | tf_op jit(solution)/shard_map/all_to_all | solution.py:215
  392.9 3.7 fusion.35
  396.9 10.6 %all_to_all.59 = bf16[8,4,2048]{2,1,0:T(4,128)(2,1)S(1)} all-to-all(bf16[8,4,2048]{2,1,0:T(4,128)(2,1)S(1)} %broadcast_in_dim.92), channel_id=1, replica_groups=mesh['seq'=8,'exp'=4] {'seq'}, dimensions={0} | all-to-all | bytes 262144 | tf_op jit(solution)/shard_map/all_to_all | solution.py:231
  407.6 7.2 %all_to_all.60 = bf16[4,4,2048]{2,1,0:T(4,128)(2,1)S(1)} all-to-all(bf16[4,4,2048]{2,1,0:T(4,128)(2,1)S(1)} %broadcast_in_dim.93), channel_id=1, replica_groups=mesh['seq'=8,'exp'=4] {'exp'}, dimensions={0} | all-to-all | bytes 131072 | tf_op jit(solution)/shard_map/all_to_all | solution.py:241
  415.1 8.4 %fusion.200 = (f32[16]{0:T(128)S(1)}, f32[16,3200]{1,0:T(8,128)S(1)}) fusion(bf16[3200,2048]{1,0:T(8,128)(2,1)} %param.23, f32[16,2048]{1,0:T(8,128)S(1)} %reshape.443, f32[2048]{0:T(1024)S(1)} %copy-done.22, f32[16]{0:T(128)S(1)} %rsqrt.30), kind=kOutput, calls=%fused_computation.236 | convolution fusion | flops 209864688 | bytes 13451392 | tf_op jit(solution)/shard_map/dot_general | solution.py:249
  423.8 8.9 %all_to_all.61 = f32[32,2,16]{2,1,0:T(2,128)S(1)} all-to-all(f32[32,2,16]{2,1,0:T(2,128)S(1)} %broadcast_in_dim.94), channel_id=1, replica_groups=mesh['seq'=8,'exp'=4] {'seq','exp'}, dimensions={0} | all-to-all | bytes 8192 | tf_op jit(solution)/shard_map/all_to_all | solution.py:255
  (146 shorter events, 28.5 us)
Async XLA Ops:
  7.2 4.0 copy-start
  7.2 114.1 %all-gather.2.cloned.1.call-start = ((), (), s32[]{:S(2)}) async-start(), calls=%async_computation.9 | async-start | bytes 4718592 | tf_op jit(solution)/shard_map/all_gather | solution.py:90
  10.6 100.7 %collective-permute-start.1 = (bf16[2,704,2048]{2,1,0:T(8,128)(2,1)}, bf16[2,704,2048]{2,1,0:T(8,128)(2,1)}, u32[]{:S(2)}, u32[]{:S(2)}) collective-permute-start(bf16[2,704,2048]{2,1,0:T(8,128)(2,1)} %bitcast.245), channel_id=1, source_target_pairs={{0,1},{1,0},{2,3},{3,2},{4,5},{5,4},{6,7},{7,6},{8,9},{9,8},{10,11... | collective-permute-start | bytes 17301512 | tf_op jit(solution)/shard_map/ppermute | solution.py:52
  12.7 7.2 %copy-start.25 = (s32[1,4]{1,0:T(1,128)S(1)}, s32[1,4]{1,0:T(1,128)}, u32[]{:S(2)}) copy-start(s32[1,4]{1,0:T(1,128)} %param.13) | copy-start | bytes 52
  12.7 97.1 %all-to-all-start = ((bf16[8,2,32,2048]{3,2,1,0:T(8,128)(2,1)}), bf16[8,2,32,2048]{3,2,1,0:T(8,128)(2,1)S(1)}, u32[]{:S(2)}, u32[]{:S(2)}) async-start(bf16[8,2,32,2048]{3,2,1,0:T(8,128)(2,1)} %broadcast_in_dim.70), calls=%async_computation | async-start | bytes 4194304 | tf_op jit(solution)/shard_map/all_to_all | solution.py:102
  19.7 91.6 %collective-permute-start.2 = (bf16[704,2048]{1,0:T(8,128)(2,1)}, bf16[704,2048]{1,0:T(8,128)(2,1)}, u32[]{:S(2)}, u32[]{:S(2)}) collective-permute-start(bf16[704,2048]{1,0:T(8,128)(2,1)} %bitcast.246), channel_id=1, source_target_pairs={{0,1},{1,0},{2,3},{3,2},{4,5},{5,4},{6,7},{7,6},{8,9},{9,8},{10,11... | collective-permute-start | bytes 8650760 | tf_op jit(solution)/shard_map/ppermute | solution.py:52
  109.8 45.3 %collective-permute-start = (bf16[16,32,2048]{2,1,0:T(8,128)(2,1)S(1)}, bf16[16,32,2048]{2,1,0:T(8,128)(2,1)}, u32[]{:S(2)}, u32[]{:S(2)}) collective-permute-start(bf16[16,32,2048]{2,1,0:T(8,128)(2,1)S(1)} %bitcast.222), channel_id=1, source_target_pairs={{0,2},{1,3},{2,0},{3,1},{4,6},{5,7},{6,4},{7,5},{8,10},{9,11},{10,... | collective-permute-start | bytes 6291464 | tf_op jit(solution)/shard_map/ppermute | solution.py:114
  127.6 1.5 copy-start.14
  127.6 1.5 copy-start.15
  129.5 0.7 copy-start.8
  129.5 0.8 copy-start.10
  129.5 0.9 copy-start.12
  131.4 3.0 copy-start.9
  131.4 3.0 copy-start.11
  131.4 3.1 copy-start.13
  131.4 3.1 copy-start.17
  138.2 2.2 copy-start.16
  142.7 2.2 copy-start.26
  144.8 1.7 copy-start.18
  146.5 20.0 %copy-start.20 = (s32[1,128,6]{1,0,2:T(1,128)S(1)}, s32[1,128,6]{1,0,2:T(1,128)}, u32[]{:S(2)}) copy-start(s32[1,128,6]{1,0,2:T(1,128)} %param.19) | copy-start | bytes 9220
  147.6 18.9 %all-to-all-start.1 = ((bf16[8,128,256]{1,2,0:T(8,128)(2,1)}), bf16[8,128,256]{1,2,0:T(8,128)(2,1)S(1)}, u32[]{:S(2)}, u32[]{:S(2)}) async-start(bf16[8,128,256]{1,2,0:T(8,128)(2,1)} %copy.127), calls=%async_computation.1 | async-start | bytes 1048576 | tf_op jit(solution)/shard_map/all_to_all | solution.py:154
  151.6 18.9 %collective-permute-start.3 = (bf16[16,32,2048]{2,1,0:T(8,128)(2,1)S(1)}, bf16[16,32,2048]{2,1,0:T(8,128)(2,1)}, u32[]{:S(2)}, u32[]{:S(2)}) collective-permute-start(bf16[16,32,2048]{2,1,0:T(8,128)(2,1)S(1)} %bitcast.223), channel_id=1, source_target_pairs={{0,1},{1,0},{2,3},{3,2},{4,5},{5,4},{6,7},{7,6},{8,9},{9,8},{10,11... | collective-permute-start | bytes 6291464 | tf_op jit(solution)/shard_map/ppermute | solution.py:52
  166.5 6.1 %copy-start.4 = (bf16[8,128,256]{1,2,0:T(8,128)(2,1)}, bf16[8,128,256]{1,2,0:T(8,128)(2,1)S(1)}, u32[]{:S(2)}) copy-start(bf16[8,128,256]{1,2,0:T(8,128)(2,1)S(1)} %all-to-all-done.1) | copy-start | bytes 1572868
  166.5 6.1 %collective-permute-start.4 = (bf16[16,32,2048]{2,1,0:T(8,128)(2,1)}, bf16[16,32,2048]{2,1,0:T(8,128)(2,1)}, u32[]{:S(2)}, u32[]{:S(2)}) collective-permute-start(bf16[16,32,2048]{2,1,0:T(8,128)(2,1)} %collective-permute-done), channel_id=1, source_target_pairs={{0,1},{1,0},{2,3},{3,2},{4,5},{5,4},{6,7},{7,6},{8,9},{9,8},{10,11... | collective-permute-start | bytes 6291464 | tf_op jit(solution)/shard_map/ppermute | solution.py:52
  172.6 2.2 copy-start.3
  174.7 2.4 copy-start.21
  177.3 5.9 %copy-start.2 = (bf16[128,2048]{1,0:T(8,128)(2,1)}, bf16[128,2048]{1,0:T(8,128)(2,1)S(1)}, u32[]{:S(2)}) copy-start(bf16[128,2048]{1,0:T(8,128)(2,1)S(1)} %multiply_convert_fusion) | copy-start | bytes 1572868
  179.3 52.8 %all-to-all-start.4 = ((bf16[32,16,2048]{2,1,0:T(8,128)(2,1)}), bf16[32,16,2048]{2,1,0:T(8,128)(2,1)}, u32[]{:S(2)}, u32[]{:S(2)}) async-start(bf16[32,16,2048]{2,1,0:T(8,128)(2,1)} %convolution_convert_fusion.2), calls=%async_computation.4 | async-start | bytes 4194304 | tf_op jit(solution)/shard_map/all_to_all | solution.py:209
  232.1 53.1 %all-to-all-start.2 = ((bf16[32,12,2048]{2,1,0:T(8,128)(2,1)}), bf16[32,12,2048]{2,1,0:T(8,128)(2,1)S(1)}, u32[]{:S(2)}, u32[]{:S(2)}) async-start(bf16[32,12,2048]{2,1,0:T(8,128)(2,1)} %copy.138), calls=%async_computation.2 | async-start | bytes 4194304 | tf_op jit(solution)/shard_map/all_to_all | solution.py:209
  249.1 1.8 copy-start.23
  285.2 1.4 copy-start.6
  286.6 53.1 %all-to-all-start.5 = ((bf16[32,16,2048]{2,1,0:T(8,128)(2,1)}), bf16[32,16,2048]{2,1,0:T(8,128)(2,1)S(1)}, u32[]{:S(2)}, u32[]{:S(2)}) async-start(bf16[32,16,2048]{2,1,0:T(8,128)(2,1)} %copy.148), calls=%async_computation.5 | async-start | bytes 4194304 | tf_op jit(solution)/shard_map/all_to_all | solution.py:215
  290.8 7.1 %copy-start.24 = (bf16[1,704,2048]{2,1,0:T(8,128)(2,1)S(1)}, bf16[1,704,2048]{2,1,0:T(8,128)(2,1)}, u32[]{:S(2)}) copy-start(bf16[1,704,2048]{2,1,0:T(8,128)(2,1)} %param.21) | copy-start | bytes 8650756
  297.9 1.6 copy-start.7
  311.5 32.7 %copy-start.19 = (bf16[2048,16]{0,1:T(8,128)(2,1)S(1)}, bf16[2048,16]{0,1:T(8,128)(2,1)}, u32[]{:S(2)}) copy-start(bf16[2048,16]{0,1:T(8,128)(2,1)} %param.18) | copy-start | bytes 196612
  339.7 53.3 %all-to-all-start.3 = ((bf16[32,12,2048]{2,1,0:T(8,128)(2,1)}), bf16[32,12,2048]{2,1,0:T(8,128)(2,1)}, u32[]{:S(2)}, u32[]{:S(2)}) async-start(bf16[32,12,2048]{2,1,0:T(8,128)(2,1)} %copy.142), calls=%async_computation.3 | async-start | bytes 4194304 | tf_op jit(solution)/shard_map/all_to_all | solution.py:215
  350.5 42.5 %slice-start = ((f32[128,32,28]{0,2,1:T(8,128)}), f32[128,32,12]{0,2,1:T(8,128)S(1)}, s32[]{:S(2)}) async-start(f32[128,32,28]{0,2,1:T(8,128)} %reshape.440), calls=%async_computation.10 | async-start | bytes 524288 | tf_op jit(solution)/shard_map/slice | solution.py:220
  354.7 60.4 %copy-start.22 = (f32[2048]{0:T(1024)S(1)}, f32[2048]{0:T(1024)}, u32[]{:S(2)}) copy-start(f32[2048]{0:T(1024)} %param.22) | copy-start | bytes 24580
  396.6 26.9 %copy-start.5 = (bf16[128,2048]{1,0:T(8,128)(2,1)}, bf16[128,2048]{1,0:T(8,128)(2,1)S(1)}, u32[]{:S(2)}) copy-start(bf16[128,2048]{1,0:T(8,128)(2,1)S(1)} %fusion.35) | copy-start | bytes 1572868
  415.1 18.5 %copy-start.1 = (bf16[2,128,2048]{2,1,0:T(8,128)(2,1)S(1)}, bf16[2,128,2048]{2,1,0:T(8,128)(2,1)}, u32[]{:S(2)}) copy-start(bf16[2,128,2048]{2,1,0:T(8,128)(2,1)} %param.16) | copy-start | bytes 3145732
Sparse Core Ops, SparseCore 0:
  10.7 110.5 all-gather.1
